TPU v7x, 256 devices: a whole 4x4x8 slice. The times are simulated.
256 devices in a mesh: req: 32 (over x, z), mlp: 8 (over y, core).
Axes of the slice: x: 4, y: 4, z: 8, core: 2. Of those that a mesh axis runs over, the one named last changes fastest.
Arguments:
- x_pages: bfloat16 [1024, 8, 4096], P('req', None, 'mlp'), may hold values from -6 to 6
- page_owner: int32 [1024], P('req'), may hold values from 0 to 31, as said below
- request_id: int32 [8192], P('req'), may hold values from 0 to 8191, as said below
- adapter_table: int32 [8192], P('req'), may hold values from 0 to 63
- ln_gain: float32 [4096], replicated, may hold values from 0.5 to 1.5
- ln_bias: float32 [4096], replicated, may hold values from -3 to 3
- w_query: bfloat16 [4096, 2048], P('req', 'mlp'), may hold values from -0.09375 to 0.09375
- w_key: bfloat16 [4096, 2048], P('req', 'mlp'), may hold values from -0.09375 to 0.09375
- w_value: bfloat16 [4096, 2048], P('req', 'mlp'), may hold values from -0.09375 to 0.09375
- w_attn_out: bfloat16 [2048, 4096], P('mlp', 'req'), may hold values from -0.125 to 0.125
- down_query: bfloat16 [4096, 1024], P('mlp'), may hold values from -0.09375 to 0.09375
- up_query: bfloat16 [1024, 2048], P(None, 'mlp'), may hold values from -1.5 to 1.5
- down_value: bfloat16 [4096, 1024], P('mlp'), may hold values from -0.09375 to 0.09375
- up_value: bfloat16 [1024, 2048], P(None, 'mlp'), may hold values from -1.5 to 1.5
- w_fc_in: bfloat16 [4096, 8192], P('req', 'mlp'), may hold values from -0.09375 to 0.09375
- b_fc_in: float32 [8192], P('mlp'), may hold values from -3 to 3
- down_fc: bfloat16 [4096, 1024], P('mlp'), may hold values from -0.09375 to 0.09375
- up_fc: bfloat16 [1024, 8192], P(None, 'mlp'), may hold values from -1.5 to 1.5
- w_fc_out: bfloat16 [8192, 4096], P('mlp', 'req'), may hold values from -0.0625 to 0.0625
- b_fc_out: float32 [4096], P('mlp'), may hold values from -3 to 3
Outputs:
- out_pages: bfloat16 [1024, 8, 4096], P('req', None, 'mlp')
Inputs may be any that keep to these rules, and one draw needn't show every extreme that they name: `page_owner`: every owner receives exactly 32 pages, at most 2 of them from one device, and some device sends exactly 2 pages to some owner. `request_id`: ids never fall; every request lies inside one owner's block of 256 rows, and the ids of block k lie in k * 256 to k * 256 + 255; some request is 256 long.
All inputs are finite; a program needn't handle non-finite values.
Results may differ from a plain program's by a relative error of at most 0.006.
Values may be sent and summed in bfloat16 or wider, within the bound.
No kernel may reach another device: no remote copies, remote signals or barrier semaphores. Data moves between devices by JAX's collectives and lax.ppermute only.
A program may use at most 128 MiB of HBM per device.

v0:
```python
import jax
import jax.numpy as jnp
from jax import lax
from jax.sharding import PartitionSpec as P

HS = 256
ROT = 64
NAD = 64
R = 16


EPS = 1e-05


def gelu_tanh(v):
    return 0.5 * v * (1.0 + jnp.tanh(0.7978845608028654 * (v + 0.044715 * v * v * v)))


def rotate(block, pos):
    half = ROT // 2
    freq = jnp.power(10000.0, -jnp.arange(half).astype(jnp.float32) * 2.0 / ROT)
    angle = pos.astype(jnp.float32)[:, None, None] * freq[None, None, :]
    cosine = jnp.cos(angle)
    sine = jnp.sin(angle)
    even = block[:, :, 0:ROT:2]
    odd = block[:, :, 1:ROT:2]
    turned = jnp.stack([even * cosine - odd * sine, odd * cosine + even * sine], axis=-1)
    turned = turned.reshape(block.shape[0], block.shape[1], ROT)
    return jnp.concatenate([turned, block[:, :, ROT:]], axis=2)


def on_device(
    x_pages,
    page_owner,
    request_id,
    adapter_table,
    ln_gain,
    ln_bias,
    w_query,
    w_key,
    w_value,
    w_attn_out,
    down_query,
    up_query,
    down_value,
    up_value,
    w_fc_in,
    b_fc_in,
    down_fc,
    up_fc,
    w_fc_out,
    b_fc_out,
):
    groups = lax.axis_size("req")
    pg_dev = x_pages.shape[0]
    page_len = x_pages.shape[1]
    width_m = x_pages.shape[2]
    tok = request_id.shape[0]
    per_owner = pg_dev // groups + 1
    slots = groups * per_owner
    page_iota = jnp.arange(pg_dev)
    earlier = (page_owner[None, :] == page_owner[:, None]) & (
        page_iota[None, :] < page_iota[:, None]
    )
    rank = jnp.sum(earlier.astype(jnp.int32), axis=1)
    slot = page_owner * per_owner + rank
    place = (slot[None, :] == jnp.arange(slots)[:, None]).astype(jnp.bfloat16)
    flat_pages = x_pages.reshape(pg_dev, page_len * width_m)
    outgoing = jnp.dot(place, flat_pages, preferred_element_type=jnp.float32).astype(jnp.bfloat16)
    outgoing = outgoing.reshape(groups, per_owner, page_len * width_m)
    filled = jnp.sum(place, axis=1).reshape(groups, per_owner)
    arrived, marks = (
        lax.all_to_all(outgoing, "req", split_axis=0, concat_axis=0, tiled=True),
        lax.all_to_all(filled, "req", split_axis=0, concat_axis=0, tiled=True),
    )
    valid = marks.reshape(slots).astype(jnp.float32)
    position = jnp.cumsum(valid) - 1.0
    take = (
        (position[None, :] == jnp.arange(pg_dev).astype(jnp.float32)[:, None])
        & (valid[None, :] > 0.5)
    ).astype(jnp.bfloat16)
    own_x = jnp.dot(
        take, arrived.reshape(slots, page_len * width_m), preferred_element_type=jnp.float32
    )
    own_x = own_x.astype(jnp.bfloat16).reshape(tok, width_m)
    column = lax.axis_index("mlp") * width_m
    whole = lax.all_gather(own_x, "mlp", axis=1, tiled=True).astype(jnp.float32)
    mean = jnp.mean(whole, axis=1, keepdims=True)
    var = jnp.mean(jnp.square(whole - mean), axis=1, keepdims=True)
    full_ln = ((whole - mean) * lax.rsqrt(var + EPS) * ln_gain + ln_bias).astype(jnp.bfloat16)
    ln_m = lax.dynamic_slice_in_dim(full_ln, column, width_m, 1)
    local_req = request_id - lax.axis_index("req") * tok
    lookup = local_req[:, None] == jnp.arange(tok)[None, :]
    adapter = jnp.sum(jnp.where(lookup, adapter_table[None, :], 0), axis=1)
    onehot = (adapter[:, None] == jnp.arange(NAD)[None, :]).astype(jnp.float32)
    onehot_low = onehot.astype(jnp.bfloat16)

    def pick(down):
        spread = jnp.dot(ln_m, down, preferred_element_type=jnp.float32).reshape(tok, NAD, R)
        return jnp.sum(spread * onehot[:, :, None], axis=1)

    picked = lax.psum((pick(down_query), pick(down_value), pick(down_fc)), "mlp")

    def lift(chosen, up):
        expanded = (onehot_low[:, :, None] * chosen.astype(jnp.bfloat16)[:, None, :]).reshape(
            tok, NAD * R
        )
        return jnp.dot(expanded, up, preferred_element_type=jnp.float32)

    row_iota = jnp.arange(tok)
    start = jnp.sum((request_id[None, :] < request_id[:, None]).astype(jnp.int32), axis=1)
    pos = row_iota - start
    mask = (request_id[:, None] == request_id[None, :]) & (row_iota[None, :] <= row_iota[:, None])
    heads_w = w_query.shape[1]
    pieces = (
        lax.all_gather(w_query, "req", axis=0, tiled=True),
        lax.all_gather(w_key, "req", axis=0, tiled=True),
        lax.all_gather(w_value, "req", axis=0, tiled=True),
    )
    cols = full_ln
    base_q, base_k, base_v = tuple(
        [jnp.dot(cols, piece, preferred_element_type=jnp.float32) for piece in pieces]
    )
    query = rotate(
        (base_q + lift(picked[0], up_query)).reshape(tok, heads_w // HS, HS), pos
    ).astype(jnp.bfloat16)
    keys = rotate(base_k.reshape(tok, heads_w // HS, HS), pos).astype(jnp.bfloat16)
    value = (
        (base_v + lift(picked[1], up_value)).astype(jnp.bfloat16).reshape(tok, heads_w // HS, HS)
    )
    scores = jnp.einsum("qhd,khd->hqk", query, keys, preferred_element_type=jnp.float32) * HS ** (
        -0.5
    )
    scores = jnp.where(mask[None, :, :], scores, -1e30)
    top = jnp.max(scores, axis=2, keepdims=True)
    weights = jnp.exp(scores - top)
    probs = (weights / jnp.sum(weights, axis=2, keepdims=True)).astype(jnp.bfloat16)
    mixed_heads = jnp.einsum("hqk,khd->qhd", probs, value, preferred_element_type=jnp.float32)
    attn = mixed_heads.astype(jnp.bfloat16).reshape(tok, heads_w)
    cols = full_ln
    hidden_pre = jnp.dot(
        cols, lax.all_gather(w_fc_in, "req", axis=0, tiled=True), preferred_element_type=jnp.float32
    )
    hidden_pre = hidden_pre + lift(picked[2], up_fc) + b_fc_in
    hidden = gelu_tanh(hidden_pre).astype(jnp.bfloat16)
    pieces = (
        lax.all_gather(w_attn_out, "req", axis=1, tiled=True),
        lax.all_gather(w_fc_out, "req", axis=1, tiled=True),
    )
    part = jnp.dot(attn, pieces[0], preferred_element_type=jnp.float32) + jnp.dot(
        hidden, pieces[1], preferred_element_type=jnp.float32
    )
    shares = lax.psum_scatter(part, "mlp", scatter_dimension=1, tiled=True)
    result = (own_x.astype(jnp.float32) + shares + b_fc_out).astype(jnp.bfloat16)
    back_flat = result.reshape(pg_dev, page_len * width_m)
    leaving = jnp.dot(take.T, back_flat, preferred_element_type=jnp.float32).astype(jnp.bfloat16)
    leaving = leaving.reshape(groups, per_owner, page_len * width_m)
    returned = lax.all_to_all(leaving, "req", split_axis=0, concat_axis=0, tiled=True)
    pages_back = jnp.dot(
        place.T, returned.reshape(slots, page_len * width_m), preferred_element_type=jnp.float32
    )
    return pages_back.astype(jnp.bfloat16).reshape(pg_dev, page_len, width_m)


def solution(mesh):
    in_specs = (
        P("req", None, "mlp"),
        P("req"),
        P("req"),
        P("req"),
        P(),
        P(),
        P("req", "mlp"),
        P("req", "mlp"),
        P("req", "mlp"),
        P("mlp", "req"),
        P("mlp", None),
        P(None, "mlp"),
        P("mlp", None),
        P(None, "mlp"),
        P("req", "mlp"),
        P("mlp"),
        P("mlp", None),
        P(None, "mlp"),
        P("mlp", "req"),
        P("mlp"),
    )
    out_specs = P("req", None, "mlp")
    return jax.shard_map(
        on_device, mesh=mesh, in_specs=in_specs, out_specs=out_specs, check_vma=False
    )
```

profile of v0, /device:TPU:57, one launch (start us, length us, event | category | flops | bytes accessed | tf_op | source)
XLA Modules:
  0.0 669.1 jit_solution(17255531953203514862)
XLA Ops:
  6.5 1.0 convert_reduce_fusion.3
  9.0 10.6 %all-to-all-start = ((bf16[32,1,2]{2,1,0:T(2,128)(2,1)}), bf16[32,1,2]{2,1,0:T(2,128)(2,1)S(1)}, u32[]{:S(2)}, u32[]{:S(2)}) async-start(bf16[32,1,2]{2,1,0:T(2,128)(2,1)} %all_to_all.16), calls=%async_computation | async-start | bytes 32768 | tf_op jit(solution)/shard_map/all_to_all | solution.py:74
  19.7 1.0 copy.46
  21.1 1.1 reshape.339
  22.3 5.1 all-to-all-done
  27.4 4.7 all-to-all-start.1
  32.6 14.9 %all-to-all-done.1 = bf16[32,2,4096]{2,1,0:T(2,128)(2,1)S(1)} async-done(((bf16[32,2,4096]{2,1,0:T(2,128)(2,1)}), bf16[32,2,4096]{2,1,0:T(2,128)(2,1)S(1)}, u32[]{:S(2)}, u32[]{:S(2)}) %all-to-all-start.1) | async-done | bytes 524320 | tf_op jit(solution)/shard_map/all_to_all | solution.py:73
  48.1 0.8 reshape.341
  53.8 21.0 %all-gather.8.cloned.1.call-done = bf16[256,4096]{1,0:T(8,128)(2,1)} async-done(((bf16[256,512]{1,0:T(8,128)(2,1)}), bf16[256,4096]{1,0:T(8,128)(2,1)}) %all-gather.8.cloned.1.call-update) | async-done | bytes 2097168 | tf_op jit(solution)/shard_map/all_gather | solution.py:87
  74.8 2.1 convert_reduce_fusion
  77.8 1.0 fusion.5
  79.6 1.4 copy-done.5
  82.6 24.0 %all-reduce = (bf16[256,16]{0,1:T(8,128)(2,1)S(1)}, bf16[256,16]{0,1:T(8,128)(2,1)S(1)}, bf16[256,16]{0,1:T(8,128)(2,1)S(1)}) all-reduce(f32[256,16]{0,1:T(8,128)S(1)} %get-tuple-element.6, f32[256,16]{0,1:T(8,128)S(1)} %get-tuple-element.7, f32[256,16]{0,1:T(8,128)S(1)} %get-tuple-element.5), channel_id=1, replica_groups=mesh['req'=32,'mlp'=8] {'mlp'}, use_global_device_ids=true, to_apply=%region_14.15 | all-reduce | flops 12288 | bytes 73728 | tf_op jit(solution)/shard_map/psum | solution.py:102
  106.6 44.5 %all-gather.12.cloned.1.call-done = bf16[4096,256]{1,0:T(8,128)(2,1)} async-done(((bf16[128,256]{1,0:T(8,128)(2,1)}), bf16[4096,256]{1,0:T(8,128)(2,1)}) %all-gather.12.cloned.1.call-update) | async-done | bytes 2097168 | tf_op jit(solution)/shard_map/all_gather | solution.py:116
  151.1 3.2 fusion.85
  155.5 73.3 %all-gather.14.cloned.1.call-done = bf16[4096,256]{1,0:T(8,128)(2,1)} async-done(((bf16[128,256]{1,0:T(8,128)(2,1)}), bf16[4096,256]{1,0:T(8,128)(2,1)}) %all-gather.14.cloned.1.call-update) | async-done | bytes 2097168 | tf_op jit(solution)/shard_map/all_gather | solution.py:117
  228.8 3.1 convolution_bitcast_fusion
  232.0 0.8 fusion.61
  233.0 0.9 fusion.40
  234.3 72.1 %all-gather.10.cloned.1.call-done = bf16[4096,256]{1,0:T(8,128)(2,1)} async-done(((bf16[128,256]{1,0:T(8,128)(2,1)}), bf16[4096,256]{1,0:T(8,128)(2,1)}) %all-gather.10.cloned.1.call-update) | async-done | bytes 2097168 | tf_op jit(solution)/shard_map/all_gather | solution.py:118
  306.4 3.0 fusion.84
  309.8 97.4 %all-gather.18.cloned.1.call-done = bf16[4096,1024]{1,0:T(8,128)(2,1)} async-done(((bf16[128,1024]{1,0:T(8,128)(2,1)}), bf16[4096,1024]{1,0:T(8,128)(2,1)}) %all-gather.18.cloned.1.call-update) | async-done | bytes 8388624 | tf_op jit(solution)/shard_map/all_gather | solution.py:142
  407.2 7.3 %fusion.86 = f32[256,1024]{1,0:T(8,128)} fusion(bf16[256,4096]{1,0:T(8,128)(2,1)} %copy-done.1, bf16[4096,1024]{1,0:T(8,128)(2,1)} %all-gather.18.cloned.1.call-done), kind=kOutput, calls=%fused_computation.132 | convolution fusion | flops 2147483648 | bytes 11534336 | tf_op jit(solution)/shard_map/dot_general | solution.py:141
  414.5 92.1 %all-gather.20.cloned.1.call-done = bf16[1024,4096]{1,0:T(8,128)(2,1)} async-done(((bf16[1024,128]{1,0:T(8,128)(2,1)}), bf16[1024,4096]{1,0:T(8,128)(2,1)}) %all-gather.20.cloned.1.call-update) | async-done | bytes 8388624 | tf_op jit(solution)/shard_map/all_gather | solution.py:148
  506.6 8.9 %fusion.16 = f32[256,4096]{1,0:T(8,128)} fusion(bf16[1024,4096]{1,0:T(8,128)(2,1)} %all-gather.20.cloned.1.call-done, f32[256,1024]{1,0:T(8,128)} %fusion.86, bf16[256,1024]{0,1:T(8,128)(2,1)S(1)} %bitcast.65, bf16[1024,1024]{1,0:T(8,128)(2,1)S(1)} %copy-done, f32[1024]{0:T(1024)S(1)} %copy-done.12), kind=kOutput, calls=%fused_computation.33 | convolution fusion | flops 2687238144 | bytes 16257024 | tf_op jit(solution)/shard_map/dot_general | solution.py:150
  515.5 67.1 %all-gather.16.cloned.1.call-done = bf16[256,4096]{1,0:T(8,128)(2,1)} async-done(((bf16[256,128]{1,0:T(8,128)(2,1)}), bf16[256,4096]{1,0:T(8,128)(2,1)}) %all-gather.16.cloned.1.call-update) | async-done | bytes 2097168 | tf_op jit(solution)/shard_map/all_gather | solution.py:147
  582.6 5.7 convolution_add_fusion
  588.3 42.6 %reduce-scatter.2.cloned.1.call-done = f32[256,512]{1,0:T(8,128)} async-done(((f32[256,4096]{1,0:T(8,128)}), f32[256,512]{1,0:T(8,128)}) %reduce-scatter.2.cloned.1.call-update) | async-done | bytes 524304 | tf_op jit(solution)/shard_map/reduce_scatter | solution.py:153
  630.9 1.1 add_convert_fusion
  632.9 27.0 %all_to_all.20 = bf16[32,2,4096]{2,1,0:T(2,128)(2,1)} all-to-all(bf16[32,2,4096]{2,1,0:T(2,128)(2,1)S(1)} %reshape.349), channel_id=1, replica_groups=mesh['req'=32,'mlp'=8] {'req'}, dimensions={0} | all-to-all | bytes 1048576 | tf_op jit(solution)/shard_map/all_to_all | solution.py:158
  660.0 1.2 reshape.350
  661.5 0.8 copy.47
  (100 shorter events, 14.1 us)
Async XLA Ops:
  6.5 500.1 %copy-start = (bf16[1024,1024]{1,0:T(8,128)(2,1)S(1)}, bf16[1024,1024]{1,0:T(8,128)(2,1)}, u32[]{:S(2)}) copy-start(bf16[1024,1024]{1,0:T(8,128)(2,1)} %param.37) | copy-start | bytes 6291460
  8.2 23.9 %copy-start.15 = (s32[32]{0:T(128)}, s32[32]{0:T(128)S(1)}, u32[]{:S(2)}) copy-start(s32[32]{0:T(128)S(1)} %multiply_add_fusion.1) | copy-start | bytes 388
  9.0 18.3 %all-to-all-start = ((bf16[32,1,2]{2,1,0:T(2,128)(2,1)}), bf16[32,1,2]{2,1,0:T(2,128)(2,1)S(1)}, u32[]{:S(2)}, u32[]{:S(2)}) async-start(bf16[32,1,2]{2,1,0:T(2,128)(2,1)} %all_to_all.16), calls=%async_computation | async-start | bytes 32768 | tf_op jit(solution)/shard_map/all_to_all | solution.py:74
  22.3 31.2 %copy-start.13 = (s32[256]{0:T(256)S(1)}, s32[256]{0:T(256)}, u32[]{:S(2)}) copy-start(s32[256]{0:T(256)} %param.22) | copy-start | bytes 3076
  22.3 31.4 %copy-start.19 = (s32[256]{0:T(256)S(1)}, s32[256]{0:T(256)}, u32[]{:S(2)}) copy-start(s32[256]{0:T(256)} %param.23) | copy-start | bytes 3076
  27.4 20.2 %all-to-all-start.1 = ((bf16[32,2,4096]{2,1,0:T(2,128)(2,1)}), bf16[32,2,4096]{2,1,0:T(2,128)(2,1)S(1)}, u32[]{:S(2)}, u32[]{:S(2)}) async-start(bf16[32,2,4096]{2,1,0:T(2,128)(2,1)} %reshape.339), calls=%async_computation.1 | async-start | bytes 1048576 | tf_op jit(solution)/shard_map/all_to_all | solution.py:73
  32.0 42.8 %all-gather.8.cloned.1.call-start = ((), (), s32[]{:S(2)}) async-start(), calls=%async_computation.4 | async-start | bytes 2359296 | tf_op jit(solution)/shard_map/all_gather | solution.py:87
  32.1 21.5 %copy-start.17 = (f32[32]{0:T(128)}, f32[32]{0:T(128)S(1)}, u32[]{:S(2)}) copy-start(f32[32]{0:T(128)S(1)} %iota_convert_fusion) | copy-start | bytes 388
  48.9 102.2 %all-gather.12.cloned.1.call-start = ((), (), s32[]{:S(2)}) async-start(), calls=%async_computation.6 | async-start | bytes 2162688 | tf_op jit(solution)/shard_map/all_gather | solution.py:116
  49.7 179.2 %all-gather.14.cloned.1.call-start = ((), (), s32[]{:S(2)}) async-start(), calls=%async_computation.7 | async-start | bytes 2162688 | tf_op jit(solution)/shard_map/all_gather | solution.py:117
  50.4 256.0 %all-gather.10.cloned.1.call-start = ((), (), s32[]{:S(2)}) async-start(), calls=%async_computation.5 | async-start | bytes 2162688 | tf_op jit(solution)/shard_map/all_gather | solution.py:118
  51.0 356.2 %all-gather.18.cloned.1.call-start = ((), (), s32[]{:S(2)}) async-start(), calls=%async_computation.9 | async-start | bytes 8650752 | tf_op jit(solution)/shard_map/all_gather | solution.py:142
  51.6 455.1 %all-gather.20.cloned.1.call-start = ((), (), s32[]{:S(2)}) async-start(), calls=%async_computation.10 | async-start | bytes 8650752 | tf_op jit(solution)/shard_map/all_gather | solution.py:148
  52.1 530.4 %all-gather.16.cloned.1.call-start = ((), (), s32[]{:S(2)}) async-start(), calls=%async_computation.8 | async-start | bytes 2162688 | tf_op jit(solution)/shard_map/all_gather | solution.py:147
  52.9 578.0 %reduce-scatter.2.cloned.1.call-start = ((), (), s32[]{:S(2)}) async-start(), calls=%async_computation.11 | async-start | bytes 4718592 | tf_op jit(solution)/shard_map/reduce_scatter | solution.py:153
  74.8 2.2 copy-start.2
  74.8 2.9 copy-start.10
  74.8 2.9 copy-start.11
  77.8 1.2 copy-start.4
  79.0 2.6 copy-start.1
  79.0 2.0 copy-start.5
  79.0 2.6 copy-start.6
  151.1 3.3 copy-start.8
  154.8 0.7 copy-start.7
  306.4 3.0 copy-start.9
  309.8 196.8 %copy-start.12 = (f32[1024]{0:T(1024)S(1)}, f32[1024]{0:T(1024)}, u32[]{:S(2)}) copy-start(f32[1024]{0:T(1024)} %param.35) | copy-start | bytes 12292
  588.3 42.6 %copy-start.3 = (bf16[256,512]{1,0:T(8,128)(2,1)S(1)}, bf16[256,512]{1,0:T(8,128)(2,1)}, u32[]{:S(2)}) copy-start(bf16[256,512]{1,0:T(8,128)(2,1)} %reshape.341) | copy-start | bytes 786436
  588.3 42.6 %copy-start.14 = (f32[512]{0:T(512)S(1)}, f32[512]{0:T(512)}, u32[]{:S(2)}) copy-start(f32[512]{0:T(512)} %param.39) | copy-start | bytes 6148
  588.3 43.9 %copy-start.18 = (f32[32]{0:T(128)S(1)}, f32[32]{0:T(128)}, u32[]{:S(2)}) copy-start(f32[32]{0:T(128)} %copy-done.17) | copy-start | bytes 388
  632.2 29.1 %copy-start.16 = (s32[32]{0:T(128)S(1)}, s32[32]{0:T(128)}, u32[]{:S(2)}) copy-start(s32[32]{0:T(128)} %copy-done.15) | copy-start | bytes 388
Sparse Core Ops, SparseCore 0:
  49.0 25.7 all-gather.7
  77.4 73.6 all-gather.11
  153.7 75.0 all-gather.13
  231.3 75.0 all-gather.9
  308.9 98.2 all-gather.17
  409.5 97.0 all-gather.19
  509.1 73.4 all-gather.15
  588.4 42.4 reduce-scatter.1
where the time goes:
time: 670 us; the launch traced here: 669 us
  waiting for transfers between devices  534 us (80%)
  blocking collectives  51 us (8%)
  matrix products  35.3 us (5%)
  starting transfers between devices  15.6 us (2%)
  between operations  13.9 us (2%)
  local copies, waits for them, and re-layouts  10.2 us (2%)
  other arithmetic  9.33 us (1%)
    all_gather x1, waiting for transfers between devices, on_device(): lax.all_gather(w_fc_in, 'req', axis=0, tiled=True)  97.4 us
    all_gather x1, waiting for transfers between devices, on_device(): lax.all_gather(w_fc_out, 'req', axis=1, tiled=True)  92.1 us
    all_gather x1, waiting for transfers between devices, on_device(): lax.all_gather(w_key, 'req', axis=0, tiled=True)  73.3 us
    all_gather x1, waiting for transfers between devices, on_device(): lax.all_gather(w_value, 'req', axis=0, tiled=True)  72.1 us
    all_gather x1, waiting for transfers between devices, on_device(): lax.all_gather(w_attn_out, 'req', axis=1, tiled=True)  67.1 us
    all_gather x1, waiting for transfers between devices, on_device(): lax.all_gather(w_query, 'req', axis=0, tiled=True)  44.5 us
    reduce_scatter x1, waiting for transfers between devices, on_device(): shares = lax.psum_scatter(part, 'mlp', scatter_dimension=1, tiled=True)  42.6 us
    all_to_all x1, blocking collectives, on_device(): lax.all_to_all(leaving, 'req', split_axis=0, concat_axis=0, tiled=True)  27 us
  transfers between devices with their start and end apart: 10, of which 10 were waited for; matrix products, arithmetic and copies ran while one was open for 6% of the time, Pallas kernels for 0%

commit v1 on v0

--- a/solution.py
+++ b/solution.py
@@ -112,15 +112,16 @@
     pos = row_iota - start
     mask = (request_id[:, None] == request_id[None, :]) & (row_iota[None, :] <= row_iota[:, None])
     heads_w = w_query.shape[1]
-    pieces = (
-        lax.all_gather(w_query, "req", axis=0, tiled=True),
-        lax.all_gather(w_key, "req", axis=0, tiled=True),
-        lax.all_gather(w_value, "req", axis=0, tiled=True),
+    ff_w = w_fc_in.shape[1]
+    packed = jnp.concatenate(
+        [w_query, w_key, w_value, w_fc_in, w_attn_out.T, w_fc_out.T], axis=1
     )
-    cols = full_ln
-    base_q, base_k, base_v = tuple(
-        [jnp.dot(cols, piece, preferred_element_type=jnp.float32) for piece in pieces]
-    )
+    gathered = lax.all_gather(packed, "req", axis=0, tiled=True)
+    n_in = 3 * heads_w + ff_w
+    base = jnp.dot(full_ln, gathered[:, :n_in], preferred_element_type=jnp.float32)
+    base_q = base[:, :heads_w]
+    base_k = base[:, heads_w : 2 * heads_w]
+    base_v = base[:, 2 * heads_w : 3 * heads_w]
     query = rotate(
         (base_q + lift(picked[0], up_query)).reshape(tok, heads_w // HS, HS), pos
     ).astype(jnp.bfloat16)
@@ -137,18 +138,15 @@
     probs = (weights / jnp.sum(weights, axis=2, keepdims=True)).astype(jnp.bfloat16)
     mixed_heads = jnp.einsum("hqk,khd->qhd", probs, value, preferred_element_type=jnp.float32)
     attn = mixed_heads.astype(jnp.bfloat16).reshape(tok, heads_w)
-    cols = full_ln
-    hidden_pre = jnp.dot(
-        cols, lax.all_gather(w_fc_in, "req", axis=0, tiled=True), preferred_element_type=jnp.float32
-    )
+    hidden_pre = base[:, 3 * heads_w :]
     hidden_pre = hidden_pre + lift(picked[2], up_fc) + b_fc_in
     hidden = gelu_tanh(hidden_pre).astype(jnp.bfloat16)
-    pieces = (
-        lax.all_gather(w_attn_out, "req", axis=1, tiled=True),
-        lax.all_gather(w_fc_out, "req", axis=1, tiled=True),
-    )
-    part = jnp.dot(attn, pieces[0], preferred_element_type=jnp.float32) + jnp.dot(
-        hidden, pieces[1], preferred_element_type=jnp.float32
+    joined = jnp.concatenate([attn, hidden], axis=1)
+    part = lax.dot_general(
+        joined,
+        gathered[:, n_in:],
+        (((1,), (1,)), ((), ())),
+        preferred_element_type=jnp.float32,
     )
     shares = lax.psum_scatter(part, "mlp", scatter_dimension=1, tiled=True)
     result = (own_x.astype(jnp.float32) + shares + b_fc_out).astype(jnp.bfloat16)

time: 670 us -> 384 us (0.57)
  waiting for transfers between devices: 534 us -> 242 us
  local copies, waits for them, and re-layouts: 10.2 us -> 24 us
  matrix products: 35.3 us -> 25.8 us
    all_gather x6 -> x1, waiting for transfers between devices: 447 us -> 163 us  [on_device(): gathered = lax.all_gather(packed, 'req', axis=0, tiled=True)]
    dot_general x6 -> x3, matrix products: 31.3 us -> 18.9 us  [the longest x1 8.85 us: on_device(): lax.dot_general(joined, gathered[:, n_in:], (((1,), (1,)), ((), ())), pre...]
  transfers between devices with their start and end apart: 10 -> 5, of which waited for: 10 -> 5; matrix products, arithmetic and copies ran while one was open for 6% -> 4% of each run, Pallas kernels for 0% -> 0%
where the time goes in v1:
time: 384 us; the launch traced here: 383 us
  waiting for transfers between devices  242 us (63%)
  blocking collectives  51.1 us (13%)
  matrix products  25.8 us (7%)
  local copies, waits for them, and re-layouts  24 us (6%)
  starting transfers between devices  15.4 us (4%)
  between operations  13.6 us (4%)
  other arithmetic  11.1 us (3%)
    all_gather x1, waiting for transfers between devices, on_device(): gathered = lax.all_gather(packed, 'req', axis=0, tiled=True)  163 us
    reduce_scatter x1, waiting for transfers between devices, on_device(): shares = lax.psum_scatter(part, 'mlp', scatter_dimension=1, tiled=True)  40.4 us
    all_to_all x1, blocking collectives, on_device(): lax.all_to_all(leaving, 'req', split_axis=0, concat_axis=0, tiled=True)  26.9 us
    psum x1, blocking collectives, on_device(): lax.psum((pick(down_query), pick(down_value), pick(down_fc)), 'mlp')  24.2 us
    all_gather x1, waiting for transfers between devices, on_device(): whole = lax.all_gather(own_x, 'mlp', axis=1, tiled=True).astype(jnp.float32)  18.4 us
    all_to_all x1, waiting for transfers between devices, on_device(): lax.all_to_all(outgoing, 'req', split_axis=0, concat_axis=0, tiled=True)  14.9 us
    all_to_all x1, starting transfers between devices, on_device(): lax.all_to_all(filled, 'req', split_axis=0, concat_axis=0, tiled=True)  10.6 us
    unnamed x57, local copies, waits for them, and re-layouts  10.3 us
  transfers between devices with their start and end apart: 5, of which 5 were waited for; matrix products, arithmetic and copies ran while one was open for 4% of the time, Pallas kernels for 0%

profile of v1, /device:TPU:57, one launch (start us, length us, event | category | flops | bytes accessed | tf_op | source)
XLA Modules:
  0.0 383.0 jit_solution(9699808319969201170)
XLA Ops:
  6.5 1.0 convert_reduce_fusion.3
  9.0 10.6 %all-to-all-start = ((bf16[32,1,2]{2,1,0:T(2,128)(2,1)}), bf16[32,1,2]{2,1,0:T(2,128)(2,1)S(1)}, u32[]{:S(2)}, u32[]{:S(2)}) async-start(bf16[32,1,2]{2,1,0:T(2,128)(2,1)} %all_to_all.16), calls=%async_computation | async-start | bytes 32768 | tf_op jit(solution)/shard_map/all_to_all | solution.py:74
  19.7 1.0 copy.82
  21.1 1.1 reshape.339
  22.3 5.1 %all-to-all-done = bf16[32,1,2]{2,1,0:T(2,128)(2,1)S(1)} async-done(((bf16[32,1,2]{2,1,0:T(2,128)(2,1)}), bf16[32,1,2]{2,1,0:T(2,128)(2,1)S(1)}, u32[]{:S(2)}, u32[]{:S(2)}) %all-to-all-start) | async-done | bytes 160 | tf_op jit(solution)/shard_map/all_to_all | solution.py:74
  27.4 4.7 %all-to-all-start.1 = ((bf16[32,2,4096]{2,1,0:T(2,128)(2,1)}), bf16[32,2,4096]{2,1,0:T(2,128)(2,1)S(1)}, u32[]{:S(2)}, u32[]{:S(2)}) async-start(bf16[32,2,4096]{2,1,0:T(2,128)(2,1)} %reshape.339), calls=%async_computation.1 | async-start | bytes 1048576 | tf_op jit(solution)/shard_map/all_to_all | solution.py:73
  32.6 14.9 %all-to-all-done.1 = bf16[32,2,4096]{2,1,0:T(2,128)(2,1)S(1)} async-done(((bf16[32,2,4096]{2,1,0:T(2,128)(2,1)}), bf16[32,2,4096]{2,1,0:T(2,128)(2,1)S(1)}, u32[]{:S(2)}, u32[]{:S(2)}) %all-to-all-start.1) | async-done | bytes 524320 | tf_op jit(solution)/shard_map/all_to_all | solution.py:73
  50.7 1.0 copy.66
  53.6 1.0 bitcast_dynamic-update-slice_fusion
  56.5 18.4 %all-gather.3.cloned.1.call-done = bf16[256,4096]{1,0:T(8,128)(2,1)} async-done(((bf16[256,512]{1,0:T(8,128)(2,1)}), bf16[256,4096]{1,0:T(8,128)(2,1)}) %all-gather.3.cloned.1.call-update) | async-done | bytes 2097168 | tf_op jit(solution)/shard_map/all_gather | solution.py:87
  74.9 2.1 convert_reduce_fusion
  77.8 1.0 fusion.9
  79.6 1.4 copy-done.5
  82.6 24.2 %all-reduce = (bf16[256,16]{0,1:T(8,128)(2,1)S(1)}, bf16[256,16]{0,1:T(8,128)(2,1)S(1)}, bf16[256,16]{0,1:T(8,128)(2,1)S(1)}) all-reduce(f32[256,16]{0,1:T(8,128)S(1)} %get-tuple-element.6, f32[256,16]{0,1:T(8,128)S(1)} %get-tuple-element.7, f32[256,16]{0,1:T(8,128)S(1)} %get-tuple-element.5), channel_id=1, replica_groups=mesh['req'=32,'mlp'=8] {'mlp'}, use_global_device_ids=true, to_apply=%region_14.15 | all-reduce | flops 12288 | bytes 73728 | tf_op jit(solution)/shard_map/psum | solution.py:102
  106.8 1.1 broadcast_multiply_fusion.1
  107.9 163.1 %all-gather.5.cloned.1.call-done = bf16[4096,3072]{0,1:T(8,128)(2,1)} async-done(((bf16[128,3072]{0,1:T(8,128)(2,1)}), bf16[4096,3072]{0,1:T(8,128)(2,1)}) %all-gather.5.cloned.1.call-update) | async-done | bytes 25165840 | tf_op jit(solution)/shard_map/all_gather | solution.py:119
  270.9 8.4 %fusion = f32[256,1792]{1,0:T(8,128)S(1)} fusion(bf16[256,4096]{1,0:T(8,128)(2,1)} %copy-done.2, bf16[4096,3072]{0,1:T(8,128)(2,1)} %all-gather.5.cloned.1.call-done), kind=kOutput, calls=%fused_computation | convolution fusion | flops 3758096384 | bytes 18612224 | tf_op jit(solution)/shard_map/dot_general | solution.py:121
  279.4 1.3 copy-done.12
  281.0 1.2 slice.41
  282.3 1.3 slice.42
  283.6 1.0 slice_bitcast_fusion
  284.6 1.2 slice.45
  285.8 1.9 slice.46
  288.5 1.5 fusion.59
  290.6 1.3 fusion.80
  292.0 1.6 fusion.14
  293.7 2.2 fusion.19
  295.9 8.9 %fusion.2 = f32[256,4096]{1,0:T(8,128)} fusion(bf16[4096,3072]{0,1:T(8,128)(2,1)} %all-gather.5.cloned.1.call-done, bf16[256,1024]{1,0:T(8,128)(2,1)S(1)} %fusion.19, bf16[256,256]{1,0:T(8,128)(2,1)S(1)} %fusion.14), kind=kOutput, calls=%fused_computation.2 | convolution fusion | flops 2685665280 | bytes 15335424 | tf_op jit(solution)/shard_map/dot_general | solution.py:145
  304.8 40.4 %reduce-scatter.2.cloned.1.call-done = f32[256,512]{1,0:T(8,128)} async-done(((f32[256,4096]{1,0:T(8,128)}), f32[256,512]{1,0:T(8,128)}) %reduce-scatter.2.cloned.1.call-update) | async-done | bytes 524304 | tf_op jit(solution)/shard_map/reduce_scatter | solution.py:151
  345.2 1.1 add_convert_fusion
  347.2 26.9 %all_to_all.20 = bf16[32,2,4096]{2,1,0:T(2,128)(2,1)} all-to-all(bf16[32,2,4096]{2,1,0:T(2,128)(2,1)S(1)} %reshape.349), channel_id=1, replica_groups=mesh['req'=32,'mlp'=8] {'req'}, dimensions={0} | all-to-all | bytes 1048576 | tf_op jit(solution)/shard_map/all_to_all | solution.py:156
  374.1 1.2 reshape.350
  (100 shorter events, 16.2 us)
Async XLA Ops:
  6.5 287.1 %copy-start = (bf16[1024,1024]{1,0:T(8,128)(2,1)S(1)}, bf16[1024,1024]{1,0:T(8,128)(2,1)}, u32[]{:S(2)}) copy-start(bf16[1024,1024]{1,0:T(8,128)(2,1)} %param.37) | copy-start | bytes 6291460
  8.2 23.9 %copy-start.18 = (s32[32]{0:T(128)}, s32[32]{0:T(128)S(1)}, u32[]{:S(2)}) copy-start(s32[32]{0:T(128)S(1)} %multiply_add_fusion.1) | copy-start | bytes 388
  9.0 18.3 %all-to-all-start = ((bf16[32,1,2]{2,1,0:T(2,128)(2,1)}), bf16[32,1,2]{2,1,0:T(2,128)(2,1)S(1)}, u32[]{:S(2)}, u32[]{:S(2)}) async-start(bf16[32,1,2]{2,1,0:T(2,128)(2,1)} %all_to_all.16), calls=%async_computation | async-start | bytes 32768 | tf_op jit(solution)/shard_map/all_to_all | solution.py:74
  22.3 26.7 %copy-start.13 = (bf16[128,256]{1,0:T(8,128)(2,1)S(1)}, bf16[128,256]{1,0:T(8,128)(2,1)}, u32[]{:S(2)}) copy-start(bf16[128,256]{1,0:T(8,128)(2,1)} %param.26) | copy-start | bytes 196612
  22.3 29.4 %copy-start.11 = (bf16[128,1024]{1,0:T(8,128)(2,1)S(1)}, bf16[128,1024]{1,0:T(8,128)(2,1)}, u32[]{:S(2)}) copy-start(bf16[128,1024]{1,0:T(8,128)(2,1)} %param.34) | copy-start | bytes 786436
  27.4 20.2 %all-to-all-start.1 = ((bf16[32,2,4096]{2,1,0:T(2,128)(2,1)}), bf16[32,2,4096]{2,1,0:T(2,128)(2,1)S(1)}, u32[]{:S(2)}, u32[]{:S(2)}) async-start(bf16[32,2,4096]{2,1,0:T(2,128)(2,1)} %reshape.339), calls=%async_computation.1 | async-start | bytes 1048576 | tf_op jit(solution)/shard_map/all_to_all | solution.py:73
  32.0 42.8 %all-gather.3.cloned.1.call-start = ((), (), s32[]{:S(2)}) async-start(), calls=%async_computation.4 | async-start | bytes 2359296 | tf_op jit(solution)/shard_map/all_gather | solution.py:87
  32.1 16.9 %copy-start.20 = (f32[32]{0:T(128)}, f32[32]{0:T(128)S(1)}, u32[]{:S(2)}) copy-start(f32[32]{0:T(128)S(1)} %iota_convert_fusion) | copy-start | bytes 388
  48.1 8.1 %copy-start.16 = (s32[256]{0:T(256)S(1)}, s32[256]{0:T(256)}, u32[]{:S(2)}) copy-start(s32[256]{0:T(256)} %param.22) | copy-start | bytes 3076
  48.1 8.2 %copy-start.22 = (s32[256]{0:T(256)S(1)}, s32[256]{0:T(256)}, u32[]{:S(2)}) copy-start(s32[256]{0:T(256)} %param.23) | copy-start | bytes 3076
  48.9 222.0 %all-gather.5.cloned.1.call-start = ((), (), s32[]{:S(2)}) async-start(), calls=%async_computation.5 | async-start | bytes 25952256 | tf_op jit(solution)/shard_map/all_gather | solution.py:119
  54.6 0.9 copy-start.7
  55.5 289.7 %reduce-scatter.2.cloned.1.call-start = ((), (), s32[]{:S(2)}) async-start(), calls=%async_computation.6 | async-start | bytes 4718592 | tf_op jit(solution)/shard_map/reduce_scatter | solution.py:151
  74.9 2.2 copy-start.1
  74.9 2.9 copy-start.14
  74.9 2.9 copy-start.15
  77.8 1.2 copy-start.4
  79.0 2.6 copy-start.2
  79.0 2.0 copy-start.5
  79.0 2.6 copy-start.6
  107.9 172.8 %copy-start.8 = (bf16[1024,256]{1,0:T(8,128)(2,1)S(1)}, bf16[1024,256]{1,0:T(8,128)(2,1)}, u32[]{:S(2)}) copy-start(bf16[1024,256]{1,0:T(8,128)(2,1)} %param.31) | copy-start | bytes 1572868
  279.4 1.3 copy-start.12
  284.6 7.5 %copy-start.10 = (bf16[256,64,16]{0,2,1:T(8,128)(2,1)S(1)}, bf16[256,64,16]{0,2,1:T(8,128)(2,1)}, u32[]{:S(2)}) copy-start(bf16[256,64,16]{0,2,1:T(8,128)(2,1)} %get-tuple-element.17) | copy-start | bytes 1572868
  290.2 3.4 copy-start.9
  304.8 40.4 %copy-start.3 = (bf16[256,512]{1,0:T(8,128)(2,1)S(1)}, bf16[256,512]{1,0:T(8,128)(2,1)}, u32[]{:S(2)}) copy-start(bf16[256,512]{1,0:T(8,128)(2,1)} %reshape.341) | copy-start | bytes 786436
  304.8 40.4 %copy-start.17 = (f32[512]{0:T(512)S(1)}, f32[512]{0:T(512)}, u32[]{:S(2)}) copy-start(f32[512]{0:T(512)} %param.39) | copy-start | bytes 6148
  304.8 41.7 %copy-start.21 = (f32[32]{0:T(128)S(1)}, f32[32]{0:T(128)}, u32[]{:S(2)}) copy-start(f32[32]{0:T(128)} %copy-done.20) | copy-start | bytes 388
  346.4 28.9 %copy-start.19 = (s32[32]{0:T(128)S(1)}, s32[32]{0:T(128)}, u32[]{:S(2)}) copy-start(s32[32]{0:T(128)} %copy-done.18) | copy-start | bytes 388
Sparse Core Ops, SparseCore 0:
  49.0 25.7 all-gather.2
  77.3 193.5 all-gather.4
  304.9 40.2 reduce-scatter.1

commit v2 on v1

--- a/solution.py
+++ b/solution.py
@@ -84,7 +84,10 @@
     )
     own_x = own_x.astype(jnp.bfloat16).reshape(tok, width_m)
     column = lax.axis_index("mlp") * width_m
-    whole = lax.all_gather(own_x, "mlp", axis=1, tiled=True).astype(jnp.float32)
+    n_mlp = lax.axis_size("mlp")
+    copies = jnp.broadcast_to(own_x[None], (n_mlp, tok, width_m))
+    spread_x = lax.all_to_all(copies, "mlp", split_axis=0, concat_axis=0, tiled=True)
+    whole = jnp.transpose(spread_x, (1, 0, 2)).reshape(tok, n_mlp * width_m).astype(jnp.float32)
     mean = jnp.mean(whole, axis=1, keepdims=True)
     var = jnp.mean(jnp.square(whole - mean), axis=1, keepdims=True)
     full_ln = ((whole - mean) * lax.rsqrt(var + EPS) * ln_gain + ln_bias).astype(jnp.bfloat16)

time: 384 us -> 338 us (0.88)
  waiting for transfers between devices: 242 us -> 178 us
  starting transfers between devices: 15.4 us -> 23.1 us
  local copies, waits for them, and re-layouts: 24 us -> 29.5 us
    all_gather x1, waiting for transfers between devices: 163 us -> 89.8 us  [on_device(): gathered = lax.all_gather(packed, 'req', axis=0, tiled=True)]
    all_to_all x0 -> x1, waiting for transfers between devices: none -> 23.7 us  [on_device(): lax.all_to_all(copies, 'mlp', split_axis=0, concat_axis=0, tiled=True)]
    all_gather x1 -> x0, waiting for transfers between devices: 18.4 us -> none  [on_device(): whole = lax.all_gather(own_x, 'mlp', axis=1, tiled=True).astype(jnp.float32)]
    all_to_all x0 -> x1, starting transfers between devices: none -> 7.83 us  [on_device(): lax.all_to_all(copies, 'mlp', split_axis=0, concat_axis=0, tiled=True)]
    all_to_all x1, waiting for transfers between devices: 14.9 us -> 19.5 us  [on_device(): lax.all_to_all(outgoing, 'req', split_axis=0, concat_axis=0, tiled=True)]
    unnamed x57 -> x59, local copies, waits for them, and re-layouts: 10.3 us -> 11.3 us
  transfers between devices with their start and end apart: 5 -> 5, of which waited for: 5 -> 5; matrix products, arithmetic and copies ran while one was open for 4% -> 5% of each run, Pallas kernels for 0% -> 0%
where the time goes in v2:
time: 338 us; the launch traced here: 337 us
  waiting for transfers between devices  178 us (53%)
  blocking collectives  52.1 us (15%)
  local copies, waits for them, and re-layouts  29.5 us (9%)
  matrix products  26.7 us (8%)
  starting transfers between devices  23.1 us (7%)
  between operations  13.9 us (4%)
  other arithmetic  12.9 us (4%)
    all_gather x1, waiting for transfers between devices, on_device(): gathered = lax.all_gather(packed, 'req', axis=0, tiled=True)  89.8 us
    reduce_scatter x1, waiting for transfers between devices, on_device(): shares = lax.psum_scatter(part, 'mlp', scatter_dimension=1, tiled=True)  40.4 us
    all_to_all x1, blocking collectives, on_device(): lax.all_to_all(leaving, 'req', split_axis=0, concat_axis=0, tiled=True)  26.5 us
    psum x1, blocking collectives, on_device(): lax.psum((pick(down_query), pick(down_value), pick(down_fc)), 'mlp')  25.6 us
    all_to_all x1, waiting for transfers between devices, on_device(): lax.all_to_all(copies, 'mlp', split_axis=0, concat_axis=0, tiled=True)  23.7 us
    all_to_all x1, waiting for transfers between devices, on_device(): lax.all_to_all(outgoing, 'req', split_axis=0, concat_axis=0, tiled=True)  19.5 us
    unnamed x59, local copies, waits for them, and re-layouts  11.3 us
    all_to_all x1, starting transfers between devices, on_device(): lax.all_to_all(filled, 'req', split_axis=0, concat_axis=0, tiled=True)  10.6 us
  transfers between devices with their start and end apart: 5, of which 5 were waited for; matrix products, arithmetic and copies ran while one was open for 5% of the time, Pallas kernels for 0%

profile of v2, /device:TPU:57, one launch (start us, length us, event | category | flops | bytes accessed | tf_op | source)
XLA Modules:
  0.0 336.7 jit_solution(6975800151234359856)
XLA Ops:
  6.5 1.1 copy.67
  9.6 1.1 copy.70
  13.7 10.6 %all-to-all-start = ((bf16[32,1,2]{2,1,0:T(2,128)(2,1)}), bf16[32,1,2]{2,1,0:T(2,128)(2,1)S(1)}, u32[]{:S(2)}, u32[]{:S(2)}) async-start(bf16[32,1,2]{2,1,0:T(2,128)(2,1)} %all_to_all.20), calls=%async_computation | async-start | bytes 32768 | tf_op jit(solution)/shard_map/all_to_all | solution.py:74
  25.8 1.2 reshape.348
  27.0 5.1 %all-to-all-done = bf16[32,1,2]{2,1,0:T(2,128)(2,1)S(1)} async-done(((bf16[32,1,2]{2,1,0:T(2,128)(2,1)}), bf16[32,1,2]{2,1,0:T(2,128)(2,1)S(1)}, u32[]{:S(2)}, u32[]{:S(2)}) %all-to-all-start) | async-done | bytes 160 | tf_op jit(solution)/shard_map/all_to_all | solution.py:74
  32.0 4.7 %all-to-all-start.1 = ((bf16[32,2,4096]{2,1,0:T(2,128)(2,1)}), bf16[32,2,4096]{2,1,0:T(2,128)(2,1)S(1)}, u32[]{:S(2)}, u32[]{:S(2)}) async-start(bf16[32,2,4096]{2,1,0:T(2,128)(2,1)} %reshape.348), calls=%async_computation.1 | async-start | bytes 1048576 | tf_op jit(solution)/shard_map/all_to_all | solution.py:73
  37.3 19.5 %all-to-all-done.1 = bf16[32,2,4096]{2,1,0:T(2,128)(2,1)S(1)} async-done(((bf16[32,2,4096]{2,1,0:T(2,128)(2,1)}), bf16[32,2,4096]{2,1,0:T(2,128)(2,1)S(1)}, u32[]{:S(2)}, u32[]{:S(2)}) %all-to-all-start.1) | async-done | bytes 524320 | tf_op jit(solution)/shard_map/all_to_all | solution.py:73
  57.5 1.4 broadcast_in_dim.13
  59.0 7.8 %all-to-all-start.2 = ((bf16[8,256,512]{1,2,0:T(8,128)(2,1)}), bf16[8,256,512]{1,2,0:T(8,128)(2,1)}, u32[]{:S(2)}, u32[]{:S(2)}) async-start(bf16[8,256,512]{1,2,0:T(8,128)(2,1)} %broadcast_in_dim.13), calls=%async_computation.2 | async-start | bytes 4194304 | tf_op jit(solution)/shard_map/all_to_all | solution.py:89
  67.7 23.7 %all-to-all-done.2 = bf16[8,256,512]{1,2,0:T(8,128)(2,1)} async-done(((bf16[8,256,512]{1,2,0:T(8,128)(2,1)}), bf16[8,256,512]{1,2,0:T(8,128)(2,1)}, u32[]{:S(2)}, u32[]{:S(2)}) %all-to-all-start.2) | async-done | bytes 2097184 | tf_op jit(solution)/shard_map/all_to_all | solution.py:89
  91.4 2.1 convert_reduce_fusion
  93.6 2.3 multiply_reduce_fusion
  95.9 2.6 fusion.7
  99.1 1.4 copy-done.3
  102.1 25.6 %all-reduce = (bf16[256,16]{0,1:T(8,128)(2,1)S(1)}, bf16[256,16]{0,1:T(8,128)(2,1)S(1)}, bf16[256,16]{0,1:T(8,128)(2,1)S(1)}) all-reduce(f32[256,16]{0,1:T(8,128)S(1)} %get-tuple-element.6, f32[256,16]{0,1:T(8,128)S(1)} %get-tuple-element.7, f32[256,16]{0,1:T(8,128)S(1)} %get-tuple-element.5), channel_id=1, replica_groups=mesh['req'=32,'mlp'=8] {'mlp'}, use_global_device_ids=true, to_apply=%region_14.15 | all-reduce | flops 12288 | bytes 73728 | tf_op jit(solution)/shard_map/psum | solution.py:105
  128.8 89.8 %all-gather.2.cloned.1.call-done = bf16[4096,3072]{0,1:T(8,128)(2,1)} async-done(((bf16[128,3072]{0,1:T(8,128)(2,1)}), bf16[4096,3072]{0,1:T(8,128)(2,1)}) %all-gather.2.cloned.1.call-update) | async-done | bytes 25165840 | tf_op jit(solution)/shard_map/all_gather | solution.py:122
  218.6 8.5 %fusion = f32[256,1792]{1,0:T(8,128)S(1)} fusion(bf16[256,4096]{0,1:T(8,128)(2,1)} %copy-done.1, bf16[4096,3072]{0,1:T(8,128)(2,1)} %all-gather.2.cloned.1.call-done), kind=kOutput, calls=%fused_computation | convolution fusion | flops 3758096384 | bytes 18612224 | tf_op jit(solution)/shard_map/dot_general | solution.py:124
  227.2 1.3 copy-done.11
  228.8 1.2 slice.41
  230.1 1.9 slice.42
  232.9 1.8 slice.45
  234.8 1.9 slice.46
  237.5 1.6 fusion.57
  239.9 1.5 copy.75
  243.0 1.3 fusion.78
  245.1 2.4 fusion.12
  247.5 2.2 fusion.17
  249.8 8.8 %fusion.2 = f32[256,4096]{1,0:T(8,128)} fusion(bf16[4096,3072]{0,1:T(8,128)(2,1)} %all-gather.2.cloned.1.call-done, bf16[256,1024]{1,0:T(8,128)(2,1)S(1)} %fusion.17, bf16[256,256]{1,0:T(8,128)(2,1)S(1)} %copy-done.23), kind=kOutput, calls=%fused_computation.2 | convolution fusion | flops 2685665280 | bytes 15335424 | tf_op jit(solution)/shard_map/dot_general | solution.py:148
  258.6 40.4 %reduce-scatter.2.cloned.1.call-done = f32[256,512]{1,0:T(8,128)} async-done(((f32[256,4096]{1,0:T(8,128)}), f32[256,512]{1,0:T(8,128)}) %reduce-scatter.2.cloned.1.call-update) | async-done | bytes 524304 | tf_op jit(solution)/shard_map/reduce_scatter | solution.py:154
  299.0 1.1 add_convert_fusion
  301.1 26.5 %all_to_all.25 = bf16[32,2,4096]{2,1,0:T(2,128)(2,1)} all-to-all(bf16[32,2,4096]{2,1,0:T(2,128)(2,1)S(1)} %reshape.358), channel_id=1, replica_groups=mesh['req'=32,'mlp'=8] {'req'}, dimensions={0} | all-to-all | bytes 1048576 | tf_op jit(solution)/shard_map/all_to_all | solution.py:159
  327.6 1.2 reshape.359
  (103 shorter events, 18.9 us)
Async XLA Ops:
  6.5 241.0 %copy-start = (bf16[1024,1024]{1,0:T(8,128)(2,1)S(1)}, bf16[1024,1024]{1,0:T(8,128)(2,1)}, u32[]{:S(2)}) copy-start(bf16[1024,1024]{1,0:T(8,128)(2,1)} %param.37) | copy-start | bytes 6291460
  6.5 5.1 %copy-start.9 = (bf16[1024,128]{1,0:T(8,128)(2,1)S(1)}, bf16[1024,128]{1,0:T(8,128)(2,1)}, u32[]{:S(2)}) copy-start(bf16[1024,128]{1,0:T(8,128)(2,1)} %param.38) | copy-start | bytes 786436
  6.5 6.1 %copy-start.22 = (s32[32]{0:T(128)S(1)}, s32[32]{0:T(128)}, u32[]{:S(2)}) copy-start(s32[32]{0:T(128)} %param.21) | copy-start | bytes 388
  6.5 212.1 %all-gather.2.cloned.1.call-start = ((), (), s32[]{:S(2)}) async-start(), calls=%async_computation.5 | async-start | bytes 25952256 | tf_op jit(solution)/shard_map/all_gather | solution.py:122
  11.7 0.9 copy-start.5
  12.8 24.4 %copy-start.16 = (s32[32]{0:T(128)}, s32[32]{0:T(128)S(1)}, u32[]{:S(2)}) copy-start(s32[32]{0:T(128)S(1)} %multiply_add_fusion.1) | copy-start | bytes 388
  13.7 18.3 %all-to-all-start = ((bf16[32,1,2]{2,1,0:T(2,128)(2,1)}), bf16[32,1,2]{2,1,0:T(2,128)(2,1)S(1)}, u32[]{:S(2)}, u32[]{:S(2)}) async-start(bf16[32,1,2]{2,1,0:T(2,128)(2,1)} %all_to_all.20), calls=%async_computation | async-start | bytes 32768 | tf_op jit(solution)/shard_map/all_to_all | solution.py:74
  32.0 24.8 %all-to-all-start.1 = ((bf16[32,2,4096]{2,1,0:T(2,128)(2,1)}), bf16[32,2,4096]{2,1,0:T(2,128)(2,1)S(1)}, u32[]{:S(2)}, u32[]{:S(2)}) async-start(bf16[32,2,4096]{2,1,0:T(2,128)(2,1)} %reshape.348), calls=%async_computation.1 | async-start | bytes 1048576 | tf_op jit(solution)/shard_map/all_to_all | solution.py:73
  36.7 22.2 %copy-start.18 = (f32[32]{0:T(128)}, f32[32]{0:T(128)S(1)}, u32[]{:S(2)}) copy-start(f32[32]{0:T(128)S(1)} %iota_convert_fusion) | copy-start | bytes 388
  59.0 8.4 %copy-start.14 = (s32[256]{0:T(256)S(1)}, s32[256]{0:T(256)}, u32[]{:S(2)}) copy-start(s32[256]{0:T(256)} %param.22) | copy-start | bytes 3076
  59.0 8.5 %copy-start.20 = (s32[256]{0:T(256)S(1)}, s32[256]{0:T(256)}, u32[]{:S(2)}) copy-start(s32[256]{0:T(256)} %param.23) | copy-start | bytes 3076
  59.0 32.5 %all-to-all-start.2 = ((bf16[8,256,512]{1,2,0:T(8,128)(2,1)}), bf16[8,256,512]{1,2,0:T(8,128)(2,1)}, u32[]{:S(2)}, u32[]{:S(2)}) async-start(bf16[8,256,512]{1,2,0:T(8,128)(2,1)} %broadcast_in_dim.13), calls=%async_computation.2 | async-start | bytes 4194304 | tf_op jit(solution)/shard_map/all_to_all | solution.py:89
  66.8 232.2 %reduce-scatter.2.cloned.1.call-start = ((), (), s32[]{:S(2)}) async-start(), calls=%async_computation.6 | async-start | bytes 4718592 | tf_op jit(solution)/shard_map/reduce_scatter | solution.py:154
  67.7 28.2 %copy-start.12 = (f32[4096]{0:T(1024)S(1)}, f32[4096]{0:T(1024)}, u32[]{:S(2)}) copy-start(f32[4096]{0:T(1024)} %param.25) | copy-start | bytes 49156
  67.7 28.2 %copy-start.13 = (f32[4096]{0:T(1024)S(1)}, f32[4096]{0:T(1024)}, u32[]{:S(2)}) copy-start(f32[4096]{0:T(1024)} %param.24) | copy-start | bytes 49156
  95.9 2.6 copy-start.2
  98.5 2.6 copy-start.1
  98.5 2.0 copy-start.3
  98.6 2.6 copy-start.4
  218.6 9.9 %copy-start.6 = (bf16[1024,256]{1,0:T(8,128)(2,1)S(1)}, bf16[1024,256]{1,0:T(8,128)(2,1)}, u32[]{:S(2)}) copy-start(bf16[1024,256]{1,0:T(8,128)(2,1)} %param.31) | copy-start | bytes 1572868
  227.2 1.3 copy-start.11
  232.9 12.2 %copy-start.8 = (bf16[256,64,16]{0,2,1:T(8,128)(2,1)S(1)}, bf16[256,64,16]{0,2,1:T(8,128)(2,1)}, u32[]{:S(2)}) copy-start(bf16[256,64,16]{0,2,1:T(8,128)(2,1)} %get-tuple-element.17) | copy-start | bytes 1572868
  239.9 7.6 %copy-start.7 = (bf16[256,64,16]{0,2,1:T(8,128)(2,1)S(1)}, bf16[256,64,16]{0,2,1:T(8,128)(2,1)}, u32[]{:S(2)}) copy-start(bf16[256,64,16]{0,2,1:T(8,128)(2,1)} %get-tuple-element.16) | copy-start | bytes 1572868
  239.9 7.6 %copy-start.21 = (f32[1024]{0:T(1024)S(1)}, f32[1024]{0:T(1024)}, u32[]{:S(2)}) copy-start(f32[1024]{0:T(1024)} %param.35) | copy-start | bytes 12292
  244.4 0.7 copy-start.10
  247.5 2.3 copy-start.23
  258.6 40.4 %copy-start.15 = (f32[512]{0:T(512)S(1)}, f32[512]{0:T(512)}, u32[]{:S(2)}) copy-start(f32[512]{0:T(512)} %param.39) | copy-start | bytes 6148
  258.6 41.7 %copy-start.19 = (f32[32]{0:T(128)S(1)}, f32[32]{0:T(128)}, u32[]{:S(2)}) copy-start(f32[32]{0:T(128)} %copy-done.18) | copy-start | bytes 388
  300.3 28.5 %copy-start.17 = (s32[32]{0:T(128)S(1)}, s32[32]{0:T(128)}, u32[]{:S(2)}) copy-start(s32[32]{0:T(128)} %copy-done.16) | copy-start | bytes 388
Sparse Core Ops, SparseCore 0:
  12.8 205.7 all-gather.1
  258.8 40.2 reduce-scatter.1

commit v3 on v2

--- a/solution.py
+++ b/solution.py
@@ -116,9 +116,9 @@
     mask = (request_id[:, None] == request_id[None, :]) & (row_iota[None, :] <= row_iota[:, None])
     heads_w = w_query.shape[1]
     ff_w = w_fc_in.shape[1]
-    packed = jnp.concatenate(
-        [w_query, w_key, w_value, w_fc_in, w_attn_out.T, w_fc_out.T], axis=1
-    )
+    packed = jnp.concatenate([w_query, w_key, w_value, w_fc_in, w_attn_out.T], axis=1)
+    fo_copies = jnp.broadcast_to(w_fc_out[None], (groups,) + w_fc_out.shape)
+    fo_rows = lax.all_to_all(fo_copies, "req", split_axis=0, concat_axis=0, tiled=True)
     gathered = lax.all_gather(packed, "req", axis=0, tiled=True)
     n_in = 3 * heads_w + ff_w
     base = jnp.dot(full_ln, gathered[:, :n_in], preferred_element_type=jnp.float32)
@@ -144,13 +144,15 @@
     hidden_pre = base[:, 3 * heads_w :]
     hidden_pre = hidden_pre + lift(picked[2], up_fc) + b_fc_in
     hidden = gelu_tanh(hidden_pre).astype(jnp.bfloat16)
-    joined = jnp.concatenate([attn, hidden], axis=1)
     part = lax.dot_general(
-        joined,
+        attn,
         gathered[:, n_in:],
         (((1,), (1,)), ((), ())),
         preferred_element_type=jnp.float32,
     )
+    part = part + jnp.einsum(
+        "tf,rfc->trc", hidden, fo_rows, preferred_element_type=jnp.float32
+    ).reshape(tok, groups * fo_rows.shape[2])
     shares = lax.psum_scatter(part, "mlp", scatter_dimension=1, tiled=True)
     result = (own_x.astype(jnp.float32) + shares + b_fc_out).astype(jnp.bfloat16)
     back_flat = result.reshape(pg_dev, page_len * width_m)

time: 338 us -> 443 us (1.31)
  waiting for transfers between devices: 178 us -> 273 us
  starting transfers between devices: 23.1 us -> 27.7 us
    all_gather x1, waiting for transfers between devices: 89.8 us -> 167 us  [on_device(): gathered = lax.all_gather(packed, 'req', axis=0, tiled=True)]
    all_to_all x0 -> x1, waiting for transfers between devices: none -> 12.2 us  [on_device(): lax.all_to_all(fo_copies, 'req', split_axis=0, concat_axis=0, tiled=True)]
    reshape x0 -> x1, matrix products: none -> 8.91 us  [on_device(): part = part + jnp.einsum('tf,rfc->trc', hidden, fo_rows, preferred_elemen...]
    dot_general x2 -> x1, matrix products: 11.2 us -> 5.79 us  [on_device(): lax.dot_general(attn, gathered[:, n_in:], (((1,), (1,)), ((), ())), prefe...]
    all_to_all x0 -> x1, starting transfers between devices: none -> 4.88 us  [on_device(): lax.all_to_all(fo_copies, 'req', split_axis=0, concat_axis=0, tiled=True)]
    unnamed x59 -> x44, local copies, waits for them, and re-layouts: 11.3 us -> 8.65 us
  transfers between devices with their start and end apart: 5 -> 6, of which waited for: 5 -> 6; matrix products, arithmetic and copies ran while one was open for 5% -> 11% of each run, Pallas kernels for 0% -> 0%
where the time goes in v3:
time: 443 us; the launch traced here: 442 us
  waiting for transfers between devices  273 us (62%)
  blocking collectives  52.7 us (12%)
  matrix products  30.4 us (7%)
  local copies, waits for them, and re-layouts  29.9 us (7%)
  starting transfers between devices  27.7 us (6%)
  other arithmetic  14.7 us (3%)
  between operations  13.9 us (3%)
    all_gather x1, waiting for transfers between devices, on_device(): gathered = lax.all_gather(packed, 'req', axis=0, tiled=True)  167 us
    reduce_scatter x1, waiting for transfers between devices, on_device(): shares = lax.psum_scatter(part, 'mlp', scatter_dimension=1, tiled=True)  43.3 us
    all_to_all x1, blocking collectives, on_device(): lax.all_to_all(leaving, 'req', split_axis=0, concat_axis=0, tiled=True)  26.9 us
    psum x1, blocking collectives, on_device(): lax.psum((pick(down_query), pick(down_value), pick(down_fc)), 'mlp')  25.8 us
    all_to_all x1, waiting for transfers between devices, on_device(): lax.all_to_all(copies, 'mlp', split_axis=0, concat_axis=0, tiled=True)  24.5 us
    all_to_all x1, waiting for transfers between devices, on_device(): lax.all_to_all(outgoing, 'req', split_axis=0, concat_axis=0, tiled=True)  21.4 us
    all_to_all x1, waiting for transfers between devices, on_device(): lax.all_to_all(fo_copies, 'req', split_axis=0, concat_axis=0, tiled=True)  12.2 us
    all_to_all x1, starting transfers between devices, on_device(): lax.all_to_all(filled, 'req', split_axis=0, concat_axis=0, tiled=True)  10.6 us
  transfers between devices with their start and end apart: 6, of which 6 were waited for; matrix products, arithmetic and copies ran while one was open for 11% of the time, Pallas kernels for 0%

profile of v3, /device:TPU:57, one launch (start us, length us, event | category | flops | bytes accessed | tf_op | source)
XLA Modules:
  0.0 442.5 jit_solution(15995266762931642183)
XLA Ops:
  14.4 10.6 %all-to-all-start = ((bf16[32,1,2]{2,1,0:T(2,128)(2,1)}), bf16[32,1,2]{2,1,0:T(2,128)(2,1)S(1)}, u32[]{:S(2)}, u32[]{:S(2)}) async-start(bf16[32,1,2]{2,1,0:T(2,128)(2,1)} %all_to_all.24), calls=%async_computation | async-start | bytes 32768 | tf_op jit(solution)/shard_map/all_to_all | solution.py:74
  26.5 1.1 reshape.352
  27.6 5.2 %all-to-all-done = bf16[32,1,2]{2,1,0:T(2,128)(2,1)S(1)} async-done(((bf16[32,1,2]{2,1,0:T(2,128)(2,1)}), bf16[32,1,2]{2,1,0:T(2,128)(2,1)S(1)}, u32[]{:S(2)}, u32[]{:S(2)}) %all-to-all-start) | async-done | bytes 160 | tf_op jit(solution)/shard_map/all_to_all | solution.py:74
  32.8 4.6 %all-to-all-start.1 = ((bf16[32,2,4096]{2,1,0:T(2,128)(2,1)}), bf16[32,2,4096]{2,1,0:T(2,128)(2,1)S(1)}, u32[]{:S(2)}, u32[]{:S(2)}) async-start(bf16[32,2,4096]{2,1,0:T(2,128)(2,1)} %reshape.352), calls=%async_computation.1 | async-start | bytes 1048576 | tf_op jit(solution)/shard_map/all_to_all | solution.py:73
  38.0 21.4 %all-to-all-done.1 = bf16[32,2,4096]{2,1,0:T(2,128)(2,1)S(1)} async-done(((bf16[32,2,4096]{2,1,0:T(2,128)(2,1)}), bf16[32,2,4096]{2,1,0:T(2,128)(2,1)S(1)}, u32[]{:S(2)}, u32[]{:S(2)}) %all-to-all-start.1) | async-done | bytes 524320 | tf_op jit(solution)/shard_map/all_to_all | solution.py:73
  60.2 1.5 broadcast_in_dim.15
  61.7 7.6 %all-to-all-start.2 = ((bf16[8,256,512]{1,2,0:T(8,128)(2,1)}), bf16[8,256,512]{1,2,0:T(8,128)(2,1)}, u32[]{:S(2)}, u32[]{:S(2)}) async-start(bf16[8,256,512]{1,2,0:T(8,128)(2,1)} %broadcast_in_dim.15), calls=%async_computation.2 | async-start | bytes 4194304 | tf_op jit(solution)/shard_map/all_to_all | solution.py:89
  69.4 24.5 %all-to-all-done.2 = bf16[8,256,512]{1,2,0:T(8,128)(2,1)} async-done(((bf16[8,256,512]{1,2,0:T(8,128)(2,1)}), bf16[8,256,512]{1,2,0:T(8,128)(2,1)}, u32[]{:S(2)}, u32[]{:S(2)}) %all-to-all-start.2) | async-done | bytes 2097184 | tf_op jit(solution)/shard_map/all_to_all | solution.py:89
  93.9 4.3 broadcast_in_dim.19
  98.2 4.9 %all-to-all-start.3 = ((bf16[32,1024,128]{1,2,0:T(8,128)(2,1)}), bf16[32,1024,128]{1,2,0:T(8,128)(2,1)}, u32[]{:S(2)}, u32[]{:S(2)}) async-start(bf16[32,1024,128]{1,2,0:T(8,128)(2,1)} %broadcast_in_dim.19), calls=%async_computation.3 | async-start | bytes 16777216 | tf_op jit(solution)/shard_map/all_to_all | solution.py:121
  104.6 2.3 convert_reduce_fusion
  106.9 2.3 multiply_reduce_fusion
  109.2 2.6 fusion.5
  114.0 25.8 %all-reduce = (bf16[256,16]{0,1:T(8,128)(2,1)S(1)}, bf16[256,16]{0,1:T(8,128)(2,1)S(1)}, bf16[256,16]{0,1:T(8,128)(2,1)S(1)}) all-reduce(f32[256,16]{0,1:T(8,128)S(1)} %get-tuple-element.6, f32[256,16]{0,1:T(8,128)S(1)} %get-tuple-element.7, f32[256,16]{0,1:T(8,128)S(1)} %get-tuple-element.5), channel_id=1, replica_groups=mesh['req'=32,'mlp'=8] {'mlp'}, use_global_device_ids=true, to_apply=%region_14.15 | all-reduce | flops 12288 | bytes 73728 | tf_op jit(solution)/shard_map/psum | solution.py:105
  140.7 166.7 %all-gather.2.cloned.1.call-done = bf16[4096,2048]{1,0:T(8,128)(2,1)} async-done(((bf16[128,2048]{1,0:T(8,128)(2,1)}), bf16[4096,2048]{1,0:T(8,128)(2,1)}) %all-gather.2.cloned.1.call-update) | async-done | bytes 16777232 | tf_op jit(solution)/shard_map/all_gather | solution.py:122
  307.3 8.6 %fusion = f32[256,1792]{1,0:T(8,128)S(1)} fusion(bf16[256,4096]{0,1:T(8,128)(2,1)} %copy-done.1, bf16[4096,2048]{1,0:T(8,128)(2,1)} %all-gather.2.cloned.1.call-done), kind=kOutput, calls=%fused_computation | convolution fusion | flops 3758096384 | bytes 18612224 | tf_op jit(solution)/shard_map/dot_general | solution.py:124
  315.9 1.2 copy-done.2
  317.8 2.1 slice.46
  319.9 2.6 slice.45
  322.6 2.2 fusion.9
  324.7 2.1 slice.41
  326.8 2.1 slice.42
  328.9 1.5 fusion.60
  331.0 1.2 fusion.47
  332.6 1.6 fusion.10
  334.2 12.2 %all-to-all-done.3 = bf16[32,1024,128]{1,2,0:T(8,128)(2,1)} async-done(((bf16[32,1024,128]{1,2,0:T(8,128)(2,1)}), bf16[32,1024,128]{1,2,0:T(8,128)(2,1)}, u32[]{:S(2)}, u32[]{:S(2)}) %all-to-all-start.3) | async-done | bytes 8388640 | tf_op jit(solution)/shard_map/all_to_all | solution.py:121
  346.4 8.9 %fusion.17 = f32[256,4096]{1,0:T(8,128)} fusion(bf16[1024,4096]{0,1:T(8,128)(2,1)} %bitcast.21, bf16[256,1024]{0,1:T(8,128)(2,1)S(1)} %bitcast.77, bf16[1024,1024]{1,0:T(8,128)(2,1)S(1)} %copy-done, f32[256,1792]{1,0:T(8,128)} %copy-done.2, f32[1024]{0:T(1024)S(1)} %copy-done.10), kind=kOutput, calls=%fused_computation.34 | convolution fusion | flops 2687238144 | bytes 16257024 | tf_op jit(solution)/shard_map/reshape | solution.py:155
  355.3 5.8 %convolution_add_fusion = f32[256,4096]{1,0:T(8,128)} fusion(f32[256,4096]{1,0:T(8,128)} %fusion.17, bf16[4096,2048]{1,0:T(8,128)(2,1)} %all-gather.2.cloned.1.call-done, bf16[256,256]{1,0:T(8,128)(2,1)S(1)} %fusion.10, f32[256,256]{0,1:T(8,128)S(1)} %get-tuple-element.23, f32[256]{0:T(256)S(1)} %fusion.24, f32[256]{0:T(256)S(1)} %get-tuple-element.22), kind=kOutput, calls=%fused_computation.2 | convolution fusion | flops 571736064 | bytes 10881024 | tf_op jit(solution)/shard_map/dot_general | solution.py:147
  361.1 43.3 %reduce-scatter.2.cloned.1.call-done = f32[256,512]{1,0:T(8,128)} async-done(((f32[256,4096]{1,0:T(8,128)}), f32[256,512]{1,0:T(8,128)}) %reduce-scatter.2.cloned.1.call-update) | async-done | bytes 524304 | tf_op jit(solution)/shard_map/reduce_scatter | solution.py:156
  404.4 1.1 add_convert_fusion
  406.4 26.9 %all_to_all.30 = bf16[32,2,4096]{2,1,0:T(2,128)(2,1)} all-to-all(bf16[32,2,4096]{2,1,0:T(2,128)(2,1)S(1)} %reshape.363), channel_id=1, replica_groups=mesh['req'=32,'mlp'=8] {'req'}, dimensions={0} | all-to-all | bytes 1048576 | tf_op jit(solution)/shard_map/all_to_all | solution.py:161
  433.3 1.2 reshape.364
  (91 shorter events, 18.8 us)
Async XLA Ops:
  6.5 339.8 %copy-start = (bf16[1024,1024]{1,0:T(8,128)(2,1)S(1)}, bf16[1024,1024]{1,0:T(8,128)(2,1)}, u32[]{:S(2)}) copy-start(bf16[1024,1024]{1,0:T(8,128)(2,1)} %param.37) | copy-start | bytes 6291460
  6.5 300.8 %all-gather.2.cloned.1.call-start = ((), (), s32[]{:S(2)}) async-start(), calls=%async_computation.6 | async-start | bytes 17301504 | tf_op jit(solution)/shard_map/all_gather | solution.py:122
  11.2 0.8 copy-start.6
  13.6 23.9 %copy-start.13 = (s32[32]{0:T(128)}, s32[32]{0:T(128)S(1)}, u32[]{:S(2)}) copy-start(s32[32]{0:T(128)S(1)} %multiply_add_fusion.1) | copy-start | bytes 388
  14.4 18.4 %all-to-all-start = ((bf16[32,1,2]{2,1,0:T(2,128)(2,1)}), bf16[32,1,2]{2,1,0:T(2,128)(2,1)S(1)}, u32[]{:S(2)}, u32[]{:S(2)}) async-start(bf16[32,1,2]{2,1,0:T(2,128)(2,1)} %all_to_all.24), calls=%async_computation | async-start | bytes 32768 | tf_op jit(solution)/shard_map/all_to_all | solution.py:74
  32.8 26.6 %all-to-all-start.1 = ((bf16[32,2,4096]{2,1,0:T(2,128)(2,1)}), bf16[32,2,4096]{2,1,0:T(2,128)(2,1)S(1)}, u32[]{:S(2)}, u32[]{:S(2)}) async-start(bf16[32,2,4096]{2,1,0:T(2,128)(2,1)} %reshape.352), calls=%async_computation.1 | async-start | bytes 1048576 | tf_op jit(solution)/shard_map/all_to_all | solution.py:73
  37.4 24.2 %copy-start.15 = (f32[32]{0:T(128)}, f32[32]{0:T(128)S(1)}, u32[]{:S(2)}) copy-start(f32[32]{0:T(128)S(1)} %iota_convert_fusion) | copy-start | bytes 388
  59.6 9.6 %copy-start.7 = (bf16[1024,128]{1,0:T(8,128)(2,1)S(1)}, bf16[1024,128]{1,0:T(8,128)(2,1)}, u32[]{:S(2)}) copy-start(bf16[1024,128]{1,0:T(8,128)(2,1)} %param.38) | copy-start | bytes 786436
  61.7 32.2 %all-to-all-start.2 = ((bf16[8,256,512]{1,2,0:T(8,128)(2,1)}), bf16[8,256,512]{1,2,0:T(8,128)(2,1)}, u32[]{:S(2)}, u32[]{:S(2)}) async-start(bf16[8,256,512]{1,2,0:T(8,128)(2,1)} %broadcast_in_dim.15), calls=%async_computation.2 | async-start | bytes 4194304 | tf_op jit(solution)/shard_map/all_to_all | solution.py:89
  98.2 5.5 %copy-start.11 = (s32[256]{0:T(256)S(1)}, s32[256]{0:T(256)}, u32[]{:S(2)}) copy-start(s32[256]{0:T(256)} %param.22) | copy-start | bytes 3076
  98.2 5.6 %copy-start.17 = (s32[256]{0:T(256)S(1)}, s32[256]{0:T(256)}, u32[]{:S(2)}) copy-start(s32[256]{0:T(256)} %param.23) | copy-start | bytes 3076
  98.2 248.2 %all-to-all-start.3 = ((bf16[32,1024,128]{1,2,0:T(8,128)(2,1)}), bf16[32,1024,128]{1,2,0:T(8,128)(2,1)}, u32[]{:S(2)}, u32[]{:S(2)}) async-start(bf16[32,1024,128]{1,2,0:T(8,128)(2,1)} %broadcast_in_dim.19), calls=%async_computation.3 | async-start | bytes 16777216 | tf_op jit(solution)/shard_map/all_to_all | solution.py:121
  103.1 6.1 %copy-start.8 = (f32[4096]{0:T(1024)S(1)}, f32[4096]{0:T(1024)}, u32[]{:S(2)}) copy-start(f32[4096]{0:T(1024)} %param.25) | copy-start | bytes 49156
  103.1 6.1 %copy-start.9 = (f32[4096]{0:T(1024)S(1)}, f32[4096]{0:T(1024)}, u32[]{:S(2)}) copy-start(f32[4096]{0:T(1024)} %param.24) | copy-start | bytes 49156
  103.1 301.3 %reduce-scatter.2.cloned.1.call-start = ((), (), s32[]{:S(2)}) async-start(), calls=%async_computation.7 | async-start | bytes 4718592 | tf_op jit(solution)/shard_map/reduce_scatter | solution.py:156
  104.6 7.2 %copy-start.3 = (bf16[512,1024]{1,0:T(8,128)(2,1)S(1)}, bf16[512,1024]{1,0:T(8,128)(2,1)}, u32[]{:S(2)}) copy-start(bf16[512,1024]{1,0:T(8,128)(2,1)} %param.30) | copy-start | bytes 3145732
  106.9 5.5 %copy-start.4 = (bf16[512,1024]{1,0:T(8,128)(2,1)S(1)}, bf16[512,1024]{1,0:T(8,128)(2,1)}, u32[]{:S(2)}) copy-start(bf16[512,1024]{1,0:T(8,128)(2,1)} %param.36) | copy-start | bytes 3145732
  109.2 3.8 copy-start.5
  111.8 2.2 copy-start.1
  315.9 1.2 copy-start.2
  317.1 29.3 %copy-start.10 = (f32[1024]{0:T(1024)S(1)}, f32[1024]{0:T(1024)}, u32[]{:S(2)}) copy-start(f32[1024]{0:T(1024)} %param.35) | copy-start | bytes 12292
  361.1 43.3 %copy-start.12 = (f32[512]{0:T(512)S(1)}, f32[512]{0:T(512)}, u32[]{:S(2)}) copy-start(f32[512]{0:T(512)} %param.39) | copy-start | bytes 6148
  361.1 44.6 %copy-start.16 = (f32[32]{0:T(128)S(1)}, f32[32]{0:T(128)}, u32[]{:S(2)}) copy-start(f32[32]{0:T(128)} %copy-done.15) | copy-start | bytes 388
  361.1 73.5 %copy-start.14 = (s32[32]{0:T(128)S(1)}, s32[32]{0:T(128)}, u32[]{:S(2)}) copy-start(s32[32]{0:T(128)} %copy-done.13) | copy-start | bytes 388
Sparse Core Ops, SparseCore 0:
  12.1 295.1 all-gather.1
  361.2 43.1 reduce-scatter.1

commit v4 on v2

--- a/solution.py
+++ b/solution.py
@@ -27,6 +27,19 @@
     turned = jnp.stack([even * cosine - odd * sine, odd * cosine + even * sine], axis=-1)
     turned = turned.reshape(block.shape[0], block.shape[1], ROT)
     return jnp.concatenate([turned, block[:, :, ROT:]], axis=2)
+
+
+def rotate_split(block, pos):
+    half = ROT // 2
+    freq = jnp.power(10000.0, -jnp.arange(half).astype(jnp.float32) * 2.0 / ROT)
+    angle = pos.astype(jnp.float32)[:, None, None] * freq[None, None, :]
+    cosine = jnp.cos(angle)
+    sine = jnp.sin(angle)
+    even = block[:, :, :half]
+    odd = block[:, :, half:ROT]
+    return jnp.concatenate(
+        [even * cosine - odd * sine, odd * cosine + even * sine, block[:, :, ROT:]], axis=2
+    )
 
 
 def on_device(
@@ -116,8 +129,14 @@
     mask = (request_id[:, None] == request_id[None, :]) & (row_iota[None, :] <= row_iota[:, None])
     heads_w = w_query.shape[1]
     ff_w = w_fc_in.shape[1]
+    def pair_major(w):
+        rows = w.shape[0]
+        lead = w[:, :ROT].reshape(rows, ROT // 2, 2).transpose(0, 2, 1).reshape(rows, ROT)
+        return jnp.concatenate([lead, w[:, ROT:]], axis=1)
+
     packed = jnp.concatenate(
-        [w_query, w_key, w_value, w_fc_in, w_attn_out.T, w_fc_out.T], axis=1
+        [pair_major(w_query), pair_major(w_key), w_value, w_fc_in, w_attn_out.T, w_fc_out.T],
+        axis=1,
     )
     gathered = lax.all_gather(packed, "req", axis=0, tiled=True)
     n_in = 3 * heads_w + ff_w
@@ -125,10 +144,10 @@
     base_q = base[:, :heads_w]
     base_k = base[:, heads_w : 2 * heads_w]
     base_v = base[:, 2 * heads_w : 3 * heads_w]
-    query = rotate(
-        (base_q + lift(picked[0], up_query)).reshape(tok, heads_w // HS, HS), pos
+    query = rotate_split(
+        (base_q + lift(picked[0], pair_major(up_query))).reshape(tok, heads_w // HS, HS), pos
     ).astype(jnp.bfloat16)
-    keys = rotate(base_k.reshape(tok, heads_w // HS, HS), pos).astype(jnp.bfloat16)
+    keys = rotate_split(base_k.reshape(tok, heads_w // HS, HS), pos).astype(jnp.bfloat16)
     value = (
         (base_v + lift(picked[1], up_value)).astype(jnp.bfloat16).reshape(tok, heads_w // HS, HS)
     )
@@ -151,7 +170,9 @@
         (((1,), (1,)), ((), ())),
         preferred_element_type=jnp.float32,
     )
-    shares = lax.psum_scatter(part, "mlp", scatter_dimension=1, tiled=True)
+    shares = lax.psum_scatter(
+        part.astype(jnp.bfloat16), "mlp", scatter_dimension=1, tiled=True
+    ).astype(jnp.float32)
     result = (own_x.astype(jnp.float32) + shares + b_fc_out).astype(jnp.bfloat16)
     back_flat = result.reshape(pg_dev, page_len * width_m)
     leaving = jnp.dot(take.T, back_flat, preferred_element_type=jnp.float32).astype(jnp.bfloat16)

time: 338 us -> 322 us (0.953)
  local copies, waits for them, and re-layouts: 29.5 us -> 21.3 us
  waiting for transfers between devices: 178 us -> 173 us
    reduce_scatter x1, waiting for transfers between devices: 40.4 us -> 36.1 us  [on_device(): lax.psum_scatter(part.astype(jnp.bfloat16), 'mlp', scatter_dimension=1, t...]
    concatenate x6 -> x2, local copies, waits for them, and re-layouts: 3.91 us -> 0.18 us  [the longest x1 0.14 us: rotate_split(): jnp.concatenate([even * cosine - odd * sine, odd * cosine + even * sine,...]
    slice x4 -> x8, local copies, waits for them, and re-layouts: 6.81 us -> 4.7 us  [the longest x3 2.89 us: pair_major(): return jnp.concatenate([lead, w[:, ROT:]], axis=1)]
    unnamed x59 -> x57, local copies, waits for them, and re-layouts: 11.3 us -> 9.75 us
  transfers between devices with their start and end apart: 5 -> 5, of which waited for: 5 -> 5; matrix products, arithmetic and copies ran while one was open for 5% -> 6% of each run, Pallas kernels for 0% -> 0%
where the time goes in v4:
time: 322 us; the launch traced here: 321 us
  waiting for transfers between devices  173 us (54%)
  blocking collectives  52.9 us (16%)
  matrix products  25.4 us (8%)
  starting transfers between devices  23.2 us (7%)
  local copies, waits for them, and re-layouts  21.3 us (7%)
  between operations  13.9 us (4%)
  other arithmetic  11.1 us (3%)
    all_gather x1, waiting for transfers between devices, on_device(): gathered = lax.all_gather(packed, 'req', axis=0, tiled=True)  90 us
    reduce_scatter x1, waiting for transfers between devices, on_device(): lax.psum_scatter(part.astype(jnp.bfloat16), 'mlp', scatter_dimension=1, t...  36.1 us
    all_to_all x1, blocking collectives, on_device(): lax.all_to_all(leaving, 'req', split_axis=0, concat_axis=0, tiled=True)  27.4 us
    psum x1, blocking collectives, on_device(): lax.psum((pick(down_query), pick(down_value), pick(down_fc)), 'mlp')  25.6 us
    all_to_all x1, waiting for transfers between devices, on_device(): lax.all_to_all(copies, 'mlp', split_axis=0, concat_axis=0, tiled=True)  22.1 us
    all_to_all x1, waiting for transfers between devices, on_device(): lax.all_to_all(outgoing, 'req', split_axis=0, concat_axis=0, tiled=True)  19.5 us
    all_to_all x1, starting transfers between devices, on_device(): lax.all_to_all(filled, 'req', split_axis=0, concat_axis=0, tiled=True)  10.6 us
    unnamed x57, local copies, waits for them, and re-layouts  9.75 us
  transfers between devices with their start and end apart: 5, of which 5 were waited for; matrix products, arithmetic and copies ran while one was open for 6% of the time, Pallas kernels for 0%

profile of v4, /device:TPU:57, one launch (start us, length us, event | category | flops | bytes accessed | tf_op | source)
XLA Modules:
  0.0 320.5 jit_solution(18361433755088756870)
XLA Ops:
  6.5 0.9 slice.56
  7.5 0.9 slice.57
  9.2 0.9 slice.59
  11.2 0.9 copy.93
  12.1 1.1 copy.94
  14.1 0.9 bitcast_dynamic-update-slice_fusion.1
  15.1 0.9 copy-done.6
  17.0 10.6 %all-to-all-start = ((bf16[32,1,2]{2,1,0:T(2,128)(2,1)}), bf16[32,1,2]{2,1,0:T(2,128)(2,1)S(1)}, u32[]{:S(2)}, u32[]{:S(2)}) async-start(bf16[32,1,2]{2,1,0:T(2,128)(2,1)} %all_to_all.20), calls=%async_computation | async-start | bytes 32768 | tf_op jit(solution)/shard_map/all_to_all | solution.py:87
  27.7 1.0 copy.112
  29.1 1.2 reshape.374
  30.3 5.1 %all-to-all-done = bf16[32,1,2]{2,1,0:T(2,128)(2,1)S(1)} async-done(((bf16[32,1,2]{2,1,0:T(2,128)(2,1)}), bf16[32,1,2]{2,1,0:T(2,128)(2,1)S(1)}, u32[]{:S(2)}, u32[]{:S(2)}) %all-to-all-start) | async-done | bytes 160 | tf_op jit(solution)/shard_map/all_to_all | solution.py:87
  35.4 4.7 %all-to-all-start.1 = ((bf16[32,2,4096]{2,1,0:T(2,128)(2,1)}), bf16[32,2,4096]{2,1,0:T(2,128)(2,1)S(1)}, u32[]{:S(2)}, u32[]{:S(2)}) async-start(bf16[32,2,4096]{2,1,0:T(2,128)(2,1)} %reshape.374), calls=%async_computation.1 | async-start | bytes 1048576 | tf_op jit(solution)/shard_map/all_to_all | solution.py:86
  40.6 19.5 %all-to-all-done.1 = bf16[32,2,4096]{2,1,0:T(2,128)(2,1)S(1)} async-done(((bf16[32,2,4096]{2,1,0:T(2,128)(2,1)}), bf16[32,2,4096]{2,1,0:T(2,128)(2,1)S(1)}, u32[]{:S(2)}, u32[]{:S(2)}) %all-to-all-start.1) | async-done | bytes 524320 | tf_op jit(solution)/shard_map/all_to_all | solution.py:86
  60.9 1.4 broadcast_in_dim.13
  62.3 7.8 %all-to-all-start.2 = ((bf16[8,256,512]{1,2,0:T(8,128)(2,1)}), bf16[8,256,512]{1,2,0:T(8,128)(2,1)}, u32[]{:S(2)}, u32[]{:S(2)}) async-start(bf16[8,256,512]{1,2,0:T(8,128)(2,1)} %broadcast_in_dim.13), calls=%async_computation.2 | async-start | bytes 4194304 | tf_op jit(solution)/shard_map/all_to_all | solution.py:102
  70.2 1.0 slice.64
  72.7 22.1 %all-to-all-done.2 = bf16[8,256,512]{1,2,0:T(8,128)(2,1)} async-done(((bf16[8,256,512]{1,2,0:T(8,128)(2,1)}), bf16[8,256,512]{1,2,0:T(8,128)(2,1)}, u32[]{:S(2)}, u32[]{:S(2)}) %all-to-all-start.2) | async-done | bytes 2097184 | tf_op jit(solution)/shard_map/all_to_all | solution.py:102
  94.8 2.1 convert_reduce_fusion
  96.9 2.3 multiply_reduce_fusion
  99.2 2.6 fusion.10
  102.5 1.4 copy-done.4
  105.5 25.6 %all-reduce = (bf16[256,16]{0,1:T(8,128)(2,1)S(1)}, bf16[256,16]{0,1:T(8,128)(2,1)S(1)}, bf16[256,16]{0,1:T(8,128)(2,1)S(1)}) all-reduce(f32[256,16]{0,1:T(8,128)S(1)} %get-tuple-element.6, f32[256,16]{0,1:T(8,128)S(1)} %get-tuple-element.7, f32[256,16]{0,1:T(8,128)S(1)} %get-tuple-element.5), channel_id=1, replica_groups=mesh['req'=32,'mlp'=8] {'mlp'}, use_global_device_ids=true, to_apply=%region_14.15 | all-reduce | flops 12288 | bytes 73728 | tf_op jit(solution)/shard_map/psum | solution.py:118
  131.0 0.9 broadcast_multiply_fusion.1
  132.0 90.0 %all-gather.2.cloned.1.call-done = bf16[4096,3072]{0,1:T(8,128)(2,1)} async-done(((bf16[128,3072]{0,1:T(8,128)(2,1)}), bf16[4096,3072]{0,1:T(8,128)(2,1)}) %all-gather.2.cloned.1.call-update) | async-done | bytes 25165840 | tf_op jit(solution)/shard_map/all_gather | solution.py:141
  222.0 8.6 %fusion = f32[256,1792]{1,0:T(8,128)S(1)} fusion(bf16[256,4096]{0,1:T(8,128)(2,1)} %copy-done.1, bf16[4096,3072]{0,1:T(8,128)(2,1)} %all-gather.2.cloned.1.call-done), kind=kOutput, calls=%fused_computation | convolution fusion | flops 3758096384 | bytes 18612224 | tf_op jit(solution)/shard_map/dot_general | solution.py:143
  233.1 2.4 fusion.15
  235.4 2.3 fusion.20
  237.7 8.2 %fusion.4 = bf16[256,4096]{1,0:T(8,128)(2,1)} fusion(bf16[4096,3072]{0,1:T(8,128)(2,1)} %all-gather.2.cloned.1.call-done, bf16[256,1024]{1,0:T(8,128)(2,1)S(1)} %fusion.20, bf16[256,256]{1,0:T(8,128)(2,1)S(1)} %copy-done.20), kind=kOutput, calls=%fused_computation.4 | convolution fusion | flops 2686713856 | bytes 13238272 | tf_op jit(solution)/shard_map/dot_general | solution.py:167
  246.0 36.1 %reduce-scatter.2.cloned.1.call-done = bf16[256,512]{1,0:T(8,128)(2,1)} async-done(((bf16[256,4096]{1,0:T(8,128)(2,1)}), bf16[256,512]{1,0:T(8,128)(2,1)}) %reduce-scatter.2.cloned.1.call-update) | async-done | bytes 262160 | tf_op jit(solution)/shard_map/reduce_scatter | solution.py:173
  282.1 1.0 add_convert_fusion
  284.0 27.4 %all_to_all.25 = bf16[32,2,4096]{2,1,0:T(2,128)(2,1)} all-to-all(bf16[32,2,4096]{2,1,0:T(2,128)(2,1)S(1)} %reshape.390), channel_id=1, replica_groups=mesh['req'=32,'mlp'=8] {'req'}, dimensions={0} | all-to-all | bytes 1048576 | tf_op jit(solution)/shard_map/all_to_all | solution.py:180
  311.4 1.2 reshape.391
  (103 shorter events, 13.4 us)
Async XLA Ops:
  6.5 228.9 %copy-start = (bf16[1024,1024]{1,0:T(8,128)(2,1)S(1)}, bf16[1024,1024]{1,0:T(8,128)(2,1)}, u32[]{:S(2)}) copy-start(bf16[1024,1024]{1,0:T(8,128)(2,1)} %param.37) | copy-start | bytes 6291460
  6.5 8.5 %copy-start.10 = (bf16[1024,128]{1,0:T(8,128)(2,1)S(1)}, bf16[1024,128]{1,0:T(8,128)(2,1)}, u32[]{:S(2)}) copy-start(bf16[1024,128]{1,0:T(8,128)(2,1)} %param.38) | copy-start | bytes 786436
  6.5 9.5 %copy-start.19 = (s32[32]{0:T(128)S(1)}, s32[32]{0:T(128)}, u32[]{:S(2)}) copy-start(s32[32]{0:T(128)} %param.21) | copy-start | bytes 388
  6.5 215.4 %all-gather.2.cloned.1.call-start = ((), (), s32[]{:S(2)}) async-start(), calls=%async_computation.5 | async-start | bytes 25952256 | tf_op jit(solution)/shard_map/all_gather | solution.py:141
  15.0 0.9 copy-start.6
  17.0 18.3 %all-to-all-start = ((bf16[32,1,2]{2,1,0:T(2,128)(2,1)}), bf16[32,1,2]{2,1,0:T(2,128)(2,1)S(1)}, u32[]{:S(2)}, u32[]{:S(2)}) async-start(bf16[32,1,2]{2,1,0:T(2,128)(2,1)} %all_to_all.20), calls=%async_computation | async-start | bytes 32768 | tf_op jit(solution)/shard_map/all_to_all | solution.py:87
  35.4 24.7 %all-to-all-start.1 = ((bf16[32,2,4096]{2,1,0:T(2,128)(2,1)}), bf16[32,2,4096]{2,1,0:T(2,128)(2,1)S(1)}, u32[]{:S(2)}, u32[]{:S(2)}) async-start(bf16[32,2,4096]{2,1,0:T(2,128)(2,1)} %reshape.374), calls=%async_computation.1 | async-start | bytes 1048576 | tf_op jit(solution)/shard_map/all_to_all | solution.py:86
  62.3 7.9 %copy-start.2 = (bf16[1024,256]{1,0:T(8,128)(2,1)S(1)}, bf16[1024,256]{1,0:T(8,128)(2,1)}, u32[]{:S(2)}) copy-start(bf16[1024,256]{1,0:T(8,128)(2,1)} %param.31) | copy-start | bytes 1572868
  62.3 8.9 %slice-start = ((bf16[1024,256]{1,0:T(8,128)(2,1)}), bf16[1024,64]{1,0:T(8,128)(2,1)S(1)}, s32[]{:S(2)}) async-start(bf16[1024,256]{1,0:T(8,128)(2,1)} %param.31), calls=%async_computation.7 | async-start | bytes 524288 | tf_op jit(solution)/shard_map/slice | solution.py:134
  62.3 32.5 %all-to-all-start.2 = ((bf16[8,256,512]{1,2,0:T(8,128)(2,1)}), bf16[8,256,512]{1,2,0:T(8,128)(2,1)}, u32[]{:S(2)}, u32[]{:S(2)}) async-start(bf16[8,256,512]{1,2,0:T(8,128)(2,1)} %broadcast_in_dim.13), calls=%async_computation.2 | async-start | bytes 4194304 | tf_op jit(solution)/shard_map/all_to_all | solution.py:102
  70.1 2.2 copy-start.15
  70.1 2.3 copy-start.17
  70.1 212.0 %reduce-scatter.2.cloned.1.call-start = ((), (), s32[]{:S(2)}) async-start(), calls=%async_computation.6 | async-start | bytes 2359296 | tf_op jit(solution)/shard_map/reduce_scatter | solution.py:173
  72.7 26.5 %copy-start.13 = (f32[4096]{0:T(1024)S(1)}, f32[4096]{0:T(1024)}, u32[]{:S(2)}) copy-start(f32[4096]{0:T(1024)} %param.25) | copy-start | bytes 49156
  72.7 26.5 %copy-start.14 = (f32[4096]{0:T(1024)S(1)}, f32[4096]{0:T(1024)}, u32[]{:S(2)}) copy-start(f32[4096]{0:T(1024)} %param.24) | copy-start | bytes 49156
  99.2 2.6 copy-start.3
  101.9 2.6 copy-start.1
  101.9 2.0 copy-start.4
  101.9 2.6 copy-start.5
  222.0 8.6 %copy-start.7 = (bf16[256,64,16]{0,2,1:T(8,128)(2,1)S(1)}, bf16[256,64,16]{0,2,1:T(8,128)(2,1)}, u32[]{:S(2)}) copy-start(bf16[256,64,16]{0,2,1:T(8,128)(2,1)} %get-tuple-element.15) | copy-start | bytes 1572868
  222.0 8.6 %copy-start.8 = (bf16[1024,192]{1,0:T(8,128)(2,1)S(1)}, bf16[1024,192]{1,0:T(8,128)(2,1)}, u32[]{:S(2)}) copy-start(bf16[1024,192]{1,0:T(8,128)(2,1)} %slice.64) | copy-start | bytes 1179652
  222.0 8.7 %copy-start.9 = (bf16[1024,64]{1,0:T(8,128)(2,1)S(1)}, bf16[1024,64]{1,0:T(8,128)(2,1)}, u32[]{:S(2)}) copy-start(bf16[1024,64]{1,0:T(8,128)(2,1)} %copy.99) | copy-start | bytes 393220
  230.6 1.7 copy-start.12
  231.9 3.5 %copy-start.18 = (f32[1024]{0:T(1024)S(1)}, f32[1024]{0:T(1024)}, u32[]{:S(2)}) copy-start(f32[1024]{0:T(1024)} %param.35) | copy-start | bytes 12292
  232.3 0.7 copy-start.11
  235.4 2.3 copy-start.20
  246.0 36.1 %copy-start.16 = (f32[512]{0:T(512)S(1)}, f32[512]{0:T(512)}, u32[]{:S(2)}) copy-start(f32[512]{0:T(512)} %param.39) | copy-start | bytes 6148
Sparse Core Ops, SparseCore 0:
  16.1 205.7 all-gather.1
  246.1 35.9 reduce-scatter.1

commit v5 on v4

--- a/solution.py
+++ b/solution.py
@@ -170,9 +170,7 @@
         (((1,), (1,)), ((), ())),
         preferred_element_type=jnp.float32,
     )
-    shares = lax.psum_scatter(
-        part.astype(jnp.bfloat16), "mlp", scatter_dimension=1, tiled=True
-    ).astype(jnp.float32)
+    shares = lax.psum_scatter(part, "mlp", scatter_dimension=1, tiled=True)
     result = (own_x.astype(jnp.float32) + shares + b_fc_out).astype(jnp.bfloat16)
     back_flat = result.reshape(pg_dev, page_len * width_m)
     leaving = jnp.dot(take.T, back_flat, preferred_element_type=jnp.float32).astype(jnp.bfloat16)

time: 322 us -> 326 us (1.012)
  waiting for transfers between devices: 173 us -> 177 us
    reduce_scatter x1, waiting for transfers between devices: 36.1 us -> 40.4 us  [on_device(): shares = lax.psum_scatter(part, 'mlp', scatter_dimension=1, tiled=True)]
where the time goes in v5:
time: 326 us; the launch traced here: 325 us
  waiting for transfers between devices  177 us (54%)
  blocking collectives  52.6 us (16%)
  matrix products  26 us (8%)
  starting transfers between devices  23.2 us (7%)
  local copies, waits for them, and re-layouts  21.3 us (7%)
  between operations  13.9 us (4%)
  other arithmetic  11.2 us (3%)
    all_gather x1, waiting for transfers between devices, on_device(): gathered = lax.all_gather(packed, 'req', axis=0, tiled=True)  90 us
    reduce_scatter x1, waiting for transfers between devices, on_device(): shares = lax.psum_scatter(part, 'mlp', scatter_dimension=1, tiled=True)  40.4 us
    all_to_all x1, blocking collectives, on_device(): lax.all_to_all(leaving, 'req', split_axis=0, concat_axis=0, tiled=True)  27 us
    psum x1, blocking collectives, on_device(): lax.psum((pick(down_query), pick(down_value), pick(down_fc)), 'mlp')  25.6 us
    all_to_all x1, waiting for transfers between devices, on_device(): lax.all_to_all(copies, 'mlp', split_axis=0, concat_axis=0, tiled=True)  22.1 us
    all_to_all x1, waiting for transfers between devices, on_device(): lax.all_to_all(outgoing, 'req', split_axis=0, concat_axis=0, tiled=True)  19.5 us
    all_to_all x1, starting transfers between devices, on_device(): lax.all_to_all(filled, 'req', split_axis=0, concat_axis=0, tiled=True)  10.6 us
    unnamed x57, local copies, waits for them, and re-layouts  9.75 us
  transfers between devices with their start and end apart: 5, of which 5 were waited for; matrix products, arithmetic and copies ran while one was open for 6% of the time, Pallas kernels for 0%

profile of v5, /device:TPU:57, one launch (start us, length us, event | category | flops | bytes accessed | tf_op | source)
XLA Modules:
  0.0 325.1 jit_solution(16954433604053925797)
XLA Ops:
  6.5 0.9 slice.56
  7.5 0.9 slice.57
  9.2 0.9 slice.59
  11.2 0.9 copy.93
  12.1 1.1 copy.94
  14.1 0.9 bitcast_dynamic-update-slice_fusion.1
  15.1 0.9 copy-done.6
  17.0 10.6 %all-to-all-start = ((bf16[32,1,2]{2,1,0:T(2,128)(2,1)}), bf16[32,1,2]{2,1,0:T(2,128)(2,1)S(1)}, u32[]{:S(2)}, u32[]{:S(2)}) async-start(bf16[32,1,2]{2,1,0:T(2,128)(2,1)} %all_to_all.20), calls=%async_computation | async-start | bytes 32768 | tf_op jit(solution)/shard_map/all_to_all | solution.py:87
  27.7 1.0 copy.112
  29.1 1.2 reshape.374
  30.3 5.1 %all-to-all-done = bf16[32,1,2]{2,1,0:T(2,128)(2,1)S(1)} async-done(((bf16[32,1,2]{2,1,0:T(2,128)(2,1)}), bf16[32,1,2]{2,1,0:T(2,128)(2,1)S(1)}, u32[]{:S(2)}, u32[]{:S(2)}) %all-to-all-start) | async-done | bytes 160 | tf_op jit(solution)/shard_map/all_to_all | solution.py:87
  35.4 4.7 %all-to-all-start.1 = ((bf16[32,2,4096]{2,1,0:T(2,128)(2,1)}), bf16[32,2,4096]{2,1,0:T(2,128)(2,1)S(1)}, u32[]{:S(2)}, u32[]{:S(2)}) async-start(bf16[32,2,4096]{2,1,0:T(2,128)(2,1)} %reshape.374), calls=%async_computation.1 | async-start | bytes 1048576 | tf_op jit(solution)/shard_map/all_to_all | solution.py:86
  40.6 19.5 %all-to-all-done.1 = bf16[32,2,4096]{2,1,0:T(2,128)(2,1)S(1)} async-done(((bf16[32,2,4096]{2,1,0:T(2,128)(2,1)}), bf16[32,2,4096]{2,1,0:T(2,128)(2,1)S(1)}, u32[]{:S(2)}, u32[]{:S(2)}) %all-to-all-start.1) | async-done | bytes 524320 | tf_op jit(solution)/shard_map/all_to_all | solution.py:86
  60.9 1.4 broadcast_in_dim.13
  62.3 7.8 %all-to-all-start.2 = ((bf16[8,256,512]{1,2,0:T(8,128)(2,1)}), bf16[8,256,512]{1,2,0:T(8,128)(2,1)}, u32[]{:S(2)}, u32[]{:S(2)}) async-start(bf16[8,256,512]{1,2,0:T(8,128)(2,1)} %broadcast_in_dim.13), calls=%async_computation.2 | async-start | bytes 4194304 | tf_op jit(solution)/shard_map/all_to_all | solution.py:102
  70.2 1.0 slice.64
  72.7 22.1 %all-to-all-done.2 = bf16[8,256,512]{1,2,0:T(8,128)(2,1)} async-done(((bf16[8,256,512]{1,2,0:T(8,128)(2,1)}), bf16[8,256,512]{1,2,0:T(8,128)(2,1)}, u32[]{:S(2)}, u32[]{:S(2)}) %all-to-all-start.2) | async-done | bytes 2097184 | tf_op jit(solution)/shard_map/all_to_all | solution.py:102
  94.8 2.1 convert_reduce_fusion
  96.9 2.3 multiply_reduce_fusion
  99.2 2.6 fusion.7
  102.5 1.4 copy-done.4
  105.5 25.6 %all-reduce = (bf16[256,16]{0,1:T(8,128)(2,1)S(1)}, bf16[256,16]{0,1:T(8,128)(2,1)S(1)}, bf16[256,16]{0,1:T(8,128)(2,1)S(1)}) all-reduce(f32[256,16]{0,1:T(8,128)S(1)} %get-tuple-element.6, f32[256,16]{0,1:T(8,128)S(1)} %get-tuple-element.7, f32[256,16]{0,1:T(8,128)S(1)} %get-tuple-element.5), channel_id=1, replica_groups=mesh['req'=32,'mlp'=8] {'mlp'}, use_global_device_ids=true, to_apply=%region_14.15 | all-reduce | flops 12288 | bytes 73728 | tf_op jit(solution)/shard_map/psum | solution.py:118
  131.0 0.9 broadcast_multiply_fusion.1
  132.0 90.0 %all-gather.2.cloned.1.call-done = bf16[4096,3072]{0,1:T(8,128)(2,1)} async-done(((bf16[128,3072]{0,1:T(8,128)(2,1)}), bf16[4096,3072]{0,1:T(8,128)(2,1)}) %all-gather.2.cloned.1.call-update) | async-done | bytes 25165840 | tf_op jit(solution)/shard_map/all_gather | solution.py:141
  222.0 8.6 %fusion = f32[256,1792]{1,0:T(8,128)S(1)} fusion(bf16[256,4096]{0,1:T(8,128)(2,1)} %copy-done.1, bf16[4096,3072]{0,1:T(8,128)(2,1)} %all-gather.2.cloned.1.call-done), kind=kOutput, calls=%fused_computation | convolution fusion | flops 3758096384 | bytes 18612224 | tf_op jit(solution)/shard_map/dot_general | solution.py:143
  233.1 2.4 fusion.12
  235.4 2.3 fusion.17
  237.7 8.8 %fusion.2 = f32[256,4096]{1,0:T(8,128)} fusion(bf16[4096,3072]{0,1:T(8,128)(2,1)} %all-gather.2.cloned.1.call-done, bf16[256,1024]{1,0:T(8,128)(2,1)S(1)} %fusion.17, bf16[256,256]{1,0:T(8,128)(2,1)S(1)} %copy-done.20), kind=kOutput, calls=%fused_computation.2 | convolution fusion | flops 2685665280 | bytes 15335424 | tf_op jit(solution)/shard_map/dot_general | solution.py:167
  246.6 40.4 %reduce-scatter.2.cloned.1.call-done = f32[256,512]{1,0:T(8,128)} async-done(((f32[256,4096]{1,0:T(8,128)}), f32[256,512]{1,0:T(8,128)}) %reduce-scatter.2.cloned.1.call-update) | async-done | bytes 524304 | tf_op jit(solution)/shard_map/reduce_scatter | solution.py:173
  287.0 1.1 add_convert_fusion
  289.0 27.0 %all_to_all.25 = bf16[32,2,4096]{2,1,0:T(2,128)(2,1)} all-to-all(bf16[32,2,4096]{2,1,0:T(2,128)(2,1)S(1)} %reshape.390), channel_id=1, replica_groups=mesh['req'=32,'mlp'=8] {'req'}, dimensions={0} | all-to-all | bytes 1048576 | tf_op jit(solution)/shard_map/all_to_all | solution.py:178
  315.9 1.2 reshape.391
  (103 shorter events, 13.4 us)
Async XLA Ops:
  6.5 228.9 %copy-start = (bf16[1024,1024]{1,0:T(8,128)(2,1)S(1)}, bf16[1024,1024]{1,0:T(8,128)(2,1)}, u32[]{:S(2)}) copy-start(bf16[1024,1024]{1,0:T(8,128)(2,1)} %param.37) | copy-start | bytes 6291460
  6.5 8.5 %copy-start.10 = (bf16[1024,128]{1,0:T(8,128)(2,1)S(1)}, bf16[1024,128]{1,0:T(8,128)(2,1)}, u32[]{:S(2)}) copy-start(bf16[1024,128]{1,0:T(8,128)(2,1)} %param.38) | copy-start | bytes 786436
  6.5 9.5 %copy-start.19 = (s32[32]{0:T(128)S(1)}, s32[32]{0:T(128)}, u32[]{:S(2)}) copy-start(s32[32]{0:T(128)} %param.21) | copy-start | bytes 388
  6.5 215.4 %all-gather.2.cloned.1.call-start = ((), (), s32[]{:S(2)}) async-start(), calls=%async_computation.5 | async-start | bytes 25952256 | tf_op jit(solution)/shard_map/all_gather | solution.py:141
  15.0 0.9 copy-start.6
  17.0 18.3 %all-to-all-start = ((bf16[32,1,2]{2,1,0:T(2,128)(2,1)}), bf16[32,1,2]{2,1,0:T(2,128)(2,1)S(1)}, u32[]{:S(2)}, u32[]{:S(2)}) async-start(bf16[32,1,2]{2,1,0:T(2,128)(2,1)} %all_to_all.20), calls=%async_computation | async-start | bytes 32768 | tf_op jit(solution)/shard_map/all_to_all | solution.py:87
  35.4 24.7 %all-to-all-start.1 = ((bf16[32,2,4096]{2,1,0:T(2,128)(2,1)}), bf16[32,2,4096]{2,1,0:T(2,128)(2,1)S(1)}, u32[]{:S(2)}, u32[]{:S(2)}) async-start(bf16[32,2,4096]{2,1,0:T(2,128)(2,1)} %reshape.374), calls=%async_computation.1 | async-start | bytes 1048576 | tf_op jit(solution)/shard_map/all_to_all | solution.py:86
  62.3 7.9 %copy-start.2 = (bf16[1024,256]{1,0:T(8,128)(2,1)S(1)}, bf16[1024,256]{1,0:T(8,128)(2,1)}, u32[]{:S(2)}) copy-start(bf16[1024,256]{1,0:T(8,128)(2,1)} %param.31) | copy-start | bytes 1572868
  62.3 8.9 %slice-start = ((bf16[1024,256]{1,0:T(8,128)(2,1)}), bf16[1024,64]{1,0:T(8,128)(2,1)S(1)}, s32[]{:S(2)}) async-start(bf16[1024,256]{1,0:T(8,128)(2,1)} %param.31), calls=%async_computation.7 | async-start | bytes 524288 | tf_op jit(solution)/shard_map/slice | solution.py:134
  62.3 32.5 %all-to-all-start.2 = ((bf16[8,256,512]{1,2,0:T(8,128)(2,1)}), bf16[8,256,512]{1,2,0:T(8,128)(2,1)}, u32[]{:S(2)}, u32[]{:S(2)}) async-start(bf16[8,256,512]{1,2,0:T(8,128)(2,1)} %broadcast_in_dim.13), calls=%async_computation.2 | async-start | bytes 4194304 | tf_op jit(solution)/shard_map/all_to_all | solution.py:102
  70.1 2.2 copy-start.15
  70.1 2.3 copy-start.17
  70.1 216.8 %reduce-scatter.2.cloned.1.call-start = ((), (), s32[]{:S(2)}) async-start(), calls=%async_computation.6 | async-start | bytes 4718592 | tf_op jit(solution)/shard_map/reduce_scatter | solution.py:173
  72.7 26.5 %copy-start.13 = (f32[4096]{0:T(1024)S(1)}, f32[4096]{0:T(1024)}, u32[]{:S(2)}) copy-start(f32[4096]{0:T(1024)} %param.25) | copy-start | bytes 49156
  72.7 26.5 %copy-start.14 = (f32[4096]{0:T(1024)S(1)}, f32[4096]{0:T(1024)}, u32[]{:S(2)}) copy-start(f32[4096]{0:T(1024)} %param.24) | copy-start | bytes 49156
  99.2 2.6 copy-start.3
  101.9 2.6 copy-start.1
  101.9 2.0 copy-start.4
  101.9 2.6 copy-start.5
  222.0 8.6 %copy-start.7 = (bf16[256,64,16]{0,2,1:T(8,128)(2,1)S(1)}, bf16[256,64,16]{0,2,1:T(8,128)(2,1)}, u32[]{:S(2)}) copy-start(bf16[256,64,16]{0,2,1:T(8,128)(2,1)} %get-tuple-element.15) | copy-start | bytes 1572868
  222.0 8.6 %copy-start.8 = (bf16[1024,192]{1,0:T(8,128)(2,1)S(1)}, bf16[1024,192]{1,0:T(8,128)(2,1)}, u32[]{:S(2)}) copy-start(bf16[1024,192]{1,0:T(8,128)(2,1)} %slice.64) | copy-start | bytes 1179652
  222.0 8.7 %copy-start.9 = (bf16[1024,64]{1,0:T(8,128)(2,1)S(1)}, bf16[1024,64]{1,0:T(8,128)(2,1)}, u32[]{:S(2)}) copy-start(bf16[1024,64]{1,0:T(8,128)(2,1)} %copy.99) | copy-start | bytes 393220
  230.6 1.7 copy-start.12
  231.9 3.5 %copy-start.18 = (f32[1024]{0:T(1024)S(1)}, f32[1024]{0:T(1024)}, u32[]{:S(2)}) copy-start(f32[1024]{0:T(1024)} %param.35) | copy-start | bytes 12292
  232.3 0.7 copy-start.11
  235.4 2.3 copy-start.20
  246.6 40.4 %copy-start.16 = (f32[512]{0:T(512)S(1)}, f32[512]{0:T(512)}, u32[]{:S(2)}) copy-start(f32[512]{0:T(512)} %param.39) | copy-start | bytes 6148
Sparse Core Ops, SparseCore 0:
  16.1 205.7 all-gather.1
  246.7 40.2 reduce-scatter.1

commit v6 on v5

--- a/solution.py
+++ b/solution.py
@@ -1,6 +1,8 @@
 import jax
 import jax.numpy as jnp
 from jax import lax
+from jax.experimental import pallas as pl
+from jax.experimental.pallas import tpu as pltpu
 from jax.sharding import PartitionSpec as P
 
 HS = 256
@@ -40,6 +42,58 @@
     return jnp.concatenate(
         [even * cosine - odd * sine, odd * cosine + even * sine, block[:, :, ROT:]], axis=2
     )
+
+
+def pack_kernel(wq_ref, wk_ref, wv_ref, wfi_ref, wao_ref, wfo_ref, out_ref):
+    hw = wq_ref.shape[1]
+    ff = wfi_ref.shape[1]
+    rows = wq_ref.shape[0]
+    src = lax.broadcasted_iota(jnp.int32, (hw, hw), 0)
+    dst = lax.broadcasted_iota(jnp.int32, (hw, hw), 1)
+    half = ROT // 2
+    origin = jnp.where(
+        dst < half, 2 * dst, jnp.where(dst < ROT, 2 * (dst - half) + 1, dst)
+    )
+    perm = (src == origin).astype(jnp.bfloat16)
+    ident = (
+        lax.broadcasted_iota(jnp.int32, (rows, rows), 0)
+        == lax.broadcasted_iota(jnp.int32, (rows, rows), 1)
+    ).astype(jnp.bfloat16)
+    nt = (((1,), (1,)), ((), ()))
+    out_ref[:, 0:hw] = jnp.dot(
+        wq_ref[...], perm, preferred_element_type=jnp.float32
+    ).astype(out_ref.dtype)
+    out_ref[:, hw : 2 * hw] = jnp.dot(
+        wk_ref[...], perm, preferred_element_type=jnp.float32
+    ).astype(out_ref.dtype)
+    out_ref[:, 2 * hw : 3 * hw] = wv_ref[...]
+    out_ref[:, 3 * hw : 3 * hw + ff] = wfi_ref[...]
+    base = 3 * hw + ff
+    n_ao = wao_ref.shape[0]
+    out_ref[:, base : base + n_ao] = lax.dot_general(
+        ident, wao_ref[...], nt, preferred_element_type=jnp.float32
+    ).astype(out_ref.dtype)
+    n_fo = wfo_ref.shape[0]
+    out_ref[:, base + n_ao : base + n_ao + n_fo] = lax.dot_general(
+        ident, wfo_ref[...], nt, preferred_element_type=jnp.float32
+    ).astype(out_ref.dtype)
+
+
+def pack_weights(wq, wk, wv, wfi, wao, wfo):
+    rows = wq.shape[0]
+    cols = 3 * wq.shape[1] + wfi.shape[1] + wao.shape[0] + wfo.shape[0]
+    vmem = pl.BlockSpec(memory_space=pltpu.VMEM)
+    return pl.pallas_call(
+        pack_kernel,
+        out_shape=jax.ShapeDtypeStruct((rows, cols), wq.dtype),
+        in_specs=[vmem] * 6,
+        out_specs=vmem,
+        cost_estimate=pl.CostEstimate(
+            flops=2 * rows * (2 * wq.shape[1] ** 2 + rows * (wao.shape[0] + wfo.shape[0])),
+            bytes_accessed=4 * rows * cols,
+            transcendentals=0,
+        ),
+    )(wq, wk, wv, wfi, wao, wfo)
 
 
 def on_device(
@@ -134,10 +188,7 @@
         lead = w[:, :ROT].reshape(rows, ROT // 2, 2).transpose(0, 2, 1).reshape(rows, ROT)
         return jnp.concatenate([lead, w[:, ROT:]], axis=1)
 
-    packed = jnp.concatenate(
-        [pair_major(w_query), pair_major(w_key), w_value, w_fc_in, w_attn_out.T, w_fc_out.T],
-        axis=1,
-    )
+    packed = pack_weights(w_query, w_key, w_value, w_fc_in, w_attn_out, w_fc_out)
     gathered = lax.all_gather(packed, "req", axis=0, tiled=True)
     n_in = 3 * heads_w + ff_w
     base = jnp.dot(full_ln, gathered[:, :n_in], preferred_element_type=jnp.float32)

time: 326 us -> 307 us (0.942)
  waiting for transfers between devices: 177 us -> 166 us
  local copies, waits for them, and re-layouts: 21.3 us -> 11 us
    all_gather x1, waiting for transfers between devices: 90 us -> 77.5 us  [on_device(): gathered = lax.all_gather(packed, 'req', axis=0, tiled=True)]
    unnamed x57 -> x42, local copies, waits for them, and re-layouts: 9.75 us -> 3.05 us
where the time goes in v6:
time: 307 us; the launch traced here: 306 us
  waiting for transfers between devices  166 us (54%)
  blocking collectives  52.5 us (17%)
  matrix products  26 us (8%)
  starting transfers between devices  22.9 us (7%)
  between operations  13.8 us (4%)
  other arithmetic  11.1 us (4%)
  local copies, waits for them, and re-layouts  11 us (4%)
    all_gather x1, waiting for transfers between devices, on_device(): gathered = lax.all_gather(packed, 'req', axis=0, tiled=True)  77.5 us
    reduce_scatter x1, waiting for transfers between devices, on_device(): shares = lax.psum_scatter(part, 'mlp', scatter_dimension=1, tiled=True)  38.7 us
    all_to_all x1, blocking collectives, on_device(): lax.all_to_all(leaving, 'req', split_axis=0, concat_axis=0, tiled=True)  27 us
    psum x1, blocking collectives, on_device(): lax.psum((pick(down_query), pick(down_value), pick(down_fc)), 'mlp')  25.6 us
    all_to_all x1, waiting for transfers between devices, on_device(): lax.all_to_all(copies, 'mlp', split_axis=0, concat_axis=0, tiled=True)  22.1 us
    all_to_all x1, waiting for transfers between devices, on_device(): lax.all_to_all(outgoing, 'req', split_axis=0, concat_axis=0, tiled=True)  21.8 us
    all_to_all x1, starting transfers between devices, on_device(): lax.all_to_all(filled, 'req', split_axis=0, concat_axis=0, tiled=True)  10.6 us
    dot_general x1, matrix products, on_device(): lax.dot_general(joined, gathered[:, n_in:], (((1,), (1,)), ((), ())), pre...  8.86 us
  transfers between devices with their start and end apart: 5, of which 5 were waited for; matrix products, arithmetic and copies ran while one was open for 6% of the time, Pallas kernels for 0%

profile of v6, /device:TPU:57, one launch (start us, length us, event | category | flops | bytes accessed | tf_op | source)
XLA Modules:
  0.0 306.0 jit_solution(2403813709763201292)
XLA Ops:
  6.5 2.5 shard_map.190
  9.4 0.7 all_to_all.20
  10.1 10.6 %all-to-all-start = ((bf16[32,1,2]{2,1,0:T(2,128)(2,1)}), bf16[32,1,2]{2,1,0:T(2,128)(2,1)S(1)}, u32[]{:S(2)}, u32[]{:S(2)}) async-start(bf16[32,1,2]{2,1,0:T(2,128)(2,1)} %all_to_all.20), calls=%async_computation | async-start | bytes 32768 | tf_op jit(solution)/shard_map/all_to_all | solution.py:141
  21.3 1.2 reshape.362
  22.5 6.0 %all-to-all-done = bf16[32,1,2]{2,1,0:T(2,128)(2,1)S(1)} async-done(((bf16[32,1,2]{2,1,0:T(2,128)(2,1)}), bf16[32,1,2]{2,1,0:T(2,128)(2,1)S(1)}, u32[]{:S(2)}, u32[]{:S(2)}) %all-to-all-start) | async-done | bytes 160 | tf_op jit(solution)/shard_map/all_to_all | solution.py:141
  28.5 4.7 %all-to-all-start.1 = ((bf16[32,2,4096]{2,1,0:T(2,128)(2,1)}), bf16[32,2,4096]{2,1,0:T(2,128)(2,1)S(1)}, u32[]{:S(2)}, u32[]{:S(2)}) async-start(bf16[32,2,4096]{2,1,0:T(2,128)(2,1)} %reshape.362), calls=%async_computation.1 | async-start | bytes 1048576 | tf_op jit(solution)/shard_map/all_to_all | solution.py:140
  33.7 21.8 %all-to-all-done.1 = bf16[32,2,4096]{2,1,0:T(2,128)(2,1)S(1)} async-done(((bf16[32,2,4096]{2,1,0:T(2,128)(2,1)}), bf16[32,2,4096]{2,1,0:T(2,128)(2,1)S(1)}, u32[]{:S(2)}, u32[]{:S(2)}) %all-to-all-start.1) | async-done | bytes 524320 | tf_op jit(solution)/shard_map/all_to_all | solution.py:140
  56.3 1.4 broadcast_in_dim.13
  57.7 7.5 %all-to-all-start.2 = ((bf16[8,256,512]{1,2,0:T(8,128)(2,1)}), bf16[8,256,512]{1,2,0:T(8,128)(2,1)}, u32[]{:S(2)}, u32[]{:S(2)}) async-start(bf16[8,256,512]{1,2,0:T(8,128)(2,1)} %broadcast_in_dim.13), calls=%async_computation.2 | async-start | bytes 4194304 | tf_op jit(solution)/shard_map/all_to_all | solution.py:156
  65.3 1.0 slice.48
  66.5 0.8 copy.53
  67.8 22.1 %all-to-all-done.2 = bf16[8,256,512]{1,2,0:T(8,128)(2,1)} async-done(((bf16[8,256,512]{1,2,0:T(8,128)(2,1)}), bf16[8,256,512]{1,2,0:T(8,128)(2,1)}, u32[]{:S(2)}, u32[]{:S(2)}) %all-to-all-start.2) | async-done | bytes 2097184 | tf_op jit(solution)/shard_map/all_to_all | solution.py:156
  89.8 2.1 convert_reduce_fusion
  92.0 2.2 multiply_reduce_fusion
  94.2 2.6 fusion.7
  96.9 0.6 fusion.27
  97.5 1.4 copy-done.4
  99.4 0.6 fusion.29
  100.4 25.6 %all-reduce = (bf16[256,16]{0,1:T(8,128)(2,1)S(1)}, bf16[256,16]{0,1:T(8,128)(2,1)S(1)}, bf16[256,16]{0,1:T(8,128)(2,1)S(1)}) all-reduce(f32[256,16]{0,1:T(8,128)S(1)} %get-tuple-element.6, f32[256,16]{0,1:T(8,128)S(1)} %get-tuple-element.7, f32[256,16]{0,1:T(8,128)S(1)} %get-tuple-element.5), channel_id=1, replica_groups=mesh['req'=32,'mlp'=8] {'mlp'}, use_global_device_ids=true, to_apply=%region_14.15 | all-reduce | flops 12288 | bytes 73728 | tf_op jit(solution)/shard_map/psum | solution.py:172
  126.0 0.9 broadcast_multiply_fusion.1
  126.9 77.5 %all-gather.2.cloned.1.call-done = bf16[4096,3072]{1,0:T(8,128)(2,1)} async-done(((bf16[128,3072]{1,0:T(8,128)(2,1)}), bf16[4096,3072]{1,0:T(8,128)(2,1)}) %all-gather.2.cloned.1.call-update) | async-done | bytes 25165840 | tf_op jit(solution)/shard_map/all_gather | solution.py:192
  204.5 8.7 %fusion = f32[256,1792]{1,0:T(8,128)S(1)} fusion(bf16[256,4096]{0,1:T(8,128)(2,1)} %copy-done.1, bf16[4096,3072]{1,0:T(8,128)(2,1)} %all-gather.2.cloned.1.call-done), kind=kOutput, calls=%fused_computation | convolution fusion | flops 3758096384 | bytes 18612224 | tf_op jit(solution)/shard_map/dot_general | solution.py:194
  213.9 0.6 fusion.64
  214.9 0.7 copy-done.10
  215.7 2.4 fusion.12
  218.0 2.3 fusion.17
  220.3 8.9 %fusion.2 = f32[256,4096]{1,0:T(8,128)} fusion(bf16[4096,3072]{1,0:T(8,128)(2,1)} %all-gather.2.cloned.1.call-done, bf16[256,1024]{1,0:T(8,128)(2,1)S(1)} %fusion.17, bf16[256,256]{1,0:T(8,128)(2,1)S(1)} %copy-done.19), kind=kOutput, calls=%fused_computation.2 | convolution fusion | flops 2685665280 | bytes 15335424 | tf_op jit(solution)/shard_map/dot_general | solution.py:218
  229.2 38.7 %reduce-scatter.2.cloned.1.call-done = f32[256,512]{1,0:T(8,128)} async-done(((f32[256,4096]{1,0:T(8,128)}), f32[256,512]{1,0:T(8,128)}) %reduce-scatter.2.cloned.1.call-update) | async-done | bytes 524304 | tf_op jit(solution)/shard_map/reduce_scatter | solution.py:224
  267.9 1.1 add_convert_fusion
  269.9 27.0 %all_to_all.25 = bf16[32,2,4096]{2,1,0:T(2,128)(2,1)} all-to-all(bf16[32,2,4096]{2,1,0:T(2,128)(2,1)S(1)} %reshape.374), channel_id=1, replica_groups=mesh['req'=32,'mlp'=8] {'req'}, dimensions={0} | all-to-all | bytes 1048576 | tf_op jit(solution)/shard_map/all_to_all | solution.py:229
  296.9 1.2 reshape.375
  298.4 0.8 copy.63
  (82 shorter events, 6.0 us)
Async XLA Ops:
  6.5 211.5 %copy-start = (bf16[1024,1024]{1,0:T(8,128)(2,1)S(1)}, bf16[1024,1024]{1,0:T(8,128)(2,1)}, u32[]{:S(2)}) copy-start(bf16[1024,1024]{1,0:T(8,128)(2,1)} %param.37) | copy-start | bytes 6291460
  6.5 2.6 copy-start.18
  6.5 14.2 %copy-start.9 = (bf16[32,8,512]{2,1,0:T(8,128)(2,1)S(1)}, bf16[32,8,512]{2,1,0:T(8,128)(2,1)}, u32[]{:S(2)}) copy-start(bf16[32,8,512]{2,1,0:T(8,128)(2,1)} %param.20) | copy-start | bytes 786436
  6.5 197.9 %all-gather.2.cloned.1.call-start = ((), (), s32[]{:S(2)}) async-start(), calls=%async_computation.5 | async-start | bytes 25952256 | tf_op jit(solution)/shard_map/all_gather | solution.py:192
  10.1 18.3 %all-to-all-start = ((bf16[32,1,2]{2,1,0:T(2,128)(2,1)}), bf16[32,1,2]{2,1,0:T(2,128)(2,1)S(1)}, u32[]{:S(2)}, u32[]{:S(2)}) async-start(bf16[32,1,2]{2,1,0:T(2,128)(2,1)} %all_to_all.20), calls=%async_computation | async-start | bytes 32768 | tf_op jit(solution)/shard_map/all_to_all | solution.py:141
  28.5 27.1 %all-to-all-start.1 = ((bf16[32,2,4096]{2,1,0:T(2,128)(2,1)}), bf16[32,2,4096]{2,1,0:T(2,128)(2,1)S(1)}, u32[]{:S(2)}, u32[]{:S(2)}) async-start(bf16[32,2,4096]{2,1,0:T(2,128)(2,1)} %reshape.362), calls=%async_computation.1 | async-start | bytes 1048576 | tf_op jit(solution)/shard_map/all_to_all | solution.py:140
  57.7 7.6 %copy-start.2 = (bf16[1024,256]{1,0:T(8,128)(2,1)S(1)}, bf16[1024,256]{1,0:T(8,128)(2,1)}, u32[]{:S(2)}) copy-start(bf16[1024,256]{1,0:T(8,128)(2,1)} %param.31) | copy-start | bytes 1572868
  57.7 8.6 %slice-start = ((bf16[1024,256]{1,0:T(8,128)(2,1)}), bf16[1024,64]{1,0:T(8,128)(2,1)S(1)}, s32[]{:S(2)}) async-start(bf16[1024,256]{1,0:T(8,128)(2,1)} %param.31), calls=%async_computation.7 | async-start | bytes 524288 | tf_op jit(solution)/shard_map/slice | solution.py:188
  57.7 32.1 %all-to-all-start.2 = ((bf16[8,256,512]{1,2,0:T(8,128)(2,1)}), bf16[8,256,512]{1,2,0:T(8,128)(2,1)}, u32[]{:S(2)}, u32[]{:S(2)}) async-start(bf16[8,256,512]{1,2,0:T(8,128)(2,1)} %broadcast_in_dim.13), calls=%async_computation.2 | async-start | bytes 4194304 | tf_op jit(solution)/shard_map/all_to_all | solution.py:156
  65.2 2.2 copy-start.14
  65.2 2.3 copy-start.16
  65.2 202.7 %reduce-scatter.2.cloned.1.call-start = ((), (), s32[]{:S(2)}) async-start(), calls=%async_computation.6 | async-start | bytes 4718592 | tf_op jit(solution)/shard_map/reduce_scatter | solution.py:224
  67.8 26.4 %copy-start.12 = (f32[4096]{0:T(1024)S(1)}, f32[4096]{0:T(1024)}, u32[]{:S(2)}) copy-start(f32[4096]{0:T(1024)} %param.25) | copy-start | bytes 49156
  67.8 26.4 %copy-start.13 = (f32[4096]{0:T(1024)S(1)}, f32[4096]{0:T(1024)}, u32[]{:S(2)}) copy-start(f32[4096]{0:T(1024)} %param.24) | copy-start | bytes 49156
  94.2 2.6 copy-start.3
  96.9 2.6 copy-start.1
  96.9 2.0 copy-start.4
  96.9 2.5 copy-start.5
  204.5 8.7 %copy-start.6 = (bf16[256,64,16]{0,2,1:T(8,128)(2,1)S(1)}, bf16[256,64,16]{0,2,1:T(8,128)(2,1)}, u32[]{:S(2)}) copy-start(bf16[256,64,16]{0,2,1:T(8,128)(2,1)} %get-tuple-element.15) | copy-start | bytes 1572868
  204.5 8.7 %copy-start.7 = (bf16[1024,192]{1,0:T(8,128)(2,1)S(1)}, bf16[1024,192]{1,0:T(8,128)(2,1)}, u32[]{:S(2)}) copy-start(bf16[1024,192]{1,0:T(8,128)(2,1)} %slice.48) | copy-start | bytes 1179652
  204.5 8.7 %copy-start.8 = (bf16[1024,64]{1,0:T(8,128)(2,1)S(1)}, bf16[1024,64]{1,0:T(8,128)(2,1)}, u32[]{:S(2)}) copy-start(bf16[1024,64]{1,0:T(8,128)(2,1)} %copy.53) | copy-start | bytes 393220
  213.2 1.7 copy-start.11
  214.5 3.5 %copy-start.17 = (f32[1024]{0:T(1024)S(1)}, f32[1024]{0:T(1024)}, u32[]{:S(2)}) copy-start(f32[1024]{0:T(1024)} %param.35) | copy-start | bytes 12292
  214.9 0.7 copy-start.10
  218.0 2.3 copy-start.19
  229.2 38.7 %copy-start.15 = (f32[512]{0:T(512)S(1)}, f32[512]{0:T(512)}, u32[]{:S(2)}) copy-start(f32[512]{0:T(512)} %param.39) | copy-start | bytes 6148
Sparse Core Ops, SparseCore 0:
  9.9 194.5 all-gather.1
  229.3 38.5 reduce-scatter.1

commit v7 on v6

--- a/solution.py
+++ b/solution.py
@@ -221,7 +221,19 @@
         (((1,), (1,)), ((), ())),
         preferred_element_type=jnp.float32,
     )
-    shares = lax.psum_scatter(part, "mlp", scatter_dimension=1, tiled=True)
+    n_c = 2
+    n_y = lax.axis_size("mlp") // n_c
+    grid = part.reshape(tok, n_y, n_c, width_m)
+    first = lax.axis_index("mlp") % n_c == 0
+    keep = jnp.where(first, grid[:, :, 0, :], grid[:, :, 1, :])
+    send = jnp.where(first, grid[:, :, 1, :], grid[:, :, 0, :])
+    mates = [(i, i ^ 1) for i in range(n_y * n_c)]
+    got = lax.ppermute(send, "mlp", mates)
+    lanes = [[y * n_c + c for y in range(n_y)] for c in range(n_c)]
+    shares = lax.psum_scatter(
+        keep + got, "mlp", scatter_dimension=1, tiled=True, axis_index_groups=lanes
+    )
+    shares = shares.reshape(tok, width_m)
     result = (own_x.astype(jnp.float32) + shares + b_fc_out).astype(jnp.bfloat16)
     back_flat = result.reshape(pg_dev, page_len * width_m)
     leaving = jnp.dot(take.T, back_flat, preferred_element_type=jnp.float32).astype(jnp.bfloat16)

time: 307 us -> 322 us (1.049); the launches traced: 306 us -> 317 us
  local copies, waits for them, and re-layouts: 11 us -> 26 us
  waiting for transfers between devices: 166 us -> 160 us
    reduce_scatter x1, waiting for transfers between devices: 38.7 us -> 28.4 us  [on_device(): lax.psum_scatter(keep + got, 'mlp', scatter_dimension=1, tiled=True, axis...]
    slice x0 -> x1, local copies, waits for them, and re-layouts: none -> 7.77 us  [on_device(): keep = jnp.where(first, grid[:, :, 0, :], grid[:, :, 1, :])]
    reshape x3 -> x2, local copies, waits for them, and re-layouts: 0.38 us -> 7.72 us  [the longest x1 6.58 us: on_device(): grid = part.reshape(tok, n_y, n_c, width_m)]
    ppermute x0 -> x1, waiting for transfers between devices: none -> 3.79 us  [on_device(): got = lax.ppermute(send, 'mlp', mates)]
  transfers between devices with their start and end apart: 5 -> 6, of which waited for: 5 -> 6; matrix products, arithmetic and copies ran while one was open for 6% -> 5% of each run, Pallas kernels for 0% -> 0%
where the time goes in v7:
time: 322 us; the launch traced here: 317 us
  waiting for transfers between devices  160 us (50%)
  blocking collectives  50.9 us (16%)
  matrix products  26.1 us (8%)
  local copies, waits for them, and re-layouts  26 us (8%)
  starting transfers between devices  24.3 us (8%)
  other arithmetic  13.8 us (4%)
  between operations  13.8 us (4%)
    all_gather x1, waiting for transfers between devices, on_device(): gathered = lax.all_gather(packed, 'req', axis=0, tiled=True)  77.5 us
    reduce_scatter x1, waiting for transfers between devices, on_device(): lax.psum_scatter(keep + got, 'mlp', scatter_dimension=1, tiled=True, axis...  28.4 us
    psum x1, blocking collectives, on_device(): lax.psum((pick(down_query), pick(down_value), pick(down_fc)), 'mlp')  25.6 us
    all_to_all x1, blocking collectives, on_device(): lax.all_to_all(leaving, 'req', split_axis=0, concat_axis=0, tiled=True)  25.3 us
    all_to_all x1, waiting for transfers between devices, on_device(): lax.all_to_all(copies, 'mlp', split_axis=0, concat_axis=0, tiled=True)  22.1 us
    all_to_all x1, waiting for transfers between devices, on_device(): lax.all_to_all(outgoing, 'req', split_axis=0, concat_axis=0, tiled=True)  21.8 us
    all_to_all x1, starting transfers between devices, on_device(): lax.all_to_all(filled, 'req', split_axis=0, concat_axis=0, tiled=True)  10.6 us
    dot_general x1, matrix products, on_device(): lax.dot_general(joined, gathered[:, n_in:], (((1,), (1,)), ((), ())), pre...  8.86 us
  transfers between devices with their start and end apart: 6, of which 6 were waited for; matrix products, arithmetic and copies ran while one was open for 5% of the time, Pallas kernels for 0%

profile of v7, /device:TPU:57, one launch (start us, length us, event | category | flops | bytes accessed | tf_op | source)
XLA Modules:
  0.0 317.1 jit_solution(16972806199803100256)
XLA Ops:
  6.5 2.5 shard_map.190
  10.1 10.6 %all-to-all-start = ((bf16[32,1,2]{2,1,0:T(2,128)(2,1)}), bf16[32,1,2]{2,1,0:T(2,128)(2,1)S(1)}, u32[]{:S(2)}, u32[]{:S(2)}) async-start(bf16[32,1,2]{2,1,0:T(2,128)(2,1)} %all_to_all.20), calls=%async_computation | async-start | bytes 32768 | tf_op jit(solution)/shard_map/all_to_all | solution.py:141
  21.3 1.2 reshape.370
  22.5 6.0 %all-to-all-done = bf16[32,1,2]{2,1,0:T(2,128)(2,1)S(1)} async-done(((bf16[32,1,2]{2,1,0:T(2,128)(2,1)}), bf16[32,1,2]{2,1,0:T(2,128)(2,1)S(1)}, u32[]{:S(2)}, u32[]{:S(2)}) %all-to-all-start) | async-done | bytes 160 | tf_op jit(solution)/shard_map/all_to_all | solution.py:141
  28.5 4.7 %all-to-all-start.1 = ((bf16[32,2,4096]{2,1,0:T(2,128)(2,1)}), bf16[32,2,4096]{2,1,0:T(2,128)(2,1)S(1)}, u32[]{:S(2)}, u32[]{:S(2)}) async-start(bf16[32,2,4096]{2,1,0:T(2,128)(2,1)} %reshape.370), calls=%async_computation.1 | async-start | bytes 1048576 | tf_op jit(solution)/shard_map/all_to_all | solution.py:140
  33.7 21.8 %all-to-all-done.1 = bf16[32,2,4096]{2,1,0:T(2,128)(2,1)S(1)} async-done(((bf16[32,2,4096]{2,1,0:T(2,128)(2,1)}), bf16[32,2,4096]{2,1,0:T(2,128)(2,1)S(1)}, u32[]{:S(2)}, u32[]{:S(2)}) %all-to-all-start.1) | async-done | bytes 524320 | tf_op jit(solution)/shard_map/all_to_all | solution.py:140
  56.3 1.4 broadcast_in_dim.16
  57.7 7.5 %all-to-all-start.2 = ((bf16[8,256,512]{1,2,0:T(8,128)(2,1)}), bf16[8,256,512]{1,2,0:T(8,128)(2,1)}, u32[]{:S(2)}, u32[]{:S(2)}) async-start(bf16[8,256,512]{1,2,0:T(8,128)(2,1)} %broadcast_in_dim.16), calls=%async_computation.2 | async-start | bytes 4194304 | tf_op jit(solution)/shard_map/all_to_all | solution.py:156
  65.3 1.0 slice.56
  66.5 0.8 copy.59
  67.8 22.1 %all-to-all-done.2 = bf16[8,256,512]{1,2,0:T(8,128)(2,1)} async-done(((bf16[8,256,512]{1,2,0:T(8,128)(2,1)}), bf16[8,256,512]{1,2,0:T(8,128)(2,1)}, u32[]{:S(2)}, u32[]{:S(2)}) %all-to-all-start.2) | async-done | bytes 2097184 | tf_op jit(solution)/shard_map/all_to_all | solution.py:156
  89.8 2.1 convert_reduce_fusion
  92.0 2.2 multiply_reduce_fusion
  94.2 2.6 fusion.7
  97.5 1.4 copy-done.4
  100.4 25.6 %all-reduce = (bf16[256,16]{0,1:T(8,128)(2,1)S(1)}, bf16[256,16]{0,1:T(8,128)(2,1)S(1)}, bf16[256,16]{0,1:T(8,128)(2,1)S(1)}) all-reduce(f32[256,16]{0,1:T(8,128)S(1)} %get-tuple-element.6, f32[256,16]{0,1:T(8,128)S(1)} %get-tuple-element.7, f32[256,16]{0,1:T(8,128)S(1)} %get-tuple-element.5), channel_id=1, replica_groups=mesh['req'=32,'mlp'=8] {'mlp'}, use_global_device_ids=true, to_apply=%region_14.15 | all-reduce | flops 12288 | bytes 73728 | tf_op jit(solution)/shard_map/psum | solution.py:172
  126.0 0.9 broadcast_multiply_fusion.1
  126.9 77.5 %all-gather.2.cloned.1.call-done = bf16[4096,3072]{1,0:T(8,128)(2,1)} async-done(((bf16[128,3072]{1,0:T(8,128)(2,1)}), bf16[4096,3072]{1,0:T(8,128)(2,1)}) %all-gather.2.cloned.1.call-update) | async-done | bytes 25165840 | tf_op jit(solution)/shard_map/all_gather | solution.py:192
  204.5 8.7 %fusion = f32[256,1792]{1,0:T(8,128)S(1)} fusion(bf16[256,4096]{0,1:T(8,128)(2,1)} %copy-done.1, bf16[4096,3072]{1,0:T(8,128)(2,1)} %all-gather.2.cloned.1.call-done), kind=kOutput, calls=%fused_computation | convolution fusion | flops 3758096384 | bytes 18612224 | tf_op jit(solution)/shard_map/dot_general | solution.py:194
  215.7 2.4 fusion.12
  218.0 2.3 fusion.17
  220.3 8.9 %fusion.2 = f32[256,4096]{1,0:T(8,128)} fusion(bf16[4096,3072]{1,0:T(8,128)(2,1)} %all-gather.2.cloned.1.call-done, bf16[256,1024]{1,0:T(8,128)(2,1)S(1)} %fusion.17, bf16[256,256]{1,0:T(8,128)(2,1)S(1)} %copy-done.19), kind=kOutput, calls=%fused_computation.2 | convolution fusion | flops 2685665280 | bytes 15335424 | tf_op jit(solution)/shard_map/dot_general | solution.py:218
  229.2 6.6 %reshape.380 = f32[256,4,2,512]{3,2,1,0:T(2,128)} reshape(f32[256,4096]{1,0:T(8,128)} %fusion.2) | data formatting | bytes 8388608 | tf_op jit(solution)/shard_map/reshape | solution.py:226
  235.7 7.8 %fusion.87 = (f32[256,4,1,512]{3,2,1,0:T(1,128)S(1)}, f32[256,4,1,512]{3,2,1,0:T(1,128)S(1)}) fusion(f32[256,4,2,512]{3,2,1,0:T(2,128)} %reshape.380), kind=kLoop, calls=%fused_computation.136 | loop fusion | bytes 8388608 | tf_op jit(solution)/shard_map/slice | solution.py:228
  243.5 1.2 select_bitcast_fusion
  244.7 1.5 collective-permute-start
  246.2 3.8 %collective-permute-done = f32[256,4,512]{2,0,1:T(8,128)S(1)} collective-permute-done((f32[256,4,512]{2,0,1:T(8,128)S(1)}, f32[256,4,512]{2,0,1:T(8,128)S(1)}, u32[]{:S(2)}, u32[]{:S(2)}) %collective-permute-start) | collective-permute-done | bytes 2097184 | tf_op jit(solution)/shard_map/ppermute | solution.py:231
  250.0 2.6 bitcast_add_fusion
  253.3 28.4 %reduce-scatter.2.cloned.1.call-done = f32[256,1,512]{2,0,1:T(8,128)} async-done(((f32[256,4,512]{2,0,1:T(8,128)}), f32[256,1,512]{2,0,1:T(8,128)}) %reduce-scatter.2.cloned.1.call-update) | async-done | bytes 524304 | tf_op jit(solution)/shard_map/reduce_scatter | solution.py:233
  281.7 1.1 reshape.381
  283.6 25.3 %all_to_all.25 = bf16[32,2,4096]{2,1,0:T(2,128)(2,1)S(1)} all-to-all(bf16[32,2,4096]{2,1,0:T(2,128)(2,1)S(1)} %reshape.382), channel_id=1, replica_groups=mesh['req'=32,'mlp'=8] {'req'}, dimensions={0} | all-to-all | bytes 1048576 | tf_op jit(solution)/shard_map/all_to_all | solution.py:241
  309.4 0.8 copy.74
  (89 shorter events, 9.9 us)
Async XLA Ops:
  6.5 211.5 %copy-start = (bf16[1024,1024]{1,0:T(8,128)(2,1)S(1)}, bf16[1024,1024]{1,0:T(8,128)(2,1)}, u32[]{:S(2)}) copy-start(bf16[1024,1024]{1,0:T(8,128)(2,1)} %param.37) | copy-start | bytes 6291460
  6.5 2.6 copy-start.18
  6.5 14.2 %copy-start.9 = (bf16[32,8,512]{2,1,0:T(8,128)(2,1)S(1)}, bf16[32,8,512]{2,1,0:T(8,128)(2,1)}, u32[]{:S(2)}) copy-start(bf16[32,8,512]{2,1,0:T(8,128)(2,1)} %param.20) | copy-start | bytes 786436
  6.5 197.9 %all-gather.2.cloned.1.call-start = ((), (), s32[]{:S(2)}) async-start(), calls=%async_computation.5 | async-start | bytes 25952256 | tf_op jit(solution)/shard_map/all_gather | solution.py:192
  10.1 18.3 %all-to-all-start = ((bf16[32,1,2]{2,1,0:T(2,128)(2,1)}), bf16[32,1,2]{2,1,0:T(2,128)(2,1)S(1)}, u32[]{:S(2)}, u32[]{:S(2)}) async-start(bf16[32,1,2]{2,1,0:T(2,128)(2,1)} %all_to_all.20), calls=%async_computation | async-start | bytes 32768 | tf_op jit(solution)/shard_map/all_to_all | solution.py:141
  28.5 27.1 %all-to-all-start.1 = ((bf16[32,2,4096]{2,1,0:T(2,128)(2,1)}), bf16[32,2,4096]{2,1,0:T(2,128)(2,1)S(1)}, u32[]{:S(2)}, u32[]{:S(2)}) async-start(bf16[32,2,4096]{2,1,0:T(2,128)(2,1)} %reshape.370), calls=%async_computation.1 | async-start | bytes 1048576 | tf_op jit(solution)/shard_map/all_to_all | solution.py:140
  57.7 7.6 %copy-start.2 = (bf16[1024,256]{1,0:T(8,128)(2,1)S(1)}, bf16[1024,256]{1,0:T(8,128)(2,1)}, u32[]{:S(2)}) copy-start(bf16[1024,256]{1,0:T(8,128)(2,1)} %param.31) | copy-start | bytes 1572868
  57.7 8.6 %slice-start = ((bf16[1024,256]{1,0:T(8,128)(2,1)}), bf16[1024,64]{1,0:T(8,128)(2,1)S(1)}, s32[]{:S(2)}) async-start(bf16[1024,256]{1,0:T(8,128)(2,1)} %param.31), calls=%async_computation.7 | async-start | bytes 524288 | tf_op jit(solution)/shard_map/slice | solution.py:188
  57.7 32.1 %all-to-all-start.2 = ((bf16[8,256,512]{1,2,0:T(8,128)(2,1)}), bf16[8,256,512]{1,2,0:T(8,128)(2,1)}, u32[]{:S(2)}, u32[]{:S(2)}) async-start(bf16[8,256,512]{1,2,0:T(8,128)(2,1)} %broadcast_in_dim.16), calls=%async_computation.2 | async-start | bytes 4194304 | tf_op jit(solution)/shard_map/all_to_all | solution.py:156
  65.2 2.2 copy-start.14
  65.2 2.3 copy-start.16
  65.2 216.5 %reduce-scatter.2.cloned.1.call-start = ((), (), s32[]{:S(2)}) async-start(), calls=%async_computation.6 | async-start | bytes 2621440 | tf_op jit(solution)/shard_map/reduce_scatter | solution.py:233
  67.8 26.4 %copy-start.12 = (f32[4096]{0:T(1024)S(1)}, f32[4096]{0:T(1024)}, u32[]{:S(2)}) copy-start(f32[4096]{0:T(1024)} %param.25) | copy-start | bytes 49156
  67.8 26.4 %copy-start.13 = (f32[4096]{0:T(1024)S(1)}, f32[4096]{0:T(1024)}, u32[]{:S(2)}) copy-start(f32[4096]{0:T(1024)} %param.24) | copy-start | bytes 49156
  94.2 2.6 copy-start.3
  96.9 2.6 copy-start.1
  96.9 2.0 copy-start.4
  96.9 2.5 copy-start.5
  204.5 8.7 %copy-start.6 = (bf16[256,64,16]{0,2,1:T(8,128)(2,1)S(1)}, bf16[256,64,16]{0,2,1:T(8,128)(2,1)}, u32[]{:S(2)}) copy-start(bf16[256,64,16]{0,2,1:T(8,128)(2,1)} %get-tuple-element.17) | copy-start | bytes 1572868
  204.5 8.7 %copy-start.7 = (bf16[1024,192]{1,0:T(8,128)(2,1)S(1)}, bf16[1024,192]{1,0:T(8,128)(2,1)}, u32[]{:S(2)}) copy-start(bf16[1024,192]{1,0:T(8,128)(2,1)} %slice.56) | copy-start | bytes 1179652
  204.5 8.7 %copy-start.8 = (bf16[1024,64]{1,0:T(8,128)(2,1)S(1)}, bf16[1024,64]{1,0:T(8,128)(2,1)}, u32[]{:S(2)}) copy-start(bf16[1024,64]{1,0:T(8,128)(2,1)} %copy.59) | copy-start | bytes 393220
  213.2 1.7 copy-start.11
  214.5 3.5 %copy-start.17 = (f32[1024]{0:T(1024)S(1)}, f32[1024]{0:T(1024)}, u32[]{:S(2)}) copy-start(f32[1024]{0:T(1024)} %param.35) | copy-start | bytes 12292
  214.9 0.7 copy-start.10
  218.0 2.3 copy-start.19
  244.7 5.3 %collective-permute-start = (f32[256,4,512]{2,0,1:T(8,128)S(1)}, f32[256,4,512]{2,0,1:T(8,128)S(1)}, u32[]{:S(2)}, u32[]{:S(2)}) collective-permute-start(f32[256,4,512]{2,0,1:T(8,128)S(1)} %select_bitcast_fusion), channel_id=1, source_target_pairs={{0,1},{1,0},{2,3},{3,2},{4,5},{5,4},{6,7},{7,6},{8,9},{9,8},{10,11... | collective-permute-start | bytes 6291464 | tf_op jit(solution)/shard_map/ppermute | solution.py:231
  252.7 0.7 copy-start.15
Sparse Core Ops, SparseCore 0:
  9.9 194.5 all-gather.1
  252.8 28.8 reduce-scatter.1

commit v8 on v7

--- a/solution.py
+++ b/solution.py
@@ -215,18 +215,16 @@
     hidden_pre = hidden_pre + lift(picked[2], up_fc) + b_fc_in
     hidden = gelu_tanh(hidden_pre).astype(jnp.bfloat16)
     joined = jnp.concatenate([attn, hidden], axis=1)
-    part = lax.dot_general(
-        joined,
-        gathered[:, n_in:],
-        (((1,), (1,)), ((), ())),
-        preferred_element_type=jnp.float32,
-    )
     n_c = 2
     n_y = lax.axis_size("mlp") // n_c
-    grid = part.reshape(tok, n_y, n_c, width_m)
+    w_out = gathered[:, n_in:].reshape(n_y, n_c, width_m, joined.shape[1])
+    halves = [
+        jnp.einsum("tk,yfk->tyf", joined, w_out[:, c], preferred_element_type=jnp.float32)
+        for c in range(n_c)
+    ]
     first = lax.axis_index("mlp") % n_c == 0
-    keep = jnp.where(first, grid[:, :, 0, :], grid[:, :, 1, :])
-    send = jnp.where(first, grid[:, :, 1, :], grid[:, :, 0, :])
+    keep = jnp.where(first, halves[0], halves[1])
+    send = jnp.where(first, halves[1], halves[0])
     mates = [(i, i ^ 1) for i in range(n_y * n_c)]
     got = lax.ppermute(send, "mlp", mates)
     lanes = [[y * n_c + c for y in range(n_y)] for c in range(n_c)]

time: 322 us -> 313 us (0.972)
  local copies, waits for them, and re-layouts: 26 us -> 21.5 us
  matrix products: 26.1 us -> 22.3 us
    reshape x1 -> x0, local copies, waits for them, and re-layouts: 6.58 us -> none  [on_device(): grid = part.reshape(tok, n_y, n_c, width_m)]
    dot_general x1 -> x2, matrix products: 8.86 us -> 5.74 us  [on_device(): jnp.einsum('tk,yfk->tyf', joined, w_out[:, c], preferred_element_type=jnp...]
  transfers between devices with their start and end apart: 6 -> 6, of which waited for: 6 -> 6; matrix products, arithmetic and copies ran while one was open for 5% -> 6% of each run, Pallas kernels for 0% -> 0%
where the time goes in v8:
time: 313 us; the launch traced here: 308 us
  waiting for transfers between devices  160 us (51%)
  blocking collectives  50.9 us (16%)
  starting transfers between devices  24.3 us (8%)
  matrix products  22.3 us (7%)
  local copies, waits for them, and re-layouts  21.5 us (7%)
  between operations  13.9 us (4%)
  other arithmetic  12.6 us (4%)
    all_gather x1, waiting for transfers between devices, on_device(): gathered = lax.all_gather(packed, 'req', axis=0, tiled=True)  77.5 us
    reduce_scatter x1, waiting for transfers between devices, on_device(): lax.psum_scatter(keep + got, 'mlp', scatter_dimension=1, tiled=True, axis...  28.4 us
    psum x1, blocking collectives, on_device(): lax.psum((pick(down_query), pick(down_value), pick(down_fc)), 'mlp')  25.6 us
    all_to_all x1, blocking collectives, on_device(): lax.all_to_all(leaving, 'req', split_axis=0, concat_axis=0, tiled=True)  25.3 us
    all_to_all x1, waiting for transfers between devices, on_device(): lax.all_to_all(copies, 'mlp', split_axis=0, concat_axis=0, tiled=True)  22.1 us
    all_to_all x1, waiting for transfers between devices, on_device(): lax.all_to_all(outgoing, 'req', split_axis=0, concat_axis=0, tiled=True)  21.8 us
    all_to_all x1, starting transfers between devices, on_device(): lax.all_to_all(filled, 'req', split_axis=0, concat_axis=0, tiled=True)  10.6 us
    dot_general x1, matrix products, on_device(): jnp.dot(full_ln, gathered[:, :n_in], preferred_element_type=jnp.float32)  8.66 us
  transfers between devices with their start and end apart: 6, of which 6 were waited for; matrix products, arithmetic and copies ran while one was open for 6% of the time, Pallas kernels for 0%

profile of v8, /device:TPU:57, one launch (start us, length us, event | category | flops | bytes accessed | tf_op | source)
XLA Modules:
  0.0 307.6 jit_solution(17254424407764039812)
XLA Ops:
  6.5 2.5 shard_map.190
  10.1 10.6 %all-to-all-start = ((bf16[32,1,2]{2,1,0:T(2,128)(2,1)}), bf16[32,1,2]{2,1,0:T(2,128)(2,1)S(1)}, u32[]{:S(2)}, u32[]{:S(2)}) async-start(bf16[32,1,2]{2,1,0:T(2,128)(2,1)} %all_to_all.20), calls=%async_computation | async-start | bytes 32768 | tf_op jit(solution)/shard_map/all_to_all | solution.py:141
  21.3 1.2 reshape.366
  22.5 6.0 %all-to-all-done = bf16[32,1,2]{2,1,0:T(2,128)(2,1)S(1)} async-done(((bf16[32,1,2]{2,1,0:T(2,128)(2,1)}), bf16[32,1,2]{2,1,0:T(2,128)(2,1)S(1)}, u32[]{:S(2)}, u32[]{:S(2)}) %all-to-all-start) | async-done | bytes 160 | tf_op jit(solution)/shard_map/all_to_all | solution.py:141
  28.5 4.7 %all-to-all-start.1 = ((bf16[32,2,4096]{2,1,0:T(2,128)(2,1)}), bf16[32,2,4096]{2,1,0:T(2,128)(2,1)S(1)}, u32[]{:S(2)}, u32[]{:S(2)}) async-start(bf16[32,2,4096]{2,1,0:T(2,128)(2,1)} %reshape.366), calls=%async_computation.1 | async-start | bytes 1048576 | tf_op jit(solution)/shard_map/all_to_all | solution.py:140
  33.7 21.8 %all-to-all-done.1 = bf16[32,2,4096]{2,1,0:T(2,128)(2,1)S(1)} async-done(((bf16[32,2,4096]{2,1,0:T(2,128)(2,1)}), bf16[32,2,4096]{2,1,0:T(2,128)(2,1)S(1)}, u32[]{:S(2)}, u32[]{:S(2)}) %all-to-all-start.1) | async-done | bytes 524320 | tf_op jit(solution)/shard_map/all_to_all | solution.py:140
  56.3 1.4 broadcast_in_dim.16
  57.7 7.5 %all-to-all-start.2 = ((bf16[8,256,512]{1,2,0:T(8,128)(2,1)}), bf16[8,256,512]{1,2,0:T(8,128)(2,1)}, u32[]{:S(2)}, u32[]{:S(2)}) async-start(bf16[8,256,512]{1,2,0:T(8,128)(2,1)} %broadcast_in_dim.16), calls=%async_computation.2 | async-start | bytes 4194304 | tf_op jit(solution)/shard_map/all_to_all | solution.py:156
  65.3 1.0 slice.54
  66.5 0.8 copy.59
  67.8 22.1 %all-to-all-done.2 = bf16[8,256,512]{1,2,0:T(8,128)(2,1)} async-done(((bf16[8,256,512]{1,2,0:T(8,128)(2,1)}), bf16[8,256,512]{1,2,0:T(8,128)(2,1)}, u32[]{:S(2)}, u32[]{:S(2)}) %all-to-all-start.2) | async-done | bytes 2097184 | tf_op jit(solution)/shard_map/all_to_all | solution.py:156
  89.8 2.1 convert_reduce_fusion
  92.0 2.2 multiply_reduce_fusion
  94.2 2.6 fusion.7
  97.5 1.4 copy-done.5
  100.4 25.6 %all-reduce = (bf16[256,16]{0,1:T(8,128)(2,1)S(1)}, bf16[256,16]{0,1:T(8,128)(2,1)S(1)}, bf16[256,16]{0,1:T(8,128)(2,1)S(1)}) all-reduce(f32[256,16]{0,1:T(8,128)S(1)} %get-tuple-element.6, f32[256,16]{0,1:T(8,128)S(1)} %get-tuple-element.7, f32[256,16]{0,1:T(8,128)S(1)} %get-tuple-element.5), channel_id=1, replica_groups=mesh['req'=32,'mlp'=8] {'mlp'}, use_global_device_ids=true, to_apply=%region_14.15 | all-reduce | flops 12288 | bytes 73728 | tf_op jit(solution)/shard_map/psum | solution.py:172
  126.0 0.9 broadcast_multiply_fusion.1
  126.9 77.5 %all-gather.2.cloned.1.call-done = bf16[4096,3072]{1,0:T(8,128)(2,1)} async-done(((bf16[128,3072]{1,0:T(8,128)(2,1)}), bf16[4096,3072]{1,0:T(8,128)(2,1)}) %all-gather.2.cloned.1.call-update) | async-done | bytes 25165840 | tf_op jit(solution)/shard_map/all_gather | solution.py:192
  204.5 8.7 %fusion = f32[256,1792]{1,0:T(8,128)S(1)} fusion(bf16[256,4096]{0,1:T(8,128)(2,1)} %copy-done.2, bf16[4096,3072]{1,0:T(8,128)(2,1)} %all-gather.2.cloned.1.call-done), kind=kOutput, calls=%fused_computation | convolution fusion | flops 3758096384 | bytes 18612224 | tf_op jit(solution)/shard_map/dot_general | solution.py:194
  216.2 1.7 fusion.12
  217.9 2.2 fusion.17
  220.1 8.5 %slice.77 = bf16[4096,1280]{1,0:T(8,128)(2,1)} slice(bf16[4096,3072]{1,0:T(8,128)(2,1)} %all-gather.2.cloned.1.call-done), slice={[0:4096], [1792:3072]} | slice | bytes 20971520 | tf_op jit(solution)/shard_map/slice | solution.py:220
  228.7 4.2 %fusion.3 = f32[256,4,512]{2,0,1:T(8,128)S(1)} fusion(bf16[4,2,512,1280]{3,2,1,0:T(8,128)(2,1)} %bitcast.84, bf16[256,1024]{1,0:T(8,128)(2,1)S(1)} %fusion.17, bf16[256,256]{1,0:T(8,128)(2,1)S(1)} %fusion.12), kind=kOutput, calls=%fused_computation.5 | convolution fusion | flops 1343488000 | bytes 7995392 | tf_op jit(solution)/shard_map/tk,yfk->tyf/dot_general | solution.py:222
  232.9 1.3 copy-done.1
  234.2 1.6 broadcast_select_fusion
  235.8 1.5 collective-permute-start
  237.3 3.8 %collective-permute-done = f32[256,4,512]{2,0,1:T(8,128)S(1)} collective-permute-done((f32[256,4,512]{2,0,1:T(8,128)S(1)}, f32[256,4,512]{2,0,1:T(8,128)S(1)}, u32[]{:S(2)}, u32[]{:S(2)}) %collective-permute-start) | collective-permute-done | bytes 2097184 | tf_op jit(solution)/shard_map/ppermute | solution.py:229
  241.1 2.1 select_add_fusion
  243.9 28.4 %reduce-scatter.2.cloned.1.call-done = f32[256,1,512]{2,0,1:T(8,128)} async-done(((f32[256,4,512]{2,0,1:T(8,128)}), f32[256,1,512]{2,0,1:T(8,128)}) %reduce-scatter.2.cloned.1.call-update) | async-done | bytes 524304 | tf_op jit(solution)/shard_map/reduce_scatter | solution.py:231
  272.2 1.1 reshape.377
  274.1 25.3 %all_to_all.25 = bf16[32,2,4096]{2,1,0:T(2,128)(2,1)S(1)} all-to-all(bf16[32,2,4096]{2,1,0:T(2,128)(2,1)S(1)} %reshape.378), channel_id=1, replica_groups=mesh['req'=32,'mlp'=8] {'req'}, dimensions={0} | all-to-all | bytes 1048576 | tf_op jit(solution)/shard_map/all_to_all | solution.py:239
  299.9 0.8 copy.74
  (88 shorter events, 10.4 us)
Async XLA Ops:
  6.5 211.4 %copy-start = (bf16[1024,1024]{1,0:T(8,128)(2,1)S(1)}, bf16[1024,1024]{1,0:T(8,128)(2,1)}, u32[]{:S(2)}) copy-start(bf16[1024,1024]{1,0:T(8,128)(2,1)} %param.37) | copy-start | bytes 6291460
  6.5 2.6 copy-start.19
  6.5 14.2 %copy-start.10 = (bf16[32,8,512]{2,1,0:T(8,128)(2,1)S(1)}, bf16[32,8,512]{2,1,0:T(8,128)(2,1)}, u32[]{:S(2)}) copy-start(bf16[32,8,512]{2,1,0:T(8,128)(2,1)} %param.20) | copy-start | bytes 786436
  6.5 197.9 %all-gather.2.cloned.1.call-start = ((), (), s32[]{:S(2)}) async-start(), calls=%async_computation.5 | async-start | bytes 25952256 | tf_op jit(solution)/shard_map/all_gather | solution.py:192
  10.1 18.3 %all-to-all-start = ((bf16[32,1,2]{2,1,0:T(2,128)(2,1)}), bf16[32,1,2]{2,1,0:T(2,128)(2,1)S(1)}, u32[]{:S(2)}, u32[]{:S(2)}) async-start(bf16[32,1,2]{2,1,0:T(2,128)(2,1)} %all_to_all.20), calls=%async_computation | async-start | bytes 32768 | tf_op jit(solution)/shard_map/all_to_all | solution.py:141
  28.5 27.1 %all-to-all-start.1 = ((bf16[32,2,4096]{2,1,0:T(2,128)(2,1)}), bf16[32,2,4096]{2,1,0:T(2,128)(2,1)S(1)}, u32[]{:S(2)}, u32[]{:S(2)}) async-start(bf16[32,2,4096]{2,1,0:T(2,128)(2,1)} %reshape.366), calls=%async_computation.1 | async-start | bytes 1048576 | tf_op jit(solution)/shard_map/all_to_all | solution.py:140
  57.7 7.6 %copy-start.3 = (bf16[1024,256]{1,0:T(8,128)(2,1)S(1)}, bf16[1024,256]{1,0:T(8,128)(2,1)}, u32[]{:S(2)}) copy-start(bf16[1024,256]{1,0:T(8,128)(2,1)} %param.31) | copy-start | bytes 1572868
  57.7 8.6 %slice-start = ((bf16[1024,256]{1,0:T(8,128)(2,1)}), bf16[1024,64]{1,0:T(8,128)(2,1)S(1)}, s32[]{:S(2)}) async-start(bf16[1024,256]{1,0:T(8,128)(2,1)} %param.31), calls=%async_computation.7 | async-start | bytes 524288 | tf_op jit(solution)/shard_map/slice | solution.py:188
  57.7 32.1 %all-to-all-start.2 = ((bf16[8,256,512]{1,2,0:T(8,128)(2,1)}), bf16[8,256,512]{1,2,0:T(8,128)(2,1)}, u32[]{:S(2)}, u32[]{:S(2)}) async-start(bf16[8,256,512]{1,2,0:T(8,128)(2,1)} %broadcast_in_dim.16), calls=%async_computation.2 | async-start | bytes 4194304 | tf_op jit(solution)/shard_map/all_to_all | solution.py:156
  65.2 2.2 copy-start.15
  65.2 2.3 copy-start.18
  65.2 207.0 %reduce-scatter.2.cloned.1.call-start = ((), (), s32[]{:S(2)}) async-start(), calls=%async_computation.6 | async-start | bytes 2621440 | tf_op jit(solution)/shard_map/reduce_scatter | solution.py:231
  67.8 26.4 %copy-start.13 = (f32[4096]{0:T(1024)S(1)}, f32[4096]{0:T(1024)}, u32[]{:S(2)}) copy-start(f32[4096]{0:T(1024)} %param.25) | copy-start | bytes 49156
  67.8 26.4 %copy-start.14 = (f32[4096]{0:T(1024)S(1)}, f32[4096]{0:T(1024)}, u32[]{:S(2)}) copy-start(f32[4096]{0:T(1024)} %param.24) | copy-start | bytes 49156
  94.2 2.6 copy-start.4
  96.9 2.6 copy-start.2
  96.9 2.0 copy-start.5
  96.9 2.5 copy-start.6
  204.5 8.7 %copy-start.7 = (bf16[256,64,16]{0,2,1:T(8,128)(2,1)S(1)}, bf16[256,64,16]{0,2,1:T(8,128)(2,1)}, u32[]{:S(2)}) copy-start(bf16[256,64,16]{0,2,1:T(8,128)(2,1)} %get-tuple-element.15) | copy-start | bytes 1572868
  204.5 8.7 %copy-start.8 = (bf16[1024,192]{1,0:T(8,128)(2,1)S(1)}, bf16[1024,192]{1,0:T(8,128)(2,1)}, u32[]{:S(2)}) copy-start(bf16[1024,192]{1,0:T(8,128)(2,1)} %slice.54) | copy-start | bytes 1179652
  204.5 8.7 %copy-start.9 = (bf16[1024,64]{1,0:T(8,128)(2,1)S(1)}, bf16[1024,64]{1,0:T(8,128)(2,1)}, u32[]{:S(2)}) copy-start(bf16[1024,64]{1,0:T(8,128)(2,1)} %copy.59) | copy-start | bytes 393220
  213.2 1.7 copy-start.12
  214.9 0.7 copy-start.11
  214.9 1.3 copy-start.17
  228.7 5.5 %copy-start.1 = (bf16[4096,1280]{1,0:T(8,128)(2,1)S(1)}, bf16[4096,1280]{1,0:T(8,128)(2,1)}, u32[]{:S(2)}) copy-start(bf16[4096,1280]{1,0:T(8,128)(2,1)} %slice.77) | copy-start | bytes 31457284
  235.8 5.3 %collective-permute-start = (f32[256,4,512]{2,0,1:T(8,128)S(1)}, f32[256,4,512]{2,0,1:T(8,128)S(1)}, u32[]{:S(2)}, u32[]{:S(2)}) collective-permute-start(f32[256,4,512]{2,0,1:T(8,128)S(1)} %get-tuple-element.24), channel_id=1, source_target_pairs={{0,1},{1,0},{2,3},{3,2},{4,5},{5,4},{6,7},{7,6},{8,9},{9,8},{10,11... | collective-permute-start | bytes 6291464 | tf_op jit(solution)/shard_map/ppermute | solution.py:229
  243.2 0.7 copy-start.16
Sparse Core Ops, SparseCore 0:
  9.9 194.5 all-gather.1
  243.3 28.8 reduce-scatter.1

commit v9 on v6

--- a/solution.py
+++ b/solution.py
@@ -94,6 +94,30 @@
             transcendentals=0,
         ),
     )(wq, wk, wv, wfi, wao, wfo)
+
+
+def project_kernel(a_ref, b_ref, o_ref):
+    o_ref[...] = jnp.dot(a_ref[...], b_ref[...], preferred_element_type=jnp.float32)
+
+
+def project(a, b, cols):
+    rows, depth = a.shape
+    tile = 256
+    return pl.pallas_call(
+        project_kernel,
+        out_shape=jax.ShapeDtypeStruct((rows, cols), jnp.float32),
+        grid=(cols // tile,),
+        in_specs=[
+            pl.BlockSpec((rows, depth), lambda j: (0, 0)),
+            pl.BlockSpec((depth, tile), lambda j: (0, j)),
+        ],
+        out_specs=pl.BlockSpec((rows, tile), lambda j: (0, j)),
+        cost_estimate=pl.CostEstimate(
+            flops=2 * rows * depth * cols,
+            bytes_accessed=2 * rows * depth + 2 * depth * cols + 4 * rows * cols,
+            transcendentals=0,
+        ),
+    )(a, b)
 
 
 def on_device(
@@ -191,7 +215,7 @@
     packed = pack_weights(w_query, w_key, w_value, w_fc_in, w_attn_out, w_fc_out)
     gathered = lax.all_gather(packed, "req", axis=0, tiled=True)
     n_in = 3 * heads_w + ff_w
-    base = jnp.dot(full_ln, gathered[:, :n_in], preferred_element_type=jnp.float32)
+    base = project(full_ln, gathered, n_in)
     base_q = base[:, :heads_w]
     base_k = base[:, heads_w : 2 * heads_w]
     base_v = base[:, 2 * heads_w : 3 * heads_w]

time: 307 us -> 311 us (1.013)
  Pallas kernels: 2.52 us -> 13.6 us
  matrix products: 26 us -> 18.7 us
    pallas_call x0 -> x1, Pallas kernels: none -> 11 us  [project(): pl.pallas_call(project_kernel, out_shape=jax.ShapeDtypeStruct((rows, cols...]
    dot_general x1 -> x0, matrix products: 8.66 us -> none  [on_device(): jnp.dot(full_ln, gathered[:, :n_in], preferred_element_type=jnp.float32)]
where the time goes in v9:
time: 311 us; the launch traced here: 310 us
  waiting for transfers between devices  165 us (53%)
  blocking collectives  52 us (17%)
  starting transfers between devices  22.6 us (7%)
  matrix products  18.7 us (6%)
  between operations  13.8 us (4%)
  Pallas kernels  13.6 us (4%)
  local copies, waits for them, and re-layouts  13 us (4%)
  other arithmetic  11.5 us (4%)
    all_gather x1, waiting for transfers between devices, on_device(): gathered = lax.all_gather(packed, 'req', axis=0, tiled=True)  76.1 us
    reduce_scatter x1, waiting for transfers between devices, on_device(): shares = lax.psum_scatter(part, 'mlp', scatter_dimension=1, tiled=True)  38.7 us
    all_to_all x1, blocking collectives, on_device(): lax.all_to_all(leaving, 'req', split_axis=0, concat_axis=0, tiled=True)  26.5 us
    psum x1, blocking collectives, on_device(): lax.psum((pick(down_query), pick(down_value), pick(down_fc)), 'mlp')  25.5 us
    all_to_all x1, waiting for transfers between devices, on_device(): lax.all_to_all(outgoing, 'req', split_axis=0, concat_axis=0, tiled=True)  22.1 us
    all_to_all x1, waiting for transfers between devices, on_device(): lax.all_to_all(copies, 'mlp', split_axis=0, concat_axis=0, tiled=True)  22.1 us
    pallas_call x1, Pallas kernels, project(): pl.pallas_call(project_kernel, out_shape=jax.ShapeDtypeStruct((rows, cols...  11 us
    all_to_all x1, starting transfers between devices, on_device(): lax.all_to_all(filled, 'req', split_axis=0, concat_axis=0, tiled=True)  10.6 us
  transfers between devices with their start and end apart: 5, of which 5 were waited for; matrix products, arithmetic and copies ran while one was open for 6% of the time, Pallas kernels for 0%

profile of v9, /device:TPU:57, one launch (start us, length us, event | category | flops | bytes accessed | tf_op | source)
XLA Modules:
  0.0 310.1 jit_solution(18260664878585416537)
XLA Ops:
  6.5 2.5 shard_map.190
  9.4 0.7 all_to_all.20
  10.1 10.6 %all-to-all-start = ((bf16[32,1,2]{2,1,0:T(2,128)(2,1)}), bf16[32,1,2]{2,1,0:T(2,128)(2,1)S(1)}, u32[]{:S(2)}, u32[]{:S(2)}) async-start(bf16[32,1,2]{2,1,0:T(2,128)(2,1)} %all_to_all.20), calls=%async_computation | async-start | bytes 32768 | tf_op jit(solution)/shard_map/all_to_all | solution.py:165
  21.3 1.2 reshape.362
  22.4 6.0 %all-to-all-done = bf16[32,1,2]{2,1,0:T(2,128)(2,1)S(1)} async-done(((bf16[32,1,2]{2,1,0:T(2,128)(2,1)}), bf16[32,1,2]{2,1,0:T(2,128)(2,1)S(1)}, u32[]{:S(2)}, u32[]{:S(2)}) %all-to-all-start) | async-done | bytes 160 | tf_op jit(solution)/shard_map/all_to_all | solution.py:165
  28.5 4.7 %all-to-all-start.1 = ((bf16[32,2,4096]{2,1,0:T(2,128)(2,1)}), bf16[32,2,4096]{2,1,0:T(2,128)(2,1)S(1)}, u32[]{:S(2)}, u32[]{:S(2)}) async-start(bf16[32,2,4096]{2,1,0:T(2,128)(2,1)} %reshape.362), calls=%async_computation.1 | async-start | bytes 1048576 | tf_op jit(solution)/shard_map/all_to_all | solution.py:164
  33.7 22.1 %all-to-all-done.1 = bf16[32,2,4096]{2,1,0:T(2,128)(2,1)S(1)} async-done(((bf16[32,2,4096]{2,1,0:T(2,128)(2,1)}), bf16[32,2,4096]{2,1,0:T(2,128)(2,1)S(1)}, u32[]{:S(2)}, u32[]{:S(2)}) %all-to-all-start.1) | async-done | bytes 524320 | tf_op jit(solution)/shard_map/all_to_all | solution.py:164
  56.4 1.6 broadcast_in_dim.13
  58.1 7.2 %all-to-all-start.2 = ((bf16[8,256,512]{2,1,0:T(8,128)(2,1)}), bf16[8,256,512]{2,1,0:T(8,128)(2,1)}, u32[]{:S(2)}, u32[]{:S(2)}) async-start(bf16[8,256,512]{2,1,0:T(8,128)(2,1)} %broadcast_in_dim.13), calls=%async_computation.2 | async-start | bytes 4194304 | tf_op jit(solution)/shard_map/all_to_all | solution.py:180
  65.3 1.1 slice.44
  66.6 0.8 copy.52
  67.8 22.1 %all-to-all-done.2 = bf16[8,256,512]{2,1,0:T(8,128)(2,1)} async-done(((bf16[8,256,512]{2,1,0:T(8,128)(2,1)}), bf16[8,256,512]{2,1,0:T(8,128)(2,1)}, u32[]{:S(2)}, u32[]{:S(2)}) %all-to-all-start.2) | async-done | bytes 2097184 | tf_op jit(solution)/shard_map/all_to_all | solution.py:180
  89.9 2.2 convert_bitcast_fusion
  92.8 2.1 convert_reduce_fusion
  94.8 2.3 fusion.3
  97.2 0.8 add_convert_fusion.a_ref
  99.0 1.4 copy-done.4
  102.0 25.5 %all-reduce = (bf16[256,16]{0,1:T(8,128)(2,1)S(1)}, bf16[256,16]{0,1:T(8,128)(2,1)S(1)}, bf16[256,16]{0,1:T(8,128)(2,1)S(1)}) all-reduce(f32[256,16]{0,1:T(8,128)S(1)} %get-tuple-element.6, f32[256,16]{0,1:T(8,128)S(1)} %get-tuple-element.7, f32[256,16]{0,1:T(8,128)S(1)} %get-tuple-element.5), channel_id=1, replica_groups=mesh['req'=32,'mlp'=8] {'mlp'}, use_global_device_ids=true, to_apply=%region_14.15 | all-reduce | flops 12288 | bytes 73728 | tf_op jit(solution)/shard_map/psum | solution.py:196
  127.5 0.9 broadcast_multiply_fusion.1
  128.4 76.1 %all-gather.2.cloned.1.call-done.b_ref = bf16[4096,3072]{1,0:T(8,128)(2,1)} async-done(((bf16[128,3072]{1,0:T(8,128)(2,1)}), bf16[4096,3072]{1,0:T(8,128)(2,1)}) %all-gather.2.cloned.1.call-update) | async-done | bytes 25165840 | tf_op jit(solution)/shard_map/all_gather | solution.py:216
  204.5 11.0 %shard_map.191 = f32[256,1792]{1,0:T(8,128)} custom-call(bf16[256,4096]{1,0:T(8,128)(2,1)} %copy-done.1, bf16[4096,3072]{1,0:T(8,128)(2,1)} %all-gather.2.cloned.1.call-done.b_ref), custom_call_target="tpu_custom_call" | custom-call | flops 3758096384 | bytes 18612224 | tf_op jit(solution)/shard_map/pallas_call | solution.py:106
  215.5 1.0 slice_bitcast_fusion
  216.5 1.9 fusion.6
  219.5 0.7 copy-done.7
  220.3 2.4 fusion.8
  222.6 2.3 fusion.13
  224.9 8.9 %fusion = f32[256,4096]{1,0:T(8,128)} fusion(bf16[4096,3072]{1,0:T(8,128)(2,1)} %all-gather.2.cloned.1.call-done.b_ref, bf16[256,1024]{1,0:T(8,128)(2,1)S(1)} %fusion.13, bf16[256,256]{1,0:T(8,128)(2,1)S(1)} %copy-done.15), kind=kOutput, calls=%fused_computation | convolution fusion | flops 2685665280 | bytes 15335424 | tf_op jit(solution)/shard_map/dot_general | solution.py:242
  233.8 38.7 %reduce-scatter.2.cloned.1.call-done = f32[256,512]{1,0:T(8,128)} async-done(((f32[256,4096]{1,0:T(8,128)}), f32[256,512]{1,0:T(8,128)}) %reduce-scatter.2.cloned.1.call-update) | async-done | bytes 524304 | tf_op jit(solution)/shard_map/reduce_scatter | solution.py:248
  272.5 1.1 add_convert_fusion.1
  274.5 26.5 %all_to_all.25 = bf16[32,2,4096]{2,1,0:T(2,128)(2,1)} all-to-all(bf16[32,2,4096]{2,1,0:T(2,128)(2,1)S(1)} %reshape.374), channel_id=1, replica_groups=mesh['req'=32,'mlp'=8] {'req'}, dimensions={0} | all-to-all | bytes 1048576 | tf_op jit(solution)/shard_map/all_to_all | solution.py:253
  301.0 1.2 reshape.375
  302.5 0.8 copy.63
  (75 shorter events, 8.0 us)
Async XLA Ops:
  6.5 216.1 %copy-start = (bf16[1024,1024]{1,0:T(8,128)(2,1)S(1)}, bf16[1024,1024]{1,0:T(8,128)(2,1)}, u32[]{:S(2)}) copy-start(bf16[1024,1024]{1,0:T(8,128)(2,1)} %param.37) | copy-start | bytes 6291460
  6.5 2.6 copy-start.14
  6.5 14.2 %copy-start.6 = (bf16[32,8,512]{2,1,0:T(8,128)(2,1)S(1)}, bf16[32,8,512]{2,1,0:T(8,128)(2,1)}, u32[]{:S(2)}) copy-start(bf16[32,8,512]{2,1,0:T(8,128)(2,1)} %param.20) | copy-start | bytes 786436
  6.5 197.9 %all-gather.2.cloned.1.call-start = ((), (), s32[]{:S(2)}) async-start(), calls=%async_computation.5 | async-start | bytes 25952256 | tf_op jit(solution)/shard_map/all_gather | solution.py:216
  10.1 18.3 %all-to-all-start = ((bf16[32,1,2]{2,1,0:T(2,128)(2,1)}), bf16[32,1,2]{2,1,0:T(2,128)(2,1)S(1)}, u32[]{:S(2)}, u32[]{:S(2)}) async-start(bf16[32,1,2]{2,1,0:T(2,128)(2,1)} %all_to_all.20), calls=%async_computation | async-start | bytes 32768 | tf_op jit(solution)/shard_map/all_to_all | solution.py:165
  28.5 27.3 %all-to-all-start.1 = ((bf16[32,2,4096]{2,1,0:T(2,128)(2,1)}), bf16[32,2,4096]{2,1,0:T(2,128)(2,1)S(1)}, u32[]{:S(2)}, u32[]{:S(2)}) async-start(bf16[32,2,4096]{2,1,0:T(2,128)(2,1)} %reshape.362), calls=%async_computation.1 | async-start | bytes 1048576 | tf_op jit(solution)/shard_map/all_to_all | solution.py:164
  58.1 7.3 %copy-start.2 = (bf16[1024,256]{1,0:T(8,128)(2,1)S(1)}, bf16[1024,256]{1,0:T(8,128)(2,1)}, u32[]{:S(2)}) copy-start(bf16[1024,256]{1,0:T(8,128)(2,1)} %param.31) | copy-start | bytes 1572868
  58.1 8.3 %slice-start = ((bf16[1024,256]{1,0:T(8,128)(2,1)}), bf16[1024,64]{1,0:T(8,128)(2,1)S(1)}, s32[]{:S(2)}) async-start(bf16[1024,256]{1,0:T(8,128)(2,1)} %param.31), calls=%async_computation.7 | async-start | bytes 524288 | tf_op jit(solution)/shard_map/slice | solution.py:212
  58.1 31.8 %all-to-all-start.2 = ((bf16[8,256,512]{2,1,0:T(8,128)(2,1)}), bf16[8,256,512]{2,1,0:T(8,128)(2,1)}, u32[]{:S(2)}, u32[]{:S(2)}) async-start(bf16[8,256,512]{2,1,0:T(8,128)(2,1)} %broadcast_in_dim.13), calls=%async_computation.2 | async-start | bytes 4194304 | tf_op jit(solution)/shard_map/all_to_all | solution.py:180
  65.3 2.2 copy-start.10
  65.3 2.3 copy-start.12
  65.3 207.2 %reduce-scatter.2.cloned.1.call-start = ((), (), s32[]{:S(2)}) async-start(), calls=%async_computation.6 | async-start | bytes 4718592 | tf_op jit(solution)/shard_map/reduce_scatter | solution.py:248
  92.7 4.4 %copy-start.8 = (f32[4096]{0:T(1024)S(1)}, f32[4096]{0:T(1024)}, u32[]{:S(2)}) copy-start(f32[4096]{0:T(1024)} %param.25) | copy-start | bytes 49156
  92.7 4.4 %copy-start.9 = (f32[4096]{0:T(1024)S(1)}, f32[4096]{0:T(1024)}, u32[]{:S(2)}) copy-start(f32[4096]{0:T(1024)} %param.24) | copy-start | bytes 49156
  97.2 1.2 copy-start.3
  98.4 2.6 copy-start.1
  98.4 2.0 copy-start.4
  98.4 2.6 copy-start.5
  219.1 3.5 %copy-start.13 = (f32[1024]{0:T(1024)S(1)}, f32[1024]{0:T(1024)}, u32[]{:S(2)}) copy-start(f32[1024]{0:T(1024)} %param.35) | copy-start | bytes 12292
  219.5 0.7 copy-start.7
  222.6 2.3 copy-start.15
  233.8 38.7 %copy-start.11 = (f32[512]{0:T(512)S(1)}, f32[512]{0:T(512)}, u32[]{:S(2)}) copy-start(f32[512]{0:T(512)} %param.39) | copy-start | bytes 6148
Sparse Core Ops, SparseCore 0:
  9.9 194.5 all-gather.1
  233.9 38.5 reduce-scatter.1

commit v10 on v6

--- a/solution.py
+++ b/solution.py
@@ -227,8 +227,11 @@
     leaving = jnp.dot(take.T, back_flat, preferred_element_type=jnp.float32).astype(jnp.bfloat16)
     leaving = leaving.reshape(groups, per_owner, page_len * width_m)
     returned = lax.all_to_all(leaving, "req", split_axis=0, concat_axis=0, tiled=True)
-    pages_back = jnp.dot(
-        place.T, returned.reshape(slots, page_len * width_m), preferred_element_type=jnp.float32
+    pages_back = jnp.einsum(
+        "pab,abk->pk",
+        place.T.reshape(pg_dev, groups, per_owner),
+        returned,
+        preferred_element_type=jnp.float32,
     )
     return pages_back.astype(jnp.bfloat16).reshape(pg_dev, page_len, width_m)
 

time: 307 us -> 307 us (level)
  blocking collectives: 52.5 us -> 25.6 us
  waiting for transfers between devices: 166 us -> 184 us
  starting transfers between devices: 22.9 us -> 32.4 us
    all_to_all x1 -> x0, blocking collectives: 27 us -> none  [on_device(): lax.all_to_all(leaving, 'req', split_axis=0, concat_axis=0, tiled=True)]
    all_to_all x0 -> x1, waiting for transfers between devices: none -> 17.6 us  [on_device(): lax.all_to_all(leaving, 'req', split_axis=0, concat_axis=0, tiled=True)]
    all_to_all x0 -> x1, starting transfers between devices: none -> 9.5 us  [on_device(): lax.all_to_all(leaving, 'req', split_axis=0, concat_axis=0, tiled=True)]
  transfers between devices with their start and end apart: 5 -> 6, of which waited for: 5 -> 6; matrix products, arithmetic and copies ran while one was open for 6% -> 6% of each run, Pallas kernels for 0% -> 0%
where the time goes in v10:
time: 307 us; the launch traced here: 306 us
  waiting for transfers between devices  184 us (60%)
  starting transfers between devices  32.4 us (11%)
  matrix products  26.2 us (9%)
  blocking collectives  25.6 us (8%)
  between operations  13.8 us (4%)
  other arithmetic  11.1 us (4%)
  local copies, waits for them, and re-layouts  10.6 us (3%)
    all_gather x1, waiting for transfers between devices, on_device(): gathered = lax.all_gather(packed, 'req', axis=0, tiled=True)  77.5 us
    reduce_scatter x1, waiting for transfers between devices, on_device(): shares = lax.psum_scatter(part, 'mlp', scatter_dimension=1, tiled=True)  38.7 us
    psum x1, blocking collectives, on_device(): lax.psum((pick(down_query), pick(down_value), pick(down_fc)), 'mlp')  25.6 us
    all_to_all x1, waiting for transfers between devices, on_device(): lax.all_to_all(copies, 'mlp', split_axis=0, concat_axis=0, tiled=True)  22.1 us
    all_to_all x1, waiting for transfers between devices, on_device(): lax.all_to_all(outgoing, 'req', split_axis=0, concat_axis=0, tiled=True)  21.8 us
    all_to_all x1, waiting for transfers between devices, on_device(): lax.all_to_all(leaving, 'req', split_axis=0, concat_axis=0, tiled=True)  17.6 us
    all_to_all x1, starting transfers between devices, on_device(): lax.all_to_all(filled, 'req', split_axis=0, concat_axis=0, tiled=True)  10.6 us
    all_to_all x1, starting transfers between devices, on_device(): lax.all_to_all(leaving, 'req', split_axis=0, concat_axis=0, tiled=True)  9.5 us
  transfers between devices with their start and end apart: 6, of which 6 were waited for; matrix products, arithmetic and copies ran while one was open for 6% of the time, Pallas kernels for 0%

profile of v10, /device:TPU:57, one launch (start us, length us, event | category | flops | bytes accessed | tf_op | source)
XLA Modules:
  0.0 305.9 jit_solution(4659468146558497643)
XLA Ops:
  6.5 2.5 shard_map.190
  9.4 0.7 all_to_all.20
  10.1 10.6 %all-to-all-start = ((bf16[32,1,2]{2,1,0:T(2,128)(2,1)}), bf16[32,1,2]{2,1,0:T(2,128)(2,1)S(1)}, u32[]{:S(2)}, u32[]{:S(2)}) async-start(bf16[32,1,2]{2,1,0:T(2,128)(2,1)} %all_to_all.20), calls=%async_computation | async-start | bytes 32768 | tf_op jit(solution)/shard_map/all_to_all | solution.py:141
  21.3 1.2 reshape.374
  22.5 6.0 %all-to-all-done = bf16[32,1,2]{2,1,0:T(2,128)(2,1)S(1)} async-done(((bf16[32,1,2]{2,1,0:T(2,128)(2,1)}), bf16[32,1,2]{2,1,0:T(2,128)(2,1)S(1)}, u32[]{:S(2)}, u32[]{:S(2)}) %all-to-all-start) | async-done | bytes 160 | tf_op jit(solution)/shard_map/all_to_all | solution.py:141
  28.5 4.7 %all-to-all-start.1 = ((bf16[32,2,4096]{2,1,0:T(2,128)(2,1)}), bf16[32,2,4096]{2,1,0:T(2,128)(2,1)S(1)}, u32[]{:S(2)}, u32[]{:S(2)}) async-start(bf16[32,2,4096]{2,1,0:T(2,128)(2,1)} %reshape.374), calls=%async_computation.1 | async-start | bytes 1048576 | tf_op jit(solution)/shard_map/all_to_all | solution.py:140
  33.7 21.8 %all-to-all-done.1 = bf16[32,2,4096]{2,1,0:T(2,128)(2,1)S(1)} async-done(((bf16[32,2,4096]{2,1,0:T(2,128)(2,1)}), bf16[32,2,4096]{2,1,0:T(2,128)(2,1)S(1)}, u32[]{:S(2)}, u32[]{:S(2)}) %all-to-all-start.1) | async-done | bytes 524320 | tf_op jit(solution)/shard_map/all_to_all | solution.py:140
  56.3 1.4 broadcast_in_dim.13
  57.7 7.5 %all-to-all-start.2 = ((bf16[8,256,512]{1,2,0:T(8,128)(2,1)}), bf16[8,256,512]{1,2,0:T(8,128)(2,1)}, u32[]{:S(2)}, u32[]{:S(2)}) async-start(bf16[8,256,512]{1,2,0:T(8,128)(2,1)} %broadcast_in_dim.13), calls=%async_computation.2 | async-start | bytes 4194304 | tf_op jit(solution)/shard_map/all_to_all | solution.py:156
  65.3 1.0 slice.48
  66.5 0.8 copy.56
  67.8 22.1 %all-to-all-done.2 = bf16[8,256,512]{1,2,0:T(8,128)(2,1)} async-done(((bf16[8,256,512]{1,2,0:T(8,128)(2,1)}), bf16[8,256,512]{1,2,0:T(8,128)(2,1)}, u32[]{:S(2)}, u32[]{:S(2)}) %all-to-all-start.2) | async-done | bytes 2097184 | tf_op jit(solution)/shard_map/all_to_all | solution.py:156
  89.8 2.1 convert_reduce_fusion
  92.0 2.2 multiply_reduce_fusion
  94.2 2.6 fusion.8
  96.9 0.6 fusion.29
  97.5 1.4 copy-done.4
  100.4 25.6 %all-reduce = (bf16[256,16]{0,1:T(8,128)(2,1)S(1)}, bf16[256,16]{0,1:T(8,128)(2,1)S(1)}, bf16[256,16]{0,1:T(8,128)(2,1)S(1)}) all-reduce(f32[256,16]{0,1:T(8,128)S(1)} %get-tuple-element.6, f32[256,16]{0,1:T(8,128)S(1)} %get-tuple-element.7, f32[256,16]{0,1:T(8,128)S(1)} %get-tuple-element.5), channel_id=1, replica_groups=mesh['req'=32,'mlp'=8] {'mlp'}, use_global_device_ids=true, to_apply=%region_14.15 | all-reduce | flops 12288 | bytes 73728 | tf_op jit(solution)/shard_map/psum | solution.py:172
  126.0 0.9 broadcast_multiply_fusion.1
  126.9 77.5 %all-gather.2.cloned.1.call-done = bf16[4096,3072]{1,0:T(8,128)(2,1)} async-done(((bf16[128,3072]{1,0:T(8,128)(2,1)}), bf16[4096,3072]{1,0:T(8,128)(2,1)}) %all-gather.2.cloned.1.call-update) | async-done | bytes 25165840 | tf_op jit(solution)/shard_map/all_gather | solution.py:192
  204.5 8.7 %fusion = f32[256,1792]{1,0:T(8,128)S(1)} fusion(bf16[256,4096]{0,1:T(8,128)(2,1)} %copy-done.1, bf16[4096,3072]{1,0:T(8,128)(2,1)} %all-gather.2.cloned.1.call-done), kind=kOutput, calls=%fused_computation | convolution fusion | flops 3758096384 | bytes 18612224 | tf_op jit(solution)/shard_map/dot_general | solution.py:194
  213.9 0.6 fusion.66
  214.9 0.7 copy-done.10
  215.7 2.4 fusion.13
  218.0 2.3 fusion.18
  220.3 8.9 %fusion.2 = f32[256,4096]{1,0:T(8,128)} fusion(bf16[4096,3072]{1,0:T(8,128)(2,1)} %all-gather.2.cloned.1.call-done, bf16[256,1024]{1,0:T(8,128)(2,1)S(1)} %fusion.18, bf16[256,256]{1,0:T(8,128)(2,1)S(1)} %copy-done.19), kind=kOutput, calls=%fused_computation.2 | convolution fusion | flops 2685665280 | bytes 15335424 | tf_op jit(solution)/shard_map/dot_general | solution.py:218
  229.2 38.7 %reduce-scatter.2.cloned.1.call-done = f32[256,512]{1,0:T(8,128)} async-done(((f32[256,4096]{1,0:T(8,128)}), f32[256,512]{1,0:T(8,128)}) %reduce-scatter.2.cloned.1.call-update) | async-done | bytes 524304 | tf_op jit(solution)/shard_map/reduce_scatter | solution.py:224
  267.9 1.1 add_convert_fusion
  269.6 1.1 reshape.386
  270.7 9.5 %all-to-all-start.3 = ((bf16[32,2,4096]{2,1,0:T(2,128)(2,1)}), bf16[32,2,4096]{2,1,0:T(2,128)(2,1)S(1)}, u32[]{:S(2)}, u32[]{:S(2)}) async-start(bf16[32,2,4096]{2,1,0:T(2,128)(2,1)} %reshape.386), calls=%async_computation.4 | async-start | bytes 1048576 | tf_op jit(solution)/shard_map/all_to_all | solution.py:229
  280.2 17.6 %all-to-all-done.3 = bf16[32,2,4096]{2,1,0:T(2,128)(2,1)S(1)} async-done(((bf16[32,2,4096]{2,1,0:T(2,128)(2,1)}), bf16[32,2,4096]{2,1,0:T(2,128)(2,1)S(1)}, u32[]{:S(2)}, u32[]{:S(2)}) %all-to-all-start.3) | async-done | bytes 524320 | tf_op jit(solution)/shard_map/all_to_all | solution.py:229
  298.2 0.8 copy.67
  (83 shorter events, 6.4 us)
Async XLA Ops:
  6.5 211.5 %copy-start = (bf16[1024,1024]{1,0:T(8,128)(2,1)S(1)}, bf16[1024,1024]{1,0:T(8,128)(2,1)}, u32[]{:S(2)}) copy-start(bf16[1024,1024]{1,0:T(8,128)(2,1)} %param.37) | copy-start | bytes 6291460
  6.5 2.6 copy-start.18
  6.5 14.2 %copy-start.9 = (bf16[32,8,512]{2,1,0:T(8,128)(2,1)S(1)}, bf16[32,8,512]{2,1,0:T(8,128)(2,1)}, u32[]{:S(2)}) copy-start(bf16[32,8,512]{2,1,0:T(8,128)(2,1)} %param.20) | copy-start | bytes 786436
  6.5 197.9 %all-gather.2.cloned.1.call-start = ((), (), s32[]{:S(2)}) async-start(), calls=%async_computation.5 | async-start | bytes 25952256 | tf_op jit(solution)/shard_map/all_gather | solution.py:192
  10.1 18.3 %all-to-all-start = ((bf16[32,1,2]{2,1,0:T(2,128)(2,1)}), bf16[32,1,2]{2,1,0:T(2,128)(2,1)S(1)}, u32[]{:S(2)}, u32[]{:S(2)}) async-start(bf16[32,1,2]{2,1,0:T(2,128)(2,1)} %all_to_all.20), calls=%async_computation | async-start | bytes 32768 | tf_op jit(solution)/shard_map/all_to_all | solution.py:141
  28.5 27.1 %all-to-all-start.1 = ((bf16[32,2,4096]{2,1,0:T(2,128)(2,1)}), bf16[32,2,4096]{2,1,0:T(2,128)(2,1)S(1)}, u32[]{:S(2)}, u32[]{:S(2)}) async-start(bf16[32,2,4096]{2,1,0:T(2,128)(2,1)} %reshape.374), calls=%async_computation.1 | async-start | bytes 1048576 | tf_op jit(solution)/shard_map/all_to_all | solution.py:140
  57.7 7.6 %copy-start.2 = (bf16[1024,256]{1,0:T(8,128)(2,1)S(1)}, bf16[1024,256]{1,0:T(8,128)(2,1)}, u32[]{:S(2)}) copy-start(bf16[1024,256]{1,0:T(8,128)(2,1)} %param.31) | copy-start | bytes 1572868
  57.7 8.6 %slice-start = ((bf16[1024,256]{1,0:T(8,128)(2,1)}), bf16[1024,64]{1,0:T(8,128)(2,1)S(1)}, s32[]{:S(2)}) async-start(bf16[1024,256]{1,0:T(8,128)(2,1)} %param.31), calls=%async_computation.7 | async-start | bytes 524288 | tf_op jit(solution)/shard_map/slice | solution.py:188
  57.7 32.1 %all-to-all-start.2 = ((bf16[8,256,512]{1,2,0:T(8,128)(2,1)}), bf16[8,256,512]{1,2,0:T(8,128)(2,1)}, u32[]{:S(2)}, u32[]{:S(2)}) async-start(bf16[8,256,512]{1,2,0:T(8,128)(2,1)} %broadcast_in_dim.13), calls=%async_computation.2 | async-start | bytes 4194304 | tf_op jit(solution)/shard_map/all_to_all | solution.py:156
  65.2 2.2 copy-start.14
  65.2 2.3 copy-start.16
  65.2 202.7 %reduce-scatter.2.cloned.1.call-start = ((), (), s32[]{:S(2)}) async-start(), calls=%async_computation.6 | async-start | bytes 4718592 | tf_op jit(solution)/shard_map/reduce_scatter | solution.py:224
  67.8 26.4 %copy-start.12 = (f32[4096]{0:T(1024)S(1)}, f32[4096]{0:T(1024)}, u32[]{:S(2)}) copy-start(f32[4096]{0:T(1024)} %param.25) | copy-start | bytes 49156
  67.8 26.4 %copy-start.13 = (f32[4096]{0:T(1024)S(1)}, f32[4096]{0:T(1024)}, u32[]{:S(2)}) copy-start(f32[4096]{0:T(1024)} %param.24) | copy-start | bytes 49156
  94.2 2.6 copy-start.3
  96.9 2.6 copy-start.1
  96.9 2.0 copy-start.4
  96.9 2.5 copy-start.5
  204.5 8.7 %copy-start.6 = (bf16[256,64,16]{0,2,1:T(8,128)(2,1)S(1)}, bf16[256,64,16]{0,2,1:T(8,128)(2,1)}, u32[]{:S(2)}) copy-start(bf16[256,64,16]{0,2,1:T(8,128)(2,1)} %get-tuple-element.15) | copy-start | bytes 1572868
  204.5 8.7 %copy-start.7 = (bf16[1024,192]{1,0:T(8,128)(2,1)S(1)}, bf16[1024,192]{1,0:T(8,128)(2,1)}, u32[]{:S(2)}) copy-start(bf16[1024,192]{1,0:T(8,128)(2,1)} %slice.48) | copy-start | bytes 1179652
  204.5 8.7 %copy-start.8 = (bf16[1024,64]{1,0:T(8,128)(2,1)S(1)}, bf16[1024,64]{1,0:T(8,128)(2,1)}, u32[]{:S(2)}) copy-start(bf16[1024,64]{1,0:T(8,128)(2,1)} %copy.56) | copy-start | bytes 393220
  213.2 1.7 copy-start.11
  214.5 3.5 %copy-start.17 = (f32[1024]{0:T(1024)S(1)}, f32[1024]{0:T(1024)}, u32[]{:S(2)}) copy-start(f32[1024]{0:T(1024)} %param.35) | copy-start | bytes 12292
  214.9 0.7 copy-start.10
  218.0 2.3 copy-start.19
  229.2 38.7 %copy-start.15 = (f32[512]{0:T(512)S(1)}, f32[512]{0:T(512)}, u32[]{:S(2)}) copy-start(f32[512]{0:T(512)} %param.39) | copy-start | bytes 6148
  270.7 27.1 %all-to-all-start.3 = ((bf16[32,2,4096]{2,1,0:T(2,128)(2,1)}), bf16[32,2,4096]{2,1,0:T(2,128)(2,1)S(1)}, u32[]{:S(2)}, u32[]{:S(2)}) async-start(bf16[32,2,4096]{2,1,0:T(2,128)(2,1)} %reshape.386), calls=%async_computation.4 | async-start | bytes 1048576 | tf_op jit(solution)/shard_map/all_to_all | solution.py:229
Sparse Core Ops, SparseCore 0:
  9.9 194.5 all-gather.1
  229.3 38.5 reduce-scatter.1

commit v11 on v6

--- a/solution.py
+++ b/solution.py
@@ -70,13 +70,9 @@
     out_ref[:, 3 * hw : 3 * hw + ff] = wfi_ref[...]
     base = 3 * hw + ff
     n_ao = wao_ref.shape[0]
-    out_ref[:, base : base + n_ao] = lax.dot_general(
-        ident, wao_ref[...], nt, preferred_element_type=jnp.float32
-    ).astype(out_ref.dtype)
+    out_ref[:, base : base + n_ao] = wao_ref[...].T
     n_fo = wfo_ref.shape[0]
-    out_ref[:, base + n_ao : base + n_ao + n_fo] = lax.dot_general(
-        ident, wfo_ref[...], nt, preferred_element_type=jnp.float32
-    ).astype(out_ref.dtype)
+    out_ref[:, base + n_ao : base + n_ao + n_fo] = wfo_ref[...].T
 
 
 def pack_weights(wq, wk, wv, wfi, wao, wfo):

time: 307 us -> 307 us (level)
  no operation moved by 1% of the time
where the time goes in v11:
time: 307 us; the launch traced here: 306 us
  waiting for transfers between devices  167 us (54%)
  blocking collectives  52.5 us (17%)
  matrix products  26 us (8%)
  starting transfers between devices  22.6 us (7%)
  between operations  13.8 us (4%)
  other arithmetic  11.1 us (4%)
  local copies, waits for them, and re-layouts  11 us (4%)
    all_gather x1, waiting for transfers between devices, on_device(): gathered = lax.all_gather(packed, 'req', axis=0, tiled=True)  77.6 us
    reduce_scatter x1, waiting for transfers between devices, on_device(): shares = lax.psum_scatter(part, 'mlp', scatter_dimension=1, tiled=True)  38.7 us
    all_to_all x1, blocking collectives, on_device(): lax.all_to_all(leaving, 'req', split_axis=0, concat_axis=0, tiled=True)  27 us
    psum x1, blocking collectives, on_device(): lax.psum((pick(down_query), pick(down_value), pick(down_fc)), 'mlp')  25.6 us
    all_to_all x1, waiting for transfers between devices, on_device(): lax.all_to_all(outgoing, 'req', split_axis=0, concat_axis=0, tiled=True)  22.1 us
    all_to_all x1, waiting for transfers between devices, on_device(): lax.all_to_all(copies, 'mlp', split_axis=0, concat_axis=0, tiled=True)  22.1 us
    all_to_all x1, starting transfers between devices, on_device(): lax.all_to_all(filled, 'req', split_axis=0, concat_axis=0, tiled=True)  10.6 us
    dot_general x1, matrix products, on_device(): lax.dot_general(joined, gathered[:, n_in:], (((1,), (1,)), ((), ())), pre...  8.86 us
  transfers between devices with their start and end apart: 5, of which 5 were waited for; matrix products, arithmetic and copies ran while one was open for 6% of the time, Pallas kernels for 0%

profile of v11, /device:TPU:57, one launch (start us, length us, event | category | flops | bytes accessed | tf_op | source)
XLA Modules:
  0.0 306.0 jit_solution(496692436811682599)
XLA Ops:
  6.5 2.4 shard_map.190
  9.3 0.7 all_to_all.20
  10.0 10.6 %all-to-all-start = ((bf16[32,1,2]{2,1,0:T(2,128)(2,1)}), bf16[32,1,2]{2,1,0:T(2,128)(2,1)S(1)}, u32[]{:S(2)}, u32[]{:S(2)}) async-start(bf16[32,1,2]{2,1,0:T(2,128)(2,1)} %all_to_all.20), calls=%async_computation | async-start | bytes 32768 | tf_op jit(solution)/shard_map/all_to_all | solution.py:137
  21.2 1.2 reshape.362
  22.4 6.0 %all-to-all-done = bf16[32,1,2]{2,1,0:T(2,128)(2,1)S(1)} async-done(((bf16[32,1,2]{2,1,0:T(2,128)(2,1)}), bf16[32,1,2]{2,1,0:T(2,128)(2,1)S(1)}, u32[]{:S(2)}, u32[]{:S(2)}) %all-to-all-start) | async-done | bytes 160 | tf_op jit(solution)/shard_map/all_to_all | solution.py:137
  28.4 4.7 %all-to-all-start.1 = ((bf16[32,2,4096]{2,1,0:T(2,128)(2,1)}), bf16[32,2,4096]{2,1,0:T(2,128)(2,1)S(1)}, u32[]{:S(2)}, u32[]{:S(2)}) async-start(bf16[32,2,4096]{2,1,0:T(2,128)(2,1)} %reshape.362), calls=%async_computation.1 | async-start | bytes 1048576 | tf_op jit(solution)/shard_map/all_to_all | solution.py:136
  33.6 22.1 %all-to-all-done.1 = bf16[32,2,4096]{2,1,0:T(2,128)(2,1)S(1)} async-done(((bf16[32,2,4096]{2,1,0:T(2,128)(2,1)}), bf16[32,2,4096]{2,1,0:T(2,128)(2,1)S(1)}, u32[]{:S(2)}, u32[]{:S(2)}) %all-to-all-start.1) | async-done | bytes 524320 | tf_op jit(solution)/shard_map/all_to_all | solution.py:136
  56.5 1.4 broadcast_in_dim.13
  57.9 7.2 %all-to-all-start.2 = ((bf16[8,256,512]{1,2,0:T(8,128)(2,1)}), bf16[8,256,512]{1,2,0:T(8,128)(2,1)}, u32[]{:S(2)}, u32[]{:S(2)}) async-start(bf16[8,256,512]{1,2,0:T(8,128)(2,1)} %broadcast_in_dim.13), calls=%async_computation.2 | async-start | bytes 4194304 | tf_op jit(solution)/shard_map/all_to_all | solution.py:152
  65.2 1.0 slice.48
  66.5 0.8 copy.53
  67.7 22.1 %all-to-all-done.2 = bf16[8,256,512]{1,2,0:T(8,128)(2,1)} async-done(((bf16[8,256,512]{1,2,0:T(8,128)(2,1)}), bf16[8,256,512]{1,2,0:T(8,128)(2,1)}, u32[]{:S(2)}, u32[]{:S(2)}) %all-to-all-start.2) | async-done | bytes 2097184 | tf_op jit(solution)/shard_map/all_to_all | solution.py:152
  89.7 2.1 convert_reduce_fusion
  91.9 2.2 multiply_reduce_fusion
  94.1 2.6 fusion.7
  96.8 0.6 fusion.27
  97.4 1.4 copy-done.4
  99.3 0.6 fusion.29
  100.3 25.6 %all-reduce = (bf16[256,16]{0,1:T(8,128)(2,1)S(1)}, bf16[256,16]{0,1:T(8,128)(2,1)S(1)}, bf16[256,16]{0,1:T(8,128)(2,1)S(1)}) all-reduce(f32[256,16]{0,1:T(8,128)S(1)} %get-tuple-element.6, f32[256,16]{0,1:T(8,128)S(1)} %get-tuple-element.7, f32[256,16]{0,1:T(8,128)S(1)} %get-tuple-element.5), channel_id=1, replica_groups=mesh['req'=32,'mlp'=8] {'mlp'}, use_global_device_ids=true, to_apply=%region_14.15 | all-reduce | flops 12288 | bytes 73728 | tf_op jit(solution)/shard_map/psum | solution.py:168
  125.9 0.9 broadcast_multiply_fusion.1
  126.8 77.6 %all-gather.2.cloned.1.call-done = bf16[4096,3072]{1,0:T(8,128)(2,1)} async-done(((bf16[128,3072]{1,0:T(8,128)(2,1)}), bf16[4096,3072]{1,0:T(8,128)(2,1)}) %all-gather.2.cloned.1.call-update) | async-done | bytes 25165840 | tf_op jit(solution)/shard_map/all_gather | solution.py:188
  204.5 8.7 %fusion = f32[256,1792]{1,0:T(8,128)S(1)} fusion(bf16[256,4096]{0,1:T(8,128)(2,1)} %copy-done.1, bf16[4096,3072]{1,0:T(8,128)(2,1)} %all-gather.2.cloned.1.call-done), kind=kOutput, calls=%fused_computation | convolution fusion | flops 3758096384 | bytes 18612224 | tf_op jit(solution)/shard_map/dot_general | solution.py:190
  213.9 0.6 fusion.64
  214.9 0.7 copy-done.10
  215.7 2.4 fusion.12
  218.0 2.3 fusion.17
  220.3 8.9 %fusion.2 = f32[256,4096]{1,0:T(8,128)} fusion(bf16[4096,3072]{1,0:T(8,128)(2,1)} %all-gather.2.cloned.1.call-done, bf16[256,1024]{1,0:T(8,128)(2,1)S(1)} %fusion.17, bf16[256,256]{1,0:T(8,128)(2,1)S(1)} %copy-done.19), kind=kOutput, calls=%fused_computation.2 | convolution fusion | flops 2685665280 | bytes 15335424 | tf_op jit(solution)/shard_map/dot_general | solution.py:214
  229.2 38.7 %reduce-scatter.2.cloned.1.call-done = f32[256,512]{1,0:T(8,128)} async-done(((f32[256,4096]{1,0:T(8,128)}), f32[256,512]{1,0:T(8,128)}) %reduce-scatter.2.cloned.1.call-update) | async-done | bytes 524304 | tf_op jit(solution)/shard_map/reduce_scatter | solution.py:220
  267.9 1.1 add_convert_fusion
  269.9 27.0 %all_to_all.25 = bf16[32,2,4096]{2,1,0:T(2,128)(2,1)} all-to-all(bf16[32,2,4096]{2,1,0:T(2,128)(2,1)S(1)} %reshape.374), channel_id=1, replica_groups=mesh['req'=32,'mlp'=8] {'req'}, dimensions={0} | all-to-all | bytes 1048576 | tf_op jit(solution)/shard_map/all_to_all | solution.py:225
  296.9 1.2 reshape.375
  298.4 0.8 copy.63
  (82 shorter events, 6.0 us)
Async XLA Ops:
  6.5 211.5 %copy-start = (bf16[1024,1024]{1,0:T(8,128)(2,1)S(1)}, bf16[1024,1024]{1,0:T(8,128)(2,1)}, u32[]{:S(2)}) copy-start(bf16[1024,1024]{1,0:T(8,128)(2,1)} %param.37) | copy-start | bytes 6291460
  6.5 2.5 copy-start.18
  6.5 14.1 %copy-start.9 = (bf16[32,8,512]{2,1,0:T(8,128)(2,1)S(1)}, bf16[32,8,512]{2,1,0:T(8,128)(2,1)}, u32[]{:S(2)}) copy-start(bf16[32,8,512]{2,1,0:T(8,128)(2,1)} %param.20) | copy-start | bytes 786436
  6.5 197.9 %all-gather.2.cloned.1.call-start = ((), (), s32[]{:S(2)}) async-start(), calls=%async_computation.5 | async-start | bytes 25952256 | tf_op jit(solution)/shard_map/all_gather | solution.py:188
  10.0 18.3 %all-to-all-start = ((bf16[32,1,2]{2,1,0:T(2,128)(2,1)}), bf16[32,1,2]{2,1,0:T(2,128)(2,1)S(1)}, u32[]{:S(2)}, u32[]{:S(2)}) async-start(bf16[32,1,2]{2,1,0:T(2,128)(2,1)} %all_to_all.20), calls=%async_computation | async-start | bytes 32768 | tf_op jit(solution)/shard_map/all_to_all | solution.py:137
  28.4 27.3 %all-to-all-start.1 = ((bf16[32,2,4096]{2,1,0:T(2,128)(2,1)}), bf16[32,2,4096]{2,1,0:T(2,128)(2,1)S(1)}, u32[]{:S(2)}, u32[]{:S(2)}) async-start(bf16[32,2,4096]{2,1,0:T(2,128)(2,1)} %reshape.362), calls=%async_computation.1 | async-start | bytes 1048576 | tf_op jit(solution)/shard_map/all_to_all | solution.py:136
  57.9 7.3 %copy-start.2 = (bf16[1024,256]{1,0:T(8,128)(2,1)S(1)}, bf16[1024,256]{1,0:T(8,128)(2,1)}, u32[]{:S(2)}) copy-start(bf16[1024,256]{1,0:T(8,128)(2,1)} %param.31) | copy-start | bytes 1572868
  57.9 8.3 %slice-start = ((bf16[1024,256]{1,0:T(8,128)(2,1)}), bf16[1024,64]{1,0:T(8,128)(2,1)S(1)}, s32[]{:S(2)}) async-start(bf16[1024,256]{1,0:T(8,128)(2,1)} %param.31), calls=%async_computation.7 | async-start | bytes 524288 | tf_op jit(solution)/shard_map/slice | solution.py:184
  57.9 31.9 %all-to-all-start.2 = ((bf16[8,256,512]{1,2,0:T(8,128)(2,1)}), bf16[8,256,512]{1,2,0:T(8,128)(2,1)}, u32[]{:S(2)}, u32[]{:S(2)}) async-start(bf16[8,256,512]{1,2,0:T(8,128)(2,1)} %broadcast_in_dim.13), calls=%async_computation.2 | async-start | bytes 4194304 | tf_op jit(solution)/shard_map/all_to_all | solution.py:152
  65.1 2.2 copy-start.14
  65.1 2.3 copy-start.16
  65.1 202.8 %reduce-scatter.2.cloned.1.call-start = ((), (), s32[]{:S(2)}) async-start(), calls=%async_computation.6 | async-start | bytes 4718592 | tf_op jit(solution)/shard_map/reduce_scatter | solution.py:220
  67.7 26.4 %copy-start.12 = (f32[4096]{0:T(1024)S(1)}, f32[4096]{0:T(1024)}, u32[]{:S(2)}) copy-start(f32[4096]{0:T(1024)} %param.25) | copy-start | bytes 49156
  67.7 26.4 %copy-start.13 = (f32[4096]{0:T(1024)S(1)}, f32[4096]{0:T(1024)}, u32[]{:S(2)}) copy-start(f32[4096]{0:T(1024)} %param.24) | copy-start | bytes 49156
  94.1 2.6 copy-start.3
  96.8 2.6 copy-start.1
  96.8 2.0 copy-start.4
  96.8 2.6 copy-start.5
  204.5 8.7 %copy-start.6 = (bf16[256,64,16]{0,2,1:T(8,128)(2,1)S(1)}, bf16[256,64,16]{0,2,1:T(8,128)(2,1)}, u32[]{:S(2)}) copy-start(bf16[256,64,16]{0,2,1:T(8,128)(2,1)} %get-tuple-element.15) | copy-start | bytes 1572868
  204.5 8.7 %copy-start.7 = (bf16[1024,192]{1,0:T(8,128)(2,1)S(1)}, bf16[1024,192]{1,0:T(8,128)(2,1)}, u32[]{:S(2)}) copy-start(bf16[1024,192]{1,0:T(8,128)(2,1)} %slice.48) | copy-start | bytes 1179652
  204.5 8.7 %copy-start.8 = (bf16[1024,64]{1,0:T(8,128)(2,1)S(1)}, bf16[1024,64]{1,0:T(8,128)(2,1)}, u32[]{:S(2)}) copy-start(bf16[1024,64]{1,0:T(8,128)(2,1)} %copy.53) | copy-start | bytes 393220
  213.2 1.7 copy-start.11
  214.5 3.5 %copy-start.17 = (f32[1024]{0:T(1024)S(1)}, f32[1024]{0:T(1024)}, u32[]{:S(2)}) copy-start(f32[1024]{0:T(1024)} %param.35) | copy-start | bytes 12292
  214.9 0.7 copy-start.10
  218.0 2.3 copy-start.19
  229.2 38.7 %copy-start.15 = (f32[512]{0:T(512)S(1)}, f32[512]{0:T(512)}, u32[]{:S(2)}) copy-start(f32[512]{0:T(512)} %param.39) | copy-start | bytes 6148
Sparse Core Ops, SparseCore 0:
  9.9 194.5 all-gather.1
  229.3 38.5 reduce-scatter.1

commit v12 on v6

--- a/solution.py
+++ b/solution.py
@@ -221,8 +221,12 @@
         (((1,), (1,)), ((), ())),
         preferred_element_type=jnp.float32,
     )
+    n_out = lax.axis_size("mlp")
+    mine = own_x.astype(jnp.float32) + b_fc_out
+    owned = (jnp.arange(n_out * width_m) // width_m) == lax.axis_index("mlp")
+    part = part + jnp.where(owned[None, :], jnp.tile(mine, (1, n_out)), 0.0)
     shares = lax.psum_scatter(part, "mlp", scatter_dimension=1, tiled=True)
-    result = (own_x.astype(jnp.float32) + shares + b_fc_out).astype(jnp.bfloat16)
+    result = shares.astype(jnp.bfloat16)
     back_flat = result.reshape(pg_dev, page_len * width_m)
     leaving = jnp.dot(take.T, back_flat, preferred_element_type=jnp.float32).astype(jnp.bfloat16)
     leaving = leaving.reshape(groups, per_owner, page_len * width_m)

time: 307 us -> 306 us (level)
  waiting for transfers between devices: 166 us -> 158 us
  local copies, waits for them, and re-layouts: 11 us -> 15.5 us
    all_to_all x1, waiting for transfers between devices: 22.1 us -> 15.2 us  [on_device(): lax.all_to_all(copies, 'mlp', split_axis=0, concat_axis=0, tiled=True)]
    unnamed x42 -> x45, local copies, waits for them, and re-layouts: 3.05 us -> 7.69 us
  transfers between devices with their start and end apart: 5 -> 5, of which waited for: 5 -> 5; matrix products, arithmetic and copies ran while one was open for 6% -> 9% of each run, Pallas kernels for 0% -> 0%
where the time goes in v12:
time: 306 us; the launch traced here: 305 us
  waiting for transfers between devices  158 us (52%)
  blocking collectives  52.5 us (17%)
  matrix products  26.2 us (9%)
  starting transfers between devices  22.8 us (7%)
  local copies, waits for them, and re-layouts  15.5 us (5%)
  between operations  13.9 us (5%)
  other arithmetic  13.8 us (5%)
    all_gather x1, waiting for transfers between devices, on_device(): gathered = lax.all_gather(packed, 'req', axis=0, tiled=True)  77.4 us
    reduce_scatter x1, waiting for transfers between devices, on_device(): shares = lax.psum_scatter(part, 'mlp', scatter_dimension=1, tiled=True)  38.7 us
    all_to_all x1, blocking collectives, on_device(): lax.all_to_all(leaving, 'req', split_axis=0, concat_axis=0, tiled=True)  27 us
    psum x1, blocking collectives, on_device(): lax.psum((pick(down_query), pick(down_value), pick(down_fc)), 'mlp')  25.6 us
    all_to_all x1, waiting for transfers between devices, on_device(): lax.all_to_all(outgoing, 'req', split_axis=0, concat_axis=0, tiled=True)  21.8 us
    all_to_all x1, waiting for transfers between devices, on_device(): lax.all_to_all(copies, 'mlp', split_axis=0, concat_axis=0, tiled=True)  15.2 us
    all_to_all x1, starting transfers between devices, on_device(): lax.all_to_all(filled, 'req', split_axis=0, concat_axis=0, tiled=True)  10.6 us
    dot_general x1, matrix products, on_device(): lax.dot_general(joined, gathered[:, n_in:], (((1,), (1,)), ((), ())), pre...  10.2 us
  transfers between devices with their start and end apart: 5, of which 5 were waited for; matrix products, arithmetic and copies ran while one was open for 9% of the time, Pallas kernels for 0%

profile of v12, /device:TPU:57, one launch (start us, length us, event | category | flops | bytes accessed | tf_op | source)
XLA Modules:
  0.0 305.4 jit_solution(266764589624229228)
XLA Ops:
  6.5 2.5 shard_map.190
  9.1 0.9 convert_reduce_fusion.3
  10.0 0.7 multiply_add_fusion.1
  10.7 0.7 all_to_all.20
  11.5 10.6 %all-to-all-start = ((bf16[32,1,2]{2,1,0:T(2,128)(2,1)}), bf16[32,1,2]{2,1,0:T(2,128)(2,1)S(1)}, u32[]{:S(2)}, u32[]{:S(2)}) async-start(bf16[32,1,2]{2,1,0:T(2,128)(2,1)} %all_to_all.20), calls=%async_computation | async-start | bytes 32768 | tf_op jit(solution)/shard_map/all_to_all | solution.py:141
  22.1 1.0 copy.62
  23.5 1.2 reshape.396
  24.7 5.1 %all-to-all-done = bf16[32,1,2]{2,1,0:T(2,128)(2,1)S(1)} async-done(((bf16[32,1,2]{2,1,0:T(2,128)(2,1)}), bf16[32,1,2]{2,1,0:T(2,128)(2,1)S(1)}, u32[]{:S(2)}, u32[]{:S(2)}) %all-to-all-start) | async-done | bytes 160 | tf_op jit(solution)/shard_map/all_to_all | solution.py:141
  29.8 4.7 %all-to-all-start.1 = ((bf16[32,2,4096]{2,1,0:T(2,128)(2,1)}), bf16[32,2,4096]{2,1,0:T(2,128)(2,1)S(1)}, u32[]{:S(2)}, u32[]{:S(2)}) async-start(bf16[32,2,4096]{2,1,0:T(2,128)(2,1)} %reshape.396), calls=%async_computation.1 | async-start | bytes 1048576 | tf_op jit(solution)/shard_map/all_to_all | solution.py:140
  35.0 21.8 %all-to-all-done.1 = bf16[32,2,4096]{2,1,0:T(2,128)(2,1)S(1)} async-done(((bf16[32,2,4096]{2,1,0:T(2,128)(2,1)}), bf16[32,2,4096]{2,1,0:T(2,128)(2,1)S(1)}, u32[]{:S(2)}, u32[]{:S(2)}) %all-to-all-start.1) | async-done | bytes 524320 | tf_op jit(solution)/shard_map/all_to_all | solution.py:140
  57.7 1.5 broadcast_in_dim.28
  59.1 7.5 %all-to-all-start.2 = ((bf16[8,256,512]{1,2,0:T(8,128)(2,1)}), bf16[8,256,512]{1,2,0:T(8,128)(2,1)}, u32[]{:S(2)}, u32[]{:S(2)}) async-start(bf16[8,256,512]{1,2,0:T(8,128)(2,1)} %broadcast_in_dim.28), calls=%async_computation.2 | async-start | bytes 4194304 | tf_op jit(solution)/shard_map/all_to_all | solution.py:156
  66.6 1.1 slice.48
  68.1 0.6 multiply_power_fusion
  70.3 5.8 %copy.63 = f32[32,8,8,512]{3,1,2,0:T(8,128)} copy(f32[32,8,8,512]{3,2,1,0:T(8,128)S(1)} %bitcast.63) | data formatting | bytes 8388608
  76.0 15.2 %all-to-all-done.2 = bf16[8,256,512]{1,2,0:T(8,128)(2,1)} async-done(((bf16[8,256,512]{1,2,0:T(8,128)(2,1)}), bf16[8,256,512]{1,2,0:T(8,128)(2,1)}, u32[]{:S(2)}, u32[]{:S(2)}) %all-to-all-start.2) | async-done | bytes 2097184 | tf_op jit(solution)/shard_map/all_to_all | solution.py:156
  91.3 2.1 convert_reduce_fusion
  93.4 2.4 multiply_reduce_fusion
  95.8 2.6 fusion.10
  100.6 25.6 %all-reduce = (bf16[256,16]{0,1:T(8,128)(2,1)S(1)}, bf16[256,16]{0,1:T(8,128)(2,1)S(1)}, bf16[256,16]{0,1:T(8,128)(2,1)S(1)}) all-reduce(f32[256,16]{0,1:T(8,128)S(1)} %get-tuple-element.6, f32[256,16]{0,1:T(8,128)S(1)} %get-tuple-element.7, f32[256,16]{0,1:T(8,128)S(1)} %get-tuple-element.5), channel_id=1, replica_groups=mesh['req'=32,'mlp'=8] {'mlp'}, use_global_device_ids=true, to_apply=%region_14.15 | all-reduce | flops 12288 | bytes 73728 | tf_op jit(solution)/shard_map/psum | solution.py:172
  126.2 0.9 broadcast_multiply_fusion.1
  127.1 77.4 %all-gather.2.cloned.1.call-done = bf16[4096,3072]{1,0:T(8,128)(2,1)} async-done(((bf16[128,3072]{1,0:T(8,128)(2,1)}), bf16[4096,3072]{1,0:T(8,128)(2,1)}) %all-gather.2.cloned.1.call-update) | async-done | bytes 25165840 | tf_op jit(solution)/shard_map/all_gather | solution.py:192
  204.5 8.6 %fusion = f32[256,1792]{1,0:T(8,128)S(1)} fusion(bf16[256,4096]{0,1:T(8,128)(2,1)} %copy-done.1, bf16[4096,3072]{1,0:T(8,128)(2,1)} %all-gather.2.cloned.1.call-done), kind=kOutput, calls=%fused_computation | convolution fusion | flops 3758096384 | bytes 18612224 | tf_op jit(solution)/shard_map/dot_general | solution.py:194
  213.9 0.6 fusion.67
  215.0 1.8 fusion.20
  216.8 1.6 fusion.15
  218.4 10.2 %fusion.4 = f32[256,4096]{1,0:T(8,128)} fusion(bf16[4096,3072]{1,0:T(8,128)(2,1)} %all-gather.2.cloned.1.call-done, f32[256,4096]{1,0:T(8,128)} %bitcast.67, pred[4096]{0:T(1024)(128)(4,1)S(1)} %copy-done.12, bf16[256,1024]{1,0:T(8,128)(2,1)} %fusion.20, bf16[256,256]{1,0:T(8,128)(2,1)S(1)} %fusion.15), kind=kOutput, calls=%fused_computation.4 | convolution fusion | flops 2687762432 | bytes 19533824 | tf_op jit(solution)/shard_map/dot_general | solution.py:218
  228.6 38.7 %reduce-scatter.2.cloned.1.call-done = f32[256,512]{1,0:T(8,128)} async-done(((f32[256,4096]{1,0:T(8,128)}), f32[256,512]{1,0:T(8,128)}) %reduce-scatter.2.cloned.1.call-update) | async-done | bytes 524304 | tf_op jit(solution)/shard_map/reduce_scatter | solution.py:228
  267.3 1.1 convert_element_type.176
  269.3 27.0 %all_to_all.25 = bf16[32,2,4096]{2,1,0:T(2,128)(2,1)} all-to-all(bf16[32,2,4096]{2,1,0:T(2,128)(2,1)S(1)} %reshape.407), channel_id=1, replica_groups=mesh['req'=32,'mlp'=8] {'req'}, dimensions={0} | all-to-all | bytes 1048576 | tf_op jit(solution)/shard_map/all_to_all | solution.py:233
  296.3 1.2 reshape.408
  297.8 0.8 copy.64
  (88 shorter events, 8.1 us)
Async XLA Ops:
  6.5 208.4 %copy-start = (bf16[1024,1024]{1,0:T(8,128)(2,1)S(1)}, bf16[1024,1024]{1,0:T(8,128)(2,1)}, u32[]{:S(2)}) copy-start(bf16[1024,1024]{1,0:T(8,128)(2,1)} %param.37) | copy-start | bytes 6291460
  6.5 197.9 %all-gather.2.cloned.1.call-start = ((), (), s32[]{:S(2)}) async-start(), calls=%async_computation.5 | async-start | bytes 25952256 | tf_op jit(solution)/shard_map/all_gather | solution.py:192
  10.6 23.8 %copy-start.14 = (s32[32]{0:T(128)}, s32[32]{0:T(128)S(1)}, u32[]{:S(2)}) copy-start(s32[32]{0:T(128)S(1)} %multiply_add_fusion.1) | copy-start | bytes 388
  11.5 18.3 %all-to-all-start = ((bf16[32,1,2]{2,1,0:T(2,128)(2,1)}), bf16[32,1,2]{2,1,0:T(2,128)(2,1)S(1)}, u32[]{:S(2)}, u32[]{:S(2)}) async-start(bf16[32,1,2]{2,1,0:T(2,128)(2,1)} %all_to_all.20), calls=%async_computation | async-start | bytes 32768 | tf_op jit(solution)/shard_map/all_to_all | solution.py:141
  29.8 27.1 %all-to-all-start.1 = ((bf16[32,2,4096]{2,1,0:T(2,128)(2,1)}), bf16[32,2,4096]{2,1,0:T(2,128)(2,1)S(1)}, u32[]{:S(2)}, u32[]{:S(2)}) async-start(bf16[32,2,4096]{2,1,0:T(2,128)(2,1)} %reshape.396), calls=%async_computation.1 | async-start | bytes 1048576 | tf_op jit(solution)/shard_map/all_to_all | solution.py:140
  34.5 24.6 %copy-start.16 = (f32[32]{0:T(128)}, f32[32]{0:T(128)S(1)}, u32[]{:S(2)}) copy-start(f32[32]{0:T(128)S(1)} %iota_convert_fusion) | copy-start | bytes 388
  57.3 9.3 %copy-start.2 = (bf16[1024,256]{1,0:T(8,128)(2,1)S(1)}, bf16[1024,256]{1,0:T(8,128)(2,1)}, u32[]{:S(2)}) copy-start(bf16[1024,256]{1,0:T(8,128)(2,1)} %param.31) | copy-start | bytes 1572868
  57.6 10.1 %slice-start = ((bf16[1024,256]{1,0:T(8,128)(2,1)}), bf16[1024,64]{1,0:T(8,128)(2,1)S(1)}, s32[]{:S(2)}) async-start(bf16[1024,256]{1,0:T(8,128)(2,1)} %param.31), calls=%async_computation.7 | async-start | bytes 524288 | tf_op jit(solution)/shard_map/slice | solution.py:188
  57.6 11.7 %copy-start.11 = (s32[256]{0:T(256)S(1)}, s32[256]{0:T(256)}, u32[]{:S(2)}) copy-start(s32[256]{0:T(256)} %param.22) | copy-start | bytes 3076
  57.6 11.8 %copy-start.18 = (s32[256]{0:T(256)S(1)}, s32[256]{0:T(256)}, u32[]{:S(2)}) copy-start(s32[256]{0:T(256)} %param.23) | copy-start | bytes 3076
  59.1 10.5 %copy-start.13 = (f32[512]{0:T(512)S(1)}, f32[512]{0:T(512)}, u32[]{:S(2)}) copy-start(f32[512]{0:T(512)} %param.39) | copy-start | bytes 6148
  59.1 32.1 %all-to-all-start.2 = ((bf16[8,256,512]{1,2,0:T(8,128)(2,1)}), bf16[8,256,512]{1,2,0:T(8,128)(2,1)}, u32[]{:S(2)}, u32[]{:S(2)}) async-start(bf16[8,256,512]{1,2,0:T(8,128)(2,1)} %broadcast_in_dim.28), calls=%async_computation.2 | async-start | bytes 4194304 | tf_op jit(solution)/shard_map/all_to_all | solution.py:156
  66.6 200.7 %reduce-scatter.2.cloned.1.call-start = ((), (), s32[]{:S(2)}) async-start(), calls=%async_computation.6 | async-start | bytes 4718592 | tf_op jit(solution)/shard_map/reduce_scatter | solution.py:228
  76.0 19.8 %copy-start.9 = (f32[4096]{0:T(1024)S(1)}, f32[4096]{0:T(1024)}, u32[]{:S(2)}) copy-start(f32[4096]{0:T(1024)} %param.25) | copy-start | bytes 49156
  76.0 19.8 %copy-start.10 = (f32[4096]{0:T(1024)S(1)}, f32[4096]{0:T(1024)}, u32[]{:S(2)}) copy-start(f32[4096]{0:T(1024)} %param.24) | copy-start | bytes 49156
  76.0 22.4 %copy-start.3 = (bf16[512,1024]{1,0:T(8,128)(2,1)S(1)}, bf16[512,1024]{1,0:T(8,128)(2,1)}, u32[]{:S(2)}) copy-start(bf16[512,1024]{1,0:T(8,128)(2,1)} %param.30) | copy-start | bytes 3145732
  93.4 5.6 %copy-start.4 = (bf16[512,1024]{1,0:T(8,128)(2,1)S(1)}, bf16[512,1024]{1,0:T(8,128)(2,1)}, u32[]{:S(2)}) copy-start(bf16[512,1024]{1,0:T(8,128)(2,1)} %param.36) | copy-start | bytes 3145732
  95.8 3.8 %copy-start.5 = (bf16[512,1024]{1,0:T(8,128)(2,1)S(1)}, bf16[512,1024]{1,0:T(8,128)(2,1)}, u32[]{:S(2)}) copy-start(bf16[512,1024]{1,0:T(8,128)(2,1)} %param.32) | copy-start | bytes 3145732
  98.4 2.2 copy-start.1
  127.1 86.8 %copy-start.19 = (f32[32]{0:T(128)S(1)}, f32[32]{0:T(128)}, u32[]{:S(2)}) copy-start(f32[32]{0:T(128)} %multiply_power_fusion) | copy-start | bytes 388
  204.5 8.7 %copy-start.6 = (bf16[256,64,16]{0,2,1:T(8,128)(2,1)S(1)}, bf16[256,64,16]{0,2,1:T(8,128)(2,1)}, u32[]{:S(2)}) copy-start(bf16[256,64,16]{0,2,1:T(8,128)(2,1)} %get-tuple-element.15) | copy-start | bytes 1572868
  204.5 8.7 %copy-start.7 = (bf16[1024,192]{1,0:T(8,128)(2,1)S(1)}, bf16[1024,192]{1,0:T(8,128)(2,1)}, u32[]{:S(2)}) copy-start(bf16[1024,192]{1,0:T(8,128)(2,1)} %slice.48) | copy-start | bytes 1179652
  213.1 3.6 %copy-start.8 = (f32[256,1792]{1,0:T(8,128)}, f32[256,1792]{1,0:T(8,128)S(1)}, u32[]{:S(2)}) copy-start(f32[256,1792]{1,0:T(8,128)S(1)} %fusion) | copy-start | bytes 5505028
  213.1 1.8 copy-start.20
  214.9 3.5 %copy-start.12 = (pred[4096]{0:T(1024)(128)(4,1)S(1)}, pred[4096]{0:T(1024)(128)(4,1)}, u32[]{:S(2)}) copy-start(pred[4096]{0:T(1024)(128)(4,1)} %fusion.72) | copy-start | bytes 12292
  228.6 39.9 %copy-start.17 = (f32[32]{0:T(128)S(1)}, f32[32]{0:T(128)}, u32[]{:S(2)}) copy-start(f32[32]{0:T(128)} %copy-done.16) | copy-start | bytes 388
  228.6 68.9 %copy-start.15 = (s32[32]{0:T(128)S(1)}, s32[32]{0:T(128)}, u32[]{:S(2)}) copy-start(s32[32]{0:T(128)} %copy-done.14) | copy-start | bytes 388
Sparse Core Ops, SparseCore 0:
  9.9 194.5 all-gather.1
  228.7 38.5 reduce-scatter.1
